TPU v7x, 32 devices: a whole 2x2x4 slice. The times are simulated.
32 devices in a mesh: groups: 2 (over x), wide: 4 (over y, core), expert: 4 (over z).
Axes of the slice: x: 2, y: 2, z: 4, core: 2. Of those that a mesh axis runs over, the one named last changes fastest.
Arguments:
- prompts: bfloat16 [8, 128, 6144], P(('groups', 'wide'), None, 'expert'), parts along dimension 0, may hold values from -6 to 6
- span_slot_owner: int32 [8], P('groups'), parts along dimension 0, may hold values from 0 to 3, as said below
- row_expert_index: int32 [768, 2], P('groups'), parts along dimension 0, may hold values from 0 to 7, all different within a row
- tile_tenant_index: int32 [6], P('groups'), parts along dimension 0, may hold values from 0 to 7
- tenant_adapter_slot: int32 [16], P('groups'), parts along dimension 0, may hold values from 0 to 7, each once
- router: bfloat16 [6144, 8], replicated, may hold values from -0.078125 to 0.078125
- gate_weight: bfloat16 [2, 6144, 16384], P(None, None, ('wide', 'expert')), may hold values from -0.078125 to 0.078125
- up_weight: bfloat16 [2, 6144, 16384], P(None, None, ('wide', 'expert')), may hold values from -0.078125 to 0.078125
- down_weight: bfloat16 [2, 16384, 6144], P(None, 'wide', 'expert'), may hold values from -0.046875 to 0.046875
- adapter_down_weight: bfloat16 [16, 2, 6144, 64], P(('groups', 'wide'), None, 'expert'), parts along dimension 0, may hold values from -0.078125 to 0.078125
- adapter_up_weight: bfloat16 [16, 2, 64, 16384], P('groups', None, None, ('wide', 'expert')), parts along dimension 0, may hold values from -0.75 to 0.75
Outputs:
- mixed: bfloat16 [768, 6144], P(('groups', 'wide'), 'expert'), parts along dimension 0
There are 2 independent parts, one for each index of `groups`. A program takes and returns all parts, laid end to end along the dimension named above; an argument that names none is the same for every part. Nothing has to cross between parts.
Inputs may be any that keep to these rules, and one draw needn't show every extreme that they name: `span_slot_owner`: a permutation of the slots; span c, for c < 3, is in slot span_slot_owner[c]. `row_expert_index`: each row names two different experts. `tenant_adapter_slot`: a permutation of the slots. `tile_tenant_index`: tenant of rows 128 * i to 128 * i + 127.
All inputs are finite; a program needn't handle non-finite values.
Results may differ from a plain program's by a relative error of at most 0.0051.
Values may be sent and summed in bfloat16 or wider, within the bound.
No kernel may reach another device: no remote copies, remote signals or barrier semaphores. Data moves between devices by JAX's collectives and lax.ppermute only.
A program may use at most 128 MiB of HBM per device.

v0:
```python
import jax
import jax.numpy as jnp
from jax import lax
from jax.sharding import PartitionSpec as P

NCHUNK = 3


ADAPTER_SCALE = 0.5


def spread(block, axis, source):
    block = jnp.where(lax.axis_index(axis) == source, block, jnp.zeros_like(block))
    return lax.psum(block, axis)


def per_device(
    prompts,
    span_slot_owner,
    row_expert_index,
    tile_tenant_index,
    tenant_adapter_slot,
    router,
    gate_weight,
    up_weight,
    down_weight,
    adapter_down_weight,
    adapter_up_weight,
):
    column = lax.axis_index("expert")
    own_slot = prompts[0]
    width_part = own_slot.shape[1]
    full_slot = lax.all_gather(own_slot, "expert", axis=1, tiled=True)
    pieces = [
        spread(full_slot, "wide", span_slot_owner[span_index]) for span_index in range(NCHUNK)
    ]
    input_rows = jnp.concatenate(pieces, axis=0)
    slices = lax.dynamic_slice_in_dim(input_rows, column * width_part, width_part, 1)
    tokens = input_rows.shape[0]
    window = gate_weight.shape[0]
    logits = jnp.dot(input_rows, router, preferred_element_type=jnp.float32)
    experts = jnp.arange(router.shape[1], dtype=jnp.int32)
    picked = (row_expert_index[:, :, None] == experts[None, None, :]).astype(jnp.float32)
    chosen = jnp.sum(picked * logits[:, None, :], axis=2)
    first_prob = jax.nn.sigmoid(chosen[:, 0] - chosen[:, 1])
    second_prob = jax.nn.sigmoid(chosen[:, 1] - chosen[:, 0])
    weight = (
        first_prob[:, None] * picked[:, 0, :window] + second_prob[:, None] * picked[:, 1, :window]
    )
    tile_count = tile_tenant_index.shape[0]
    tile_rows = tokens // tile_count
    resident_slots = adapter_down_weight.shape[0]
    tile_slot_index = jnp.take(tenant_adapter_slot, tile_tenant_index)
    owners = tile_slot_index // resident_slots
    local_expert_index = tile_slot_index % resident_slots
    tile_slices = slices.reshape(tile_count, tile_rows, width_part)

    def fetch_one(state_carry, tile_position):
        adapter_piece = lax.dynamic_index_in_dim(
            adapter_down_weight, local_expert_index[tile_position], 0, keepdims=False
        )
        return (state_carry, spread(adapter_piece, "wide", owners[tile_position]))

    unused, fetched = lax.scan(fetch_one, jnp.int32(0), jnp.arange(tile_count, dtype=jnp.int32))
    partial_rank = jnp.einsum(
        "ntd,nedr->nter", tile_slices, fetched, preferred_element_type=jnp.float32
    )
    summed = lax.psum(partial_rank, "expert")
    lowrank = summed.astype(jnp.bfloat16)
    tenant_list = adapter_up_weight.shape[0]
    select_tenant = (
        tile_tenant_index[:, None] == jnp.arange(tenant_list, dtype=jnp.int32)[None, :]
    ).astype(adapter_up_weight.dtype)
    tile_up = jnp.einsum(
        "cj,jvqz->cvqz", select_tenant, adapter_up_weight, preferred_element_type=jnp.float32
    ).astype(jnp.bfloat16)
    adapted_hidden = jnp.einsum(
        "nter,nerf->ntef", lowrank, tile_up, preferred_element_type=jnp.float32
    )
    adapted_hidden = adapted_hidden.reshape(tokens, window, adapted_hidden.shape[3])
    gate_pre = jnp.einsum(
        "td,edf->tef", input_rows, gate_weight, preferred_element_type=jnp.float32
    )
    up_projection_value = (
        jnp.einsum("td,edf->tef", input_rows, up_weight, preferred_element_type=jnp.float32)
        + ADAPTER_SCALE * adapted_hidden
    )
    hidden = (weight[:, :, None] * jax.nn.silu(gate_pre) * up_projection_value).astype(jnp.bfloat16)
    partial_out = jnp.einsum(
        "tef,efd->td",
        lax.all_gather(hidden, "expert", axis=2, tiled=True),
        down_weight,
        preferred_element_type=jnp.float32,
    )
    mixed_rows = lax.psum_scatter(partial_out, "wide", scatter_dimension=0, tiled=True)
    return mixed_rows.astype(jnp.bfloat16)


def solution(mesh):
    in_specs = (
        P(("groups", "wide"), None, "expert"),
        P("groups"),
        P("groups", None),
        P("groups"),
        P("groups"),
        P(),
        P(None, None, ("wide", "expert")),
        P(None, None, ("wide", "expert")),
        P(None, "wide", "expert"),
        P(("groups", "wide"), None, "expert", None),
        P("groups", None, None, ("wide", "expert")),
    )
    out_specs = P(("groups", "wide"), "expert")
    return jax.shard_map(
        per_device, mesh=mesh, in_specs=in_specs, out_specs=out_specs, check_vma=False
    )
```

profile of v0, /device:TPU:0, one launch (start us, length us, event | category | flops | bytes accessed | tf_op | source)
XLA Modules:
  0.0 514.7 jit_solution(17569741497082177469)
XLA Ops:
  6.5 0.7 all-gather.6.cloned.1.call-update
  7.3 1.4 fusion.18
  10.5 38.3 %all-gather.6.cloned.1.call-done = bf16[1,128,6144]{2,1,0:T(8,128)(2,1)} async-done(((bf16[1,128,1536]{2,1,0:T(8,128)(2,1)}), bf16[1,128,6144]{2,1,0:T(8,128)(2,1)}) %all-gather.6.cloned.1.call-update) | async-done | bytes 1572880 | tf_op jit(solution)/shard_map/all_gather | solution.py:33
  48.8 3.7 select_bitcast_fusion
  52.5 0.6 copy-done.10
  53.1 0.6 gather_fusion
  53.8 2.5 fusion.6
  56.3 89.6 %all-reduce.5.cloned.1.call-done = (bf16[128,6144]{1,0:T(8,128)(2,1)}, bf16[128,6144]{1,0:T(8,128)(2,1)}, bf16[128,6144]{1,0:T(8,128)(2,1)}) async-done(((bf16[128,6144]{1,0:T(8,128)(2,1)}, bf16[128,6144]{1,0:T(8,128)(2,1)}, bf16[128,6144]{1,0:T(8,128)(2,1)}), (bf16[128,6144]{1,0:T(8,128)(2,1)}, bf16[128,6144]{1,0:T(8,128)(2,1)}, bf16[128,6144]{1,0:T(8,128)(2,1)})) %all-reduce.5.cloned.1.call-update) | async-done | bytes 4718608 | tf_op jit(solution)/shard_map/psum | solution.py:14
  145.9 1.7 constant_dynamic-update-slice_fusion.3
  148.8 1.3 fusion.19
  150.3 0.6 copy-done.3
  150.9 134.1 %while.10 = (s32[]{:T(128)}, bf16[3,2,1536,64]{3,2,1,0:T(8,128)(2,1)}, s32[3]{0:T(128)S(1)}, s32[3]{0:T(128)S(1)}, s32[3]{0:T(128)S(1)}, /*index=5*/bf16[2,2,153...) while((s32[]{:T(128)}, ...), condition=%wide.region_6.7_spmd, body=%wide.region_4.6_spmd.sunk | while | flops 393228 | bytes 7078207 | solution.py:64
  157.6 1.0 broadcast_select_fusion.2
  158.7 34.9 %all-reduce.7.cloned.1.call-done = bf16[1,2,1536,64]{3,2,1,0:T(8,128)(2,1)} async-done(((bf16[1,2,1536,64]{3,2,1,0:T(8,128)(2,1)}), bf16[1,2,1536,64]{3,2,1,0:T(8,128)(2,1)}) %all-reduce.7.cloned.1.call-update) | async-done | bytes 393232 | tf_op jit(solution)/shard_map/while/body/eval_jaxpr/psum | solution.py:14
  193.6 2.1 constant_dynamic-update-slice_fusion.5
  201.1 0.6 dynamic_slice.27
  202.4 1.0 broadcast_select_fusion.2
  203.4 34.8 %all-reduce.7.cloned.1.call-done = bf16[1,2,1536,64]{3,2,1,0:T(8,128)(2,1)} async-done(((bf16[1,2,1536,64]{3,2,1,0:T(8,128)(2,1)}), bf16[1,2,1536,64]{3,2,1,0:T(8,128)(2,1)}) %all-reduce.7.cloned.1.call-update) | async-done | bytes 393232 | tf_op jit(solution)/shard_map/while/body/eval_jaxpr/psum | solution.py:14
  238.2 2.1 constant_dynamic-update-slice_fusion.5
  247.0 1.0 broadcast_select_fusion.2
  248.1 34.8 %all-reduce.7.cloned.1.call-done = bf16[1,2,1536,64]{3,2,1,0:T(8,128)(2,1)} async-done(((bf16[1,2,1536,64]{3,2,1,0:T(8,128)(2,1)}), bf16[1,2,1536,64]{3,2,1,0:T(8,128)(2,1)}) %all-reduce.7.cloned.1.call-update) | async-done | bytes 393232 | tf_op jit(solution)/shard_map/while/body/eval_jaxpr/psum | solution.py:14
  282.9 2.1 constant_dynamic-update-slice_fusion.5
  285.0 2.6 fusion.20
  287.6 22.5 %all-reduce.8 = bf16[3,128,2,64]{1,3,2,0:T(8,128)(2,1)S(1)} all-reduce(f32[3,128,2,64]{1,3,2,0:T(8,128)S(1)} %fusion.20), channel_id=1, replica_groups=mesh['groups'=2,'wide'=4,'expert'=4] {'expert'}, use_global_device_ids=true, to_apply=%region_7.8 | all-reduce | flops 49152 | bytes 294912 | tf_op jit(solution)/shard_map/psum | solution.py:68
  310.1 0.8 multiply_bitcast_fusion
  311.1 1.2 slice-done.1
  312.2 15.1 %fusion.2 = f32[384,2,1024]{2,0,1:T(8,128)} fusion(bf16[2,6144,1024]{2,1,0:T(8,128)(2,1)} %param.19, bf16[384,6144]{1,0:T(8,128)(2,1)S(1)} %bitcast.68), kind=kOutput, calls=%fused_computation.6 | convolution fusion | flops 9663676416 | bytes 33030144 | tf_op jit(solution)/shard_map/td,edf->tef/dot_general | solution.py:81
  327.4 16.2 %fusion.5 = bf16[384,2,1024]{2,0,1:T(8,128)(2,1)} fusion(f32[3,128,2,1024]{3,1,0,2:T(8,128)S(1)} %copy.15, f32[384,2,1024]{2,0,1:T(8,128)} %fusion.2, f32[384,2]{0,1:T(2,128)S(1)} %fusion.13, bf16[2,6144,1024]{2,1,0:T(8,128)(2,1)} %param.20, bf16[384,6144]{1,0:T(8,128)(2,1)S(1)} %bitcast.68), kind=kOutput, calls=%fused_computation.10 | convolution fusion | flops 9669967872 | bytes 37751808 | tf_op jit(solution)/shard_map/td,edf->tef/dot_general | solution.py:85
  343.7 113.3 %all-gather.4.cloned.1.call-done = bf16[384,2,4096]{2,0,1:T(8,128)(2,1)} async-done(((bf16[384,2,1024]{2,0,1:T(8,128)(2,1)}), bf16[384,2,4096]{2,0,1:T(8,128)(2,1)}) %all-gather.4.cloned.1.call-update) | async-done | bytes 6291472 | tf_op jit(solution)/shard_map/all_gather | solution.py:91
  456.9 17.7 %convolution_bitcast_fusion = f32[384,1536]{1,0:T(8,128)} fusion(bf16[384,2,4096]{2,0,1:T(8,128)(2,1)} %all-gather.4.cloned.1.call-done, bf16[2,4096,1536]{2,1,0:T(8,128)(2,1)} %param.21), kind=kOutput, calls=%fused_computation.12 | convolution fusion | flops 9663676416 | bytes 33816576 | tf_op jit(solution)/shard_map/tef,efd->td/dot_general | solution.py:89
  474.6 31.4 %reduce-scatter.2.cloned.1.call-done = f32[96,1536]{1,0:T(8,128)} async-done(((f32[384,1536]{1,0:T(8,128)}), f32[96,1536]{1,0:T(8,128)}) %reduce-scatter.2.cloned.1.call-update) | async-done | bytes 589840 | tf_op jit(solution)/shard_map/reduce_scatter | solution.py:95
  506.0 1.8 convert_element_type.20
  (65 shorter events, 7.8 us)
Async XLA Ops:
  6.5 47.3 %copy-start = (bf16[8,2,64,1024]{3,2,1,0:T(8,128)(2,1)S(1)}, bf16[8,2,64,1024]{3,2,1,0:T(8,128)(2,1)}, u32[]{:S(2)}) copy-start(bf16[8,2,64,1024]{3,2,1,0:T(8,128)(2,1)} %param.23) | copy-start | bytes 6291460
  6.5 42.2 %all-gather.6.cloned.1.call-start = ((), (), s32[]{:S(2)}) async-start(), calls=%async_computation.3 | async-start | bytes 1966080 | tf_op jit(solution)/shard_map/all_gather | solution.py:33
  7.3 138.6 %all-reduce.5.cloned.1.call-start = ((), (), s32[]{:S(2)}) async-start(), calls=%async_computation.4 | async-start | bytes 9437184 | tf_op jit(solution)/shard_map/psum | solution.py:14
  52.4 0.7 copy-start.10
  52.4 0.7 copy-start.2
  52.4 1.3 copy-start.9
  145.9 1.9 copy-start.7
  145.9 2.4 copy-start.6
  147.8 1.0 copy-start.8
  148.8 2.1 copy-start.3
  148.8 2.1 copy-start.4
  150.9 42.7 %all-reduce.7.cloned.1.call-start = ((), (), s32[]{:S(2)}) async-start(), calls=%async_computation.5 | async-start | bytes 1572864 | tf_op jit(solution)/shard_map/while/body/eval_jaxpr/psum | solution.py:14
  195.7 42.6 %all-reduce.7.cloned.1.call-start = ((), (), s32[]{:S(2)}) async-start(), calls=%async_computation.5 | async-start | bytes 1572864 | tf_op jit(solution)/shard_map/while/body/eval_jaxpr/psum | solution.py:14
  240.3 42.6 %all-reduce.7.cloned.1.call-start = ((), (), s32[]{:S(2)}) async-start(), calls=%async_computation.5 | async-start | bytes 1572864 | tf_op jit(solution)/shard_map/while/body/eval_jaxpr/psum | solution.py:14
  285.0 25.1 %copy-start.5 = (bf16[3,2,64,1024]{3,0,2,1:T(4,128)(2,1)S(1)}, bf16[3,2,64,1024]{3,0,2,1:T(4,128)(2,1)}, u32[]{:S(2)}) copy-start(bf16[3,2,64,1024]{3,0,2,1:T(4,128)(2,1)} %fusion.6) | copy-start | bytes 2359300
  285.0 171.9 %all-gather.4.cloned.1.call-start = ((), (), s32[]{:S(2)}) async-start(), calls=%async_computation.1 | async-start | bytes 7864320 | tf_op jit(solution)/shard_map/all_gather | solution.py:91
  285.0 26.1 %slice-start = ((s8[4718592]{0:T(1024)(128)(4,1)}), s8[524288]{0:T(1024)(128)(4,1)S(1)}, s32[]{:S(2)}) async-start(s8[4718592]{0:T(1024)(128)(4,1)} %bitcast.67), calls=%async_computation.6 | async-start | bytes 1048576
  310.1 2.2 slice-start.1
  343.6 162.4 %reduce-scatter.2.cloned.1.call-start = ((), (), s32[]{:S(2)}) async-start(), calls=%async_computation.2 | async-start | bytes 2949120 | tf_op jit(solution)/shard_map/reduce_scatter | solution.py:95
  456.9 50.9 %copy-start.1 = (bf16[8,2,64,1024]{3,2,1,0:T(8,128)(2,1)S(1)}, bf16[8,2,64,1024]{3,2,1,0:T(8,128)(2,1)}, u32[]{:S(2)}) copy-start(bf16[8,2,64,1024]{3,2,1,0:T(8,128)(2,1)} %param.23) | copy-start | bytes 6291460
Sparse Core Ops, SparseCore 0:
  8.9 39.7 all-gather.5
  52.6 93.2 all-reduce.4
  158.8 34.7 all-reduce.6
  203.5 34.6 all-reduce.6
  248.2 34.6 all-reduce.6
  343.7 113.1 all-gather.3
  474.7 31.2 reduce-scatter.1
where the time goes:
time: 515 us
  waiting for transfers between devices  378 us (73%)
  matrix products  56.1 us (11%)
  blocking collectives  22.5 us (4%)
  local copies, waits for them, and re-layouts  20.4 us (4%)
  between operations  15.4 us (3%)
  loops' own time  13.7 us (3%)
  other arithmetic  8.61 us (2%)
    psum x4, waiting for transfers between devices, spread(): return lax.psum(block, axis)  194 us
    all_gather x1, waiting for transfers between devices, per_device(): lax.all_gather(hidden, 'expert', axis=2, tiled=True)  113 us
    all_gather x1, waiting for transfers between devices, per_device(): full_slot = lax.all_gather(own_slot, 'expert', axis=1, tiled=True)  38.3 us
    reduce_scatter x1, waiting for transfers between devices, per_device(): lax.psum_scatter(partial_out, 'wide', scatter_dimension=0, tiled=True)  31.4 us
    psum x1, blocking collectives, per_device(): summed = lax.psum(partial_rank, 'expert')  22.5 us
    dot_general x1, matrix products, per_device(): jnp.einsum('tef,efd->td', lax.all_gather(hidden, 'expert', axis=2, tiled=...  17.7 us
    dot_general x1, matrix products, per_device(): jnp.einsum('td,edf->tef', input_rows, up_weight, preferred_element_type=j...  16.2 us
    dot_general x1, matrix products, per_device(): jnp.einsum('td,edf->tef', input_rows, gate_weight, preferred_element_type...  15.1 us
  transfers between devices with their start and end apart: 7, of which 7 were waited for; matrix products, arithmetic and copies ran while one was open for 1% of the time, Pallas kernels for 0%

commit v1 on v0

v1 whole, which is shorter than its diff:
```python
import jax
import jax.numpy as jnp
import numpy as np
from jax import lax
from jax.sharding import Mesh
from jax.sharding import PartitionSpec as P

ADAPTER_SCALE = 0.5

WIDE = ("wy", "wc")
GROUP = ("wy", "wc", "expert")


def per_device(
    prompts,
    span_slot_owner,
    row_expert_index,
    tile_tenant_index,
    tenant_adapter_slot,
    router,
    gate_weight,
    up_weight,
    down_weight,
    adapter_down_weight,
    adapter_up_weight,
):
    span = prompts.shape[1]
    quarter = prompts.shape[2]
    tokens = row_expert_index.shape[0]
    nchunk = tokens // span
    window = gate_weight.shape[0]
    core = lax.axis_index("wc")
    cores = lax.axis_size("wc")
    wide_index = lax.axis_index(WIDE)

    slots_q = lax.all_gather(prompts, WIDE, axis=0, tiled=True)
    rows_q = jnp.take(slots_q, span_slot_owner[:nchunk], axis=0).reshape(tokens, quarter)

    half = tokens // cores
    mine_q = lax.dynamic_slice_in_dim(rows_q, core * half, half, 0)
    mine = lax.all_gather(mine_q, "expert", axis=1, tiled=True)
    input_rows = lax.all_gather(mine, "wc", axis=0, tiled=True)

    logits = jnp.dot(input_rows, router, preferred_element_type=jnp.float32)
    experts = jnp.arange(router.shape[1], dtype=jnp.int32)
    picked = (row_expert_index[:, :, None] == experts[None, None, :]).astype(jnp.float32)
    chosen = jnp.sum(picked * logits[:, None, :], axis=2)
    first_prob = jax.nn.sigmoid(chosen[:, 0] - chosen[:, 1])
    second_prob = jax.nn.sigmoid(chosen[:, 1] - chosen[:, 0])
    weight = (
        first_prob[:, None] * picked[:, 0, :window] + second_prob[:, None] * picked[:, 1, :window]
    )

    tile_count = tile_tenant_index.shape[0]
    tile_rows = tokens // tile_count
    resident_slots = adapter_down_weight.shape[0]
    tile_slot_index = jnp.take(tenant_adapter_slot, tile_tenant_index)
    owners = tile_slot_index // resident_slots
    local_index = tile_slot_index % resident_slots
    held = jnp.take(adapter_down_weight, local_index, axis=0)
    partial_rank = jnp.einsum(
        "ntd,nedr->nter",
        rows_q.reshape(tile_count, tile_rows, quarter),
        held,
        preferred_element_type=jnp.float32,
    )
    partial_rank = jnp.where(
        (owners == wide_index)[:, None, None, None], partial_rank, jnp.zeros_like(partial_rank)
    )
    lowrank = lax.psum(partial_rank, GROUP).astype(jnp.bfloat16)
    tile_up = jnp.take(adapter_up_weight, tile_tenant_index, axis=0)
    adapted_hidden = jnp.einsum(
        "nter,nerf->ntef", lowrank, tile_up, preferred_element_type=jnp.float32
    ).reshape(tokens, window, tile_up.shape[3])

    running = None
    for expert_number in range(window):
        gate_pre = jnp.dot(
            input_rows, gate_weight[expert_number], preferred_element_type=jnp.float32
        )
        up_value = (
            jnp.dot(input_rows, up_weight[expert_number], preferred_element_type=jnp.float32)
            + ADAPTER_SCALE * adapted_hidden[:, expert_number]
        )
        hidden = (
            weight[:, expert_number, None] * jax.nn.silu(gate_pre) * up_value
        ).astype(jnp.bfloat16)
        gathered = lax.all_gather(hidden, "expert", axis=1, tiled=True)
        part = jnp.dot(gathered, down_weight[expert_number], preferred_element_type=jnp.float32)
        running = part if running is None else running + part
    mixed_rows = lax.psum_scatter(running, WIDE, scatter_dimension=0, tiled=True)
    return mixed_rows.astype(jnp.bfloat16)


def solution(mesh):
    groups = mesh.shape["groups"]
    wide = mesh.shape["wide"]
    expert = mesh.shape["expert"]
    split = Mesh(
        np.asarray(mesh.devices).reshape(groups, wide // 2, 2, expert),
        ("groups", "wy", "wc", "expert"),
    )
    rows = ("groups", "wy", "wc")
    in_specs = (
        P(rows, None, "expert"),
        P("groups"),
        P("groups", None),
        P("groups"),
        P("groups"),
        P(),
        P(None, None, GROUP),
        P(None, None, GROUP),
        P(None, WIDE, "expert"),
        P(rows, None, "expert", None),
        P("groups", None, None, GROUP),
    )
    out_specs = P(rows, "expert")
    return jax.shard_map(
        per_device, mesh=split, in_specs=in_specs, out_specs=out_specs, check_vma=False
    )
```

time: 515 us -> 352 us (0.68)
  waiting for transfers between devices: 378 us -> 201 us
  blocking collectives: 22.5 us -> 62 us
  loops' own time: 13.7 us -> 0 us
  local copies, waits for them, and re-layouts: 20.4 us -> 8.18 us
  matrix products: 56.1 us -> 62.8 us
    psum x4 -> x0, waiting for transfers between devices: 194 us -> none  [spread(): return lax.psum(block, axis)]
    psum x1, blocking collectives: 22.5 us -> 62 us  [per_device(): lowrank = lax.psum(partial_rank, GROUP).astype(jnp.bfloat16)]
    all_gather x2 -> x5, waiting for transfers between devices: 152 us -> 168 us  [the longest x2 94.4 us: per_device(): gathered = lax.all_gather(hidden, 'expert', axis=1, tiled=True)]
    another operation x1 -> x0, loops' own time: 13.7 us -> none  [per_device(): lax.scan(fetch_one, jnp.int32(0), jnp.arange(tile_count, dtype=jnp.int32))]
    dynamic_slice x16 -> x1, local copies, waits for them, and re-layouts: 6.59 us -> 0.08 us  [per_device(): mine_q = lax.dynamic_slice_in_dim(rows_q, core * half, half, 0)]
    dynamic_update_slice x3 -> x0, local copies, waits for them, and re-layouts: 6.26 us -> none  [per_device(): lax.scan(fetch_one, jnp.int32(0), jnp.arange(tile_count, dtype=jnp.int32))]
    select_n x7 -> x4, other arithmetic: 6.71 us -> 1.46 us  [the longest x1 1.19 us: per_device(): jnp.take(slots_q, span_slot_owner[:nchunk], axis=0).reshape(tokens, quarter)]
    dot_general x5 -> x6, matrix products: 54 us -> 57.9 us  [the longest x2 20.5 us: per_device(): jnp.dot(gathered, down_weight[expert_number], preferred_element_type=jnp....]
  transfers between devices with their start and end apart: 7 -> 6, of which waited for: 7 -> 5; matrix products, arithmetic and copies ran while one was open for 1% -> 11% of each run, Pallas kernels for 0% -> 0%
where the time goes in v1:
time: 352 us
  waiting for transfers between devices  201 us (57%)
  matrix products  62.8 us (18%)
  blocking collectives  62 us (18%)
  between operations  13.7 us (4%)
  local copies, waits for them, and re-layouts  8.18 us (2%)
  other arithmetic  4.06 us (1%)
    all_gather x2, waiting for transfers between devices, per_device(): gathered = lax.all_gather(hidden, 'expert', axis=1, tiled=True)  94.4 us
    psum x1, blocking collectives, per_device(): lowrank = lax.psum(partial_rank, GROUP).astype(jnp.bfloat16)  62 us
    all_gather x1, waiting for transfers between devices, per_device(): mine = lax.all_gather(mine_q, 'expert', axis=1, tiled=True)  50.5 us
    reduce_scatter x1, waiting for transfers between devices, per_device(): lax.psum_scatter(running, WIDE, scatter_dimension=0, tiled=True)  31.9 us
    all_gather x1, waiting for transfers between devices, per_device(): slots_q = lax.all_gather(prompts, WIDE, axis=0, tiled=True)  23.2 us
    dot_general x2, matrix products, per_device(): jnp.dot(gathered, down_weight[expert_number], preferred_element_type=jnp....  20.5 us
    dot_general x2, matrix products, per_device(): jnp.dot(input_rows, gate_weight[expert_number], preferred_element_type=jn...  19.6 us
    dot_general x2, matrix products, per_device(): jnp.dot(input_rows, up_weight[expert_number], preferred_element_type=jnp....  17.8 us
  transfers between devices with their start and end apart: 6, of which 5 were waited for; matrix products, arithmetic and copies ran while one was open for 11% of the time, Pallas kernels for 0%

profile of v1, /device:TPU:0, one launch (start us, length us, event | category | flops | bytes accessed | tf_op | source)
XLA Modules:
  0.0 351.9 jit_solution(3892074524616595105)
XLA Ops:
  6.5 0.7 all-gather.6.cloned.1.call-update
  7.3 0.7 compare_and_fusion.2
  8.0 0.1 broadcast_bitcast_fusion
  8.1 0.1 dynamic-slice
  8.1 23.2 %all-gather.6.cloned.1.call-done = bf16[4,128,1536]{2,1,0:T(8,128)(2,1)} async-done(((bf16[1,128,1536]{2,1,0:T(8,128)(2,1)}), bf16[4,128,1536]{2,1,0:T(8,128)(2,1)}) %all-gather.6.cloned.1.call-update) | async-done | bytes 1572880 | tf_op jit(solution)/shard_map/all_gather | solution.py:36
  31.3 2.0 gather_fusion
  33.4 1.2 dynamic-slice_select_fusion
  34.7 50.5 %all-gather.8.cloned.1.call-done = bf16[192,6144]{1,0:T(8,128)(2,1)} async-done(((bf16[192,1536]{1,0:T(8,128)(2,1)}), bf16[192,6144]{1,0:T(8,128)(2,1)}) %all-gather.8.cloned.1.call-update) | async-done | bytes 2359312 | tf_op jit(solution)/shard_map/all_gather | solution.py:41
  85.3 0.6 gather_fusion.2
  86.0 1.6 gather_fusion.1
  87.6 0.6 gather_fusion.3
  88.2 0.0 copy-done.11
  88.3 0.2 broadcast_select_fusion
  88.5 1.1 copy-done.9
  89.6 0.5 fusion.33
  90.1 0.1 broadcast_select_fusion.1
  90.2 62.0 %all-reduce.1 = bf16[3,128,2,64]{1,3,2,0:T(8,128)(2,1)S(1)} all-reduce(f32[3,128,2,64]{1,3,2,0:T(8,128)S(1)} %broadcast_select_fusion.1), channel_id=1, replica_groups=mesh['groups'=2,'wy'=2,'wc'=2,'expert'=4] {'wy','wc','expert'}, use_global_device_ids=true, to_apply=%region_1.2 | all-reduce | flops 49152 | bytes 294912 | tf_op jit(solution)/shard_map/psum | solution.py:70
  152.2 0.6 convolution_bitcast_fusion
  152.8 2.0 copy.17
  154.8 3.8 %fusion.48 = f32[384,8]{0,1:T(8,128)S(1)} fusion(bf16[384,6144]{1,0:T(8,128)(2,1)} %all-gather.10.cloned.1.call-done, bf16[6144,8]{0,1:T(8,128)(2,1)S(1)} %copy-done.10), kind=kOutput, calls=%fused_computation.76 | convolution fusion | flops 37748736 | bytes 4829184 | tf_op jit(solution)/shard_map/dot_general | solution.py:44
  158.7 8.2 %fusion.2 = f32[384,1024]{1,0:T(8,128)S(1)} fusion(bf16[384,6144]{1,0:T(8,128)(2,1)S(1)} %copy-done.4, bf16[2,6144,1024]{2,1,0:T(8,128)(2,1)} %param.18), kind=kOutput, calls=%fused_computation.6 | convolution fusion | flops 4831838208 | bytes 18874368 | tf_op jit(solution)/shard_map/dot_general | solution.py:82
  166.9 9.1 %fusion.24 = bf16[384,1024]{1,0:T(8,128)(2,1)} fusion(f32[384,1024]{1,0:T(8,128)S(1)} %fusion.2, f32[384,2,1024]{2,0,1:T(8,128)S(1)} %bitcast.72, bf16[384,6144]{1,0:T(8,128)(2,1)S(1)} %copy-done.4, bf16[2,6144,1024]{2,1,0:T(8,128)(2,1)} %param.17, f32[384]{0:T(512)S(1)} %get-tuple-element.6), kind=kOutput, calls=%fused_computation.28 | convolution fusion | flops 4835377152 | bytes 21235200 | tf_op jit(solution)/shard_map/dot_general | solution.py:78
  176.1 0.0 all-gather.12.cloned.1.call-start
  176.1 9.6 %fusion.8 = f32[384,1024]{1,0:T(8,128)S(1)} fusion(bf16[384,6144]{1,0:T(8,128)(2,1)} %all-gather.10.cloned.1.call-done, bf16[2,6144,1024]{2,1,0:T(8,128)(2,1)} %param.18), kind=kOutput, calls=%fused_computation.12 | convolution fusion | flops 4831838208 | bytes 18874368 | tf_op jit(solution)/shard_map/dot_general | solution.py:82
  185.7 10.5 %fusion.28 = bf16[384,1024]{1,0:T(8,128)(2,1)} fusion(f32[384,1024]{1,0:T(8,128)S(1)} %fusion.8, f32[384,2,1024]{2,0,1:T(8,128)S(1)} %bitcast.73, bf16[384,6144]{1,0:T(8,128)(2,1)} %all-gather.10.cloned.1.call-done, bf16[2,6144,1024]{2,1,0:T(8,128)(2,1)} %param.17, f32[384]{0:T(512)S(1)} %get-tuple-element.5), kind=kOutput, calls=%fused_computation.33 | convolution fusion | flops 4835377152 | bytes 21235200 | tf_op jit(solution)/shard_map/dot_general | solution.py:78
  196.3 0.2 reduce-scatter.2.cloned.1.call-start
  196.5 40.8 %all-gather.14.cloned.1.call-done = bf16[384,4096]{1,0:T(8,128)(2,1)} async-done(((bf16[384,1024]{1,0:T(8,128)(2,1)}), bf16[384,4096]{1,0:T(8,128)(2,1)}) %all-gather.14.cloned.1.call-update) | async-done | bytes 3145744 | tf_op jit(solution)/shard_map/all_gather | solution.py:88
  237.2 10.0 %fusion = f32[384,1536]{1,0:T(8,128)} fusion(bf16[384,4096]{1,0:T(8,128)(2,1)} %all-gather.14.cloned.1.call-done, bf16[2,4096,1536]{2,1,0:T(8,128)(2,1)} %param.19), kind=kOutput, calls=%fused_computation.4 | convolution fusion | flops 4831838208 | bytes 18087936 | tf_op jit(solution)/shard_map/dot_general | solution.py:89
  247.2 53.6 %all-gather.12.cloned.1.call-done = bf16[384,4096]{1,0:T(8,128)(2,1)} async-done(((bf16[384,1024]{1,0:T(8,128)(2,1)}), bf16[384,4096]{1,0:T(8,128)(2,1)}) %all-gather.12.cloned.1.call-update) | async-done | bytes 3145744 | tf_op jit(solution)/shard_map/all_gather | solution.py:88
  300.9 10.5 %fusion.18 = f32[384,1536]{1,0:T(8,128)} fusion(f32[384,1536]{1,0:T(8,128)} %fusion, bf16[384,4096]{1,0:T(8,128)(2,1)} %all-gather.12.cloned.1.call-done, bf16[2,4096,1536]{2,1,0:T(8,128)(2,1)} %param.19), kind=kOutput, calls=%fused_computation.22 | convolution fusion | flops 4832428032 | bytes 20447232 | tf_op jit(solution)/shard_map/dot_general | solution.py:89
  311.4 31.9 %reduce-scatter.2.cloned.1.call-done = f32[96,1536]{1,0:T(8,128)} async-done(((f32[384,1536]{1,0:T(8,128)}), f32[96,1536]{1,0:T(8,128)}) %reduce-scatter.2.cloned.1.call-update) | async-done | bytes 589840 | tf_op jit(solution)/shard_map/reduce_scatter | solution.py:91
  343.3 1.8 convert_element_type.19
  (45 shorter events, 0.4 us)
Async XLA Ops:
  6.5 79.5 %copy-start = (bf16[8,2,64,1024]{3,2,1,0:T(8,128)(2,1)S(1)}, bf16[8,2,64,1024]{3,2,1,0:T(8,128)(2,1)}, u32[]{:S(2)}) copy-start(bf16[8,2,64,1024]{3,2,1,0:T(8,128)(2,1)} %param.21) | copy-start | bytes 6291460
  6.5 24.8 %all-gather.6.cloned.1.call-start = ((), (), s32[]{:S(2)}) async-start(), calls=%async_computation.1 | async-start | bytes 1966080 | tf_op jit(solution)/shard_map/all_gather | solution.py:36
  7.3 78.0 %all-gather.8.cloned.1.call-start = ((), (), s32[]{:S(2)}) async-start(), calls=%async_computation.2 | async-start | bytes 2949120 | tf_op jit(solution)/shard_map/all_gather | solution.py:41
  33.3 1.2 copy-start.8
  33.4 51.9 %copy-start.12 = (s32[3]{0:T(128)S(1)}, s32[3]{0:T(128)}, u32[]{:S(2)}) copy-start(s32[3]{0:T(128)} %param.14) | copy-start | bytes 40
  33.4 52.0 %copy-start.2 = (s32[8]{0:T(128)S(1)}, s32[8]{0:T(128)}, u32[]{:S(2)}) copy-start(s32[8]{0:T(128)} %param.15) | copy-start | bytes 100
  34.6 53.0 %copy-start.3 = (bf16[2,2,1536,64]{2,3,1,0:T(8,128)(2,1)S(1)}, bf16[2,2,1536,64]{2,3,1,0:T(8,128)(2,1)}, u32[]{:S(2)}) copy-start(bf16[2,2,1536,64]{2,3,1,0:T(8,128)(2,1)} %param.20) | copy-start | bytes 2359300
  34.6 120.2 %all-gather.10.cloned.1.call-start = ((), (), s32[]{:S(2)}) async-start(), calls=%async_computation.3 | async-start | bytes 7077888 | tf_op jit(solution)/shard_map/all_gather | solution.py:42
  85.2 152.0 %all-gather.14.cloned.1.call-start = ((), (), s32[]{:S(2)}) async-start(), calls=%async_computation.5 | async-start | bytes 3932160 | tf_op jit(solution)/shard_map/all_gather | solution.py:88
  87.6 0.7 copy-start.11
  88.3 1.3 copy-start.9
  88.5 63.7 %copy-start.7 = (bf16[3,2,64,1024]{3,2,1,0:T(8,128)(2,1)S(1)}, bf16[3,2,64,1024]{3,2,1,0:T(8,128)(2,1)}, u32[]{:S(2)}) copy-start(bf16[3,2,64,1024]{3,2,1,0:T(8,128)(2,1)} %gather_fusion.1) | copy-start | bytes 2359300
  152.8 2.0 copy-start.10
  154.8 3.9 %copy-start.4 = (bf16[384,6144]{1,0:T(8,128)(2,1)S(1)}, bf16[384,6144]{1,0:T(8,128)(2,1)}, u32[]{:S(2)}) copy-start(bf16[384,6144]{1,0:T(8,128)(2,1)} %all-gather.10.cloned.1.call-done) | copy-start | bytes 14155780
  158.7 8.2 %copy-start.5 = (f32[3,128,2,1024]{3,1,0,2:T(8,128)S(1)}, f32[3,128,2,1024]{3,1,0,2:T(8,128)}, u32[]{:S(2)}) copy-start(f32[3,128,2,1024]{3,1,0,2:T(8,128)} %copy.17) | copy-start | bytes 9437188
  176.1 124.8 %all-gather.12.cloned.1.call-start = ((), (), s32[]{:S(2)}) async-start(), calls=%async_computation.4 | async-start | bytes 3932160 | tf_op jit(solution)/shard_map/all_gather | solution.py:88
  176.1 9.6 %copy-start.6 = (f32[3,128,2,1024]{3,1,0,2:T(8,128)S(1)}, f32[3,128,2,1024]{3,1,0,2:T(8,128)}, u32[]{:S(2)}) copy-start(f32[3,128,2,1024]{3,1,0,2:T(8,128)} %copy.17) | copy-start | bytes 9437188
  196.3 147.0 %reduce-scatter.2.cloned.1.call-start = ((), (), s32[]{:S(2)}) async-start(), calls=%async_computation.6 | async-start | bytes 2949120 | tf_op jit(solution)/shard_map/reduce_scatter | solution.py:91
  300.9 44.2 %copy-start.1 = (bf16[8,2,64,1024]{3,2,1,0:T(8,128)(2,1)S(1)}, bf16[8,2,64,1024]{3,2,1,0:T(8,128)(2,1)}, u32[]{:S(2)}) copy-start(bf16[8,2,64,1024]{3,2,1,0:T(8,128)(2,1)} %param.21) | copy-start | bytes 6291460
Sparse Core Ops, SparseCore 0:
  8.9 22.3 all-gather.5
  34.7 50.4 all-gather.7
  86.8 13.2 all-gather.9
  176.2 61.0 all-gather.13
  238.7 62.1 all-gather.11
  311.5 31.7 reduce-scatter.1

commit v2 on v1

--- a/solution.py
+++ b/solution.py
@@ -39,7 +39,10 @@
     half = tokens // cores
     mine_q = lax.dynamic_slice_in_dim(rows_q, core * half, half, 0)
     mine = lax.all_gather(mine_q, "expert", axis=1, tiled=True)
-    input_rows = lax.all_gather(mine, "wc", axis=0, tiled=True)
+    other = lax.ppermute(mine, "wc", [(i, (i + 1) % cores) for i in range(cores)])
+    first = jnp.where(core == 0, mine, other)
+    second = jnp.where(core == 0, other, mine)
+    input_rows = jnp.concatenate([first, second], axis=0)
 
     logits = jnp.dot(input_rows, router, preferred_element_type=jnp.float32)
     experts = jnp.arange(router.shape[1], dtype=jnp.int32)
@@ -67,10 +70,10 @@
     partial_rank = jnp.where(
         (owners == wide_index)[:, None, None, None], partial_rank, jnp.zeros_like(partial_rank)
     )
-    lowrank = lax.psum(partial_rank, GROUP).astype(jnp.bfloat16)
+    lowrank = lax.reduce_precision(lax.psum(partial_rank, GROUP), exponent_bits=8, mantissa_bits=7)
     tile_up = jnp.take(adapter_up_weight, tile_tenant_index, axis=0)
     adapted_hidden = jnp.einsum(
-        "nter,nerf->ntef", lowrank, tile_up, preferred_element_type=jnp.float32
+        "nter,nerf->ntef", lowrank, tile_up.astype(jnp.float32), preferred_element_type=jnp.float32
     ).reshape(tokens, window, tile_up.shape[3])
 
     running = None

time: 352 us -> 383 us (1.088)
  waiting for transfers between devices: 201 us -> 290 us
  blocking collectives: 62 us -> 0 us
    psum x0 -> x1, waiting for transfers between devices: none -> 88.2 us  [per_device(): lax.psum(partial_rank, GROUP)]
    psum x1 -> x0, blocking collectives: 62 us -> none  [per_device(): lowrank = lax.psum(partial_rank, GROUP).astype(jnp.bfloat16)]
  transfers between devices with their start and end apart: 6 -> 7, of which waited for: 5 -> 6; matrix products, arithmetic and copies ran while one was open for 11% -> 10% of each run, Pallas kernels for 0% -> 0%
where the time goes in v2:
time: 383 us
  waiting for transfers between devices  290 us (76%)
  matrix products  63.1 us (16%)
  between operations  13.8 us (4%)
  local copies, waits for them, and re-layouts  8.6 us (2%)
  other arithmetic  6.66 us (2%)
    all_gather x2, waiting for transfers between devices, per_device(): gathered = lax.all_gather(hidden, 'expert', axis=1, tiled=True)  95.5 us
    psum x1, waiting for transfers between devices, per_device(): lax.psum(partial_rank, GROUP)  88.2 us
    all_gather x1, waiting for transfers between devices, per_device(): mine = lax.all_gather(mine_q, 'expert', axis=1, tiled=True)  50.6 us
    reduce_scatter x1, waiting for transfers between devices, per_device(): lax.psum_scatter(running, WIDE, scatter_dimension=0, tiled=True)  31.9 us
    all_gather x1, waiting for transfers between devices, per_device(): slots_q = lax.all_gather(prompts, WIDE, axis=0, tiled=True)  23.2 us
    dot_general x2, matrix products, per_device(): jnp.dot(input_rows, up_weight[expert_number], preferred_element_type=jnp....  21.6 us
    dot_general x2, matrix products, per_device(): jnp.dot(gathered, down_weight[expert_number], preferred_element_type=jnp....  20.5 us
    dot_general x2, matrix products, per_device(): jnp.dot(input_rows, gate_weight[expert_number], preferred_element_type=jn...  17.7 us
  transfers between devices with their start and end apart: 7, of which 6 were waited for; matrix products, arithmetic and copies ran while one was open for 10% of the time, Pallas kernels for 0%

profile of v2, /device:TPU:0, one launch (start us, length us, event | category | flops | bytes accessed | tf_op | source)
XLA Modules:
  0.0 382.7 jit_solution(16340851096399354820)
XLA Ops:
  6.5 0.7 all-gather.5.cloned.1.call-update
  7.3 0.7 compare_and_fusion.2
  8.0 0.1 broadcast_bitcast_fusion
  8.1 0.1 dynamic-slice
  8.1 23.2 %all-gather.5.cloned.1.call-done = bf16[4,128,1536]{2,1,0:T(8,128)(2,1)} async-done(((bf16[1,128,1536]{2,1,0:T(8,128)(2,1)}), bf16[4,128,1536]{2,1,0:T(8,128)(2,1)}) %all-gather.5.cloned.1.call-update) | async-done | bytes 1572880 | tf_op jit(solution)/shard_map/all_gather | solution.py:36
  31.3 2.0 gather_fusion
  33.4 1.1 dynamic-slice_select_fusion
  34.6 50.6 %all-gather.7.cloned.1.call-done = bf16[192,6144]{1,0:T(8,128)(2,1)} async-done(((bf16[192,1536]{1,0:T(8,128)(2,1)}), bf16[192,6144]{1,0:T(8,128)(2,1)}) %all-gather.7.cloned.1.call-update) | async-done | bytes 2359312 | tf_op jit(solution)/shard_map/all_gather | solution.py:41
  85.2 0.6 gather_fusion.2
  85.9 1.8 gather_fusion.3
  87.7 0.2 broadcast_select_fusion.2
  87.8 1.1 copy-done.6
  88.9 0.5 fusion.33
  89.5 0.8 broadcast_select_fusion.3
  90.3 0.6 gather_fusion.1
  90.9 88.2 %all-reduce.2.cloned.1.call-done = f32[3,128,2,64]{1,3,2,0:T(8,128)} async-done(((f32[3,128,2,64]{1,3,2,0:T(8,128)}), f32[3,128,2,64]{1,3,2,0:T(8,128)}) %all-reduce.2.cloned.1.call-update) | async-done | bytes 196624 | tf_op jit(solution)/shard_map/psum | solution.py:73
  179.1 1.6 convolution_bitcast_fusion
  180.7 0.4 copy.17
  181.1 1.9 copy-done.7
  183.0 2.0 broadcast_select_fusion.1
  185.0 1.3 fusion.48
  186.4 8.1 %fusion.4 = f32[384,1024]{1,0:T(8,128)S(1)} fusion(bf16[2,6144,1024]{2,1,0:T(8,128)(2,1)} %param.17, bf16[192,6144]{1,0:T(8,128)(2,1)S(1)} %get-tuple-element.16, bf16[192,6144]{1,0:T(8,128)(2,1)S(1)} %get-tuple-element.15), kind=kOutput, calls=%fused_computation.8 | convolution fusion | flops 4841275392 | bytes 18874368 | tf_op jit(solution)/shard_map/dot_general | solution.py:81
  194.6 10.7 %fusion.24 = bf16[384,1024]{1,0:T(8,128)(2,1)} fusion(f32[384,2,1024]{2,0,1:T(8,128)S(1)} %bitcast.66, f32[384,1024]{1,0:T(8,128)S(1)} %fusion.4, bf16[2,6144,1024]{2,1,0:T(8,128)(2,1)} %param.18, f32[384]{0:T(512)S(1)} %get-tuple-element.6, bf16[192,6144]{1,0:T(8,128)(2,1)S(1)} %get-tuple-element.16, bf16[192,6144]{1,0:T(8,128)(2,1)S(1)} %get-tuple-element.15), kind=kOutput, calls=%fused_computation.31 | convolution fusion | flops 4844814336 | bytes 21235200 | tf_op jit(solution)/shard_map/dot_general | solution.py:85
  205.4 0.2 all-gather.9.cloned.1.call-start
  205.6 9.5 %fusion.10 = f32[384,1024]{1,0:T(8,128)S(1)} fusion(bf16[2,6144,1024]{2,1,0:T(8,128)(2,1)} %param.17, bf16[192,6144]{1,0:T(8,128)(2,1)} %copy-done.10, bf16[192,6144]{1,0:T(8,128)(2,1)} %copy-done.8), kind=kOutput, calls=%fused_computation.14 | convolution fusion | flops 4841275392 | bytes 18874368 | tf_op jit(solution)/shard_map/dot_general | solution.py:81
  215.2 10.8 %fusion.28 = bf16[384,1024]{1,0:T(8,128)(2,1)} fusion(f32[384,2,1024]{2,0,1:T(8,128)S(1)} %bitcast.67, f32[384,1024]{1,0:T(8,128)S(1)} %fusion.10, bf16[2,6144,1024]{2,1,0:T(8,128)(2,1)} %param.18, f32[384]{0:T(512)S(1)} %get-tuple-element.5, bf16[192,6144]{1,0:T(8,128)(2,1)S(1)} %copy-done.11, bf16[192,6144]{1,0:T(8,128)(2,1)S(1)} %copy-done.9), kind=kOutput, calls=%fused_computation.36 | convolution fusion | flops 4844814336 | bytes 21235200 | tf_op jit(solution)/shard_map/dot_general | solution.py:85
  226.1 41.9 %all-gather.11.cloned.1.call-done = bf16[384,4096]{1,0:T(8,128)(2,1)} async-done(((bf16[384,1024]{1,0:T(8,128)(2,1)}), bf16[384,4096]{1,0:T(8,128)(2,1)}) %all-gather.11.cloned.1.call-update) | async-done | bytes 3145744 | tf_op jit(solution)/shard_map/all_gather | solution.py:91
  268.0 10.0 %fusion = f32[384,1536]{1,0:T(8,128)} fusion(bf16[384,4096]{1,0:T(8,128)(2,1)} %all-gather.11.cloned.1.call-done, bf16[2,4096,1536]{2,1,0:T(8,128)(2,1)} %param.19), kind=kOutput, calls=%fused_computation.4 | convolution fusion | flops 4831838208 | bytes 18087936 | tf_op jit(solution)/shard_map/dot_general | solution.py:92
  278.0 53.6 %all-gather.9.cloned.1.call-done = bf16[384,4096]{1,0:T(8,128)(2,1)} async-done(((bf16[384,1024]{1,0:T(8,128)(2,1)}), bf16[384,4096]{1,0:T(8,128)(2,1)}) %all-gather.9.cloned.1.call-update) | async-done | bytes 3145744 | tf_op jit(solution)/shard_map/all_gather | solution.py:91
  331.6 10.5 %fusion.18 = f32[384,1536]{1,0:T(8,128)} fusion(f32[384,1536]{1,0:T(8,128)} %fusion, bf16[384,4096]{1,0:T(8,128)(2,1)} %all-gather.9.cloned.1.call-done, bf16[2,4096,1536]{2,1,0:T(8,128)(2,1)} %param.19), kind=kOutput, calls=%fused_computation.23 | convolution fusion | flops 4832428032 | bytes 20447232 | tf_op jit(solution)/shard_map/dot_general | solution.py:92
  342.1 31.9 %reduce-scatter.2.cloned.1.call-done = f32[96,1536]{1,0:T(8,128)} async-done(((f32[384,1536]{1,0:T(8,128)}), f32[96,1536]{1,0:T(8,128)}) %reduce-scatter.2.cloned.1.call-update) | async-done | bytes 589840 | tf_op jit(solution)/shard_map/reduce_scatter | solution.py:94
  374.0 1.8 convert_element_type.16
  (51 shorter events, 0.5 us)
Async XLA Ops:
  6.5 83.8 %copy-start = (bf16[8,2,64,1024]{3,2,1,0:T(8,128)(2,1)S(1)}, bf16[8,2,64,1024]{3,2,1,0:T(8,128)(2,1)}, u32[]{:S(2)}) copy-start(bf16[8,2,64,1024]{3,2,1,0:T(8,128)(2,1)} %param.21) | copy-start | bytes 6291460
  6.5 78.6 %copy-start.13 = (s32[3]{0:T(128)S(1)}, s32[3]{0:T(128)}, u32[]{:S(2)}) copy-start(s32[3]{0:T(128)} %param.14) | copy-start | bytes 40
  6.5 78.6 %copy-start.2 = (s32[8]{0:T(128)S(1)}, s32[8]{0:T(128)}, u32[]{:S(2)}) copy-start(s32[8]{0:T(128)} %param.15) | copy-start | bytes 100
  6.5 24.8 %all-gather.5.cloned.1.call-start = ((), (), s32[]{:S(2)}) async-start(), calls=%async_computation.1 | async-start | bytes 1966080 | tf_op jit(solution)/shard_map/all_gather | solution.py:36
  7.3 77.9 %all-gather.7.cloned.1.call-start = ((), (), s32[]{:S(2)}) async-start(), calls=%async_computation.2 | async-start | bytes 2949120 | tf_op jit(solution)/shard_map/all_gather | solution.py:41
  33.4 52.5 %copy-start.5 = (bf16[3,128,1536]{2,1,0:T(8,128)(2,1)}, bf16[3,128,1536]{2,1,0:T(8,128)(2,1)S(1)}, u32[]{:S(2)}) copy-start(bf16[3,128,1536]{2,1,0:T(8,128)(2,1)S(1)} %gather_fusion) | copy-start | bytes 3538948
  34.5 144.6 %all-reduce.2.cloned.1.call-start = ((), (), s32[]{:S(2)}) async-start(), calls=%async_computation.3 | async-start | bytes 393216 | tf_op jit(solution)/shard_map/psum | solution.py:73
  85.1 96.0 %collective-permute-start = (bf16[192,6144]{1,0:T(8,128)(2,1)}, bf16[192,6144]{1,0:T(8,128)(2,1)}, u32[]{:S(2)}, u32[]{:S(2)}) collective-permute-start(bf16[192,6144]{1,0:T(8,128)(2,1)} %all-gather.7.cloned.1.call-done), channel_id=1, source_target_pairs={{0,4},{4,0},{1,5},{5,1},{2,6},{6,2},{3,7},{7,3},{8,12},{12,8},{9,1... | collective-permute-start | bytes 7077896 | tf_op jit(solution)/shard_map/ppermute | solution.py:42
  87.6 1.3 copy-start.6
  87.8 2.5 copy-start.12
  90.2 177.7 %all-gather.11.cloned.1.call-start = ((), (), s32[]{:S(2)}) async-start(), calls=%async_computation.5 | async-start | bytes 3932160 | tf_op jit(solution)/shard_map/all_gather | solution.py:91
  180.7 2.3 copy-start.7
  181.1 13.5 %copy-start.3 = (f32[3,128,2,1024]{3,1,0,2:T(8,128)}, f32[3,128,2,1024]{3,1,0,2:T(8,128)S(1)}, u32[]{:S(2)}) copy-start(f32[3,128,2,1024]{3,1,0,2:T(8,128)S(1)} %copy.17) | copy-start | bytes 9437188
  181.1 3.9 %copy-start.14 = (bf16[6144,8]{0,1:T(8,128)(2,1)S(1)}, bf16[6144,8]{0,1:T(8,128)(2,1)}, u32[]{:S(2)}) copy-start(bf16[6144,8]{0,1:T(8,128)(2,1)} %param.16) | copy-start | bytes 294916
  185.0 9.6 %copy-start.8 = (bf16[192,6144]{1,0:T(8,128)(2,1)}, bf16[192,6144]{1,0:T(8,128)(2,1)S(1)}, u32[]{:S(2)}) copy-start(bf16[192,6144]{1,0:T(8,128)(2,1)S(1)} %get-tuple-element.15) | copy-start | bytes 7077892
  185.0 9.6 %copy-start.10 = (bf16[192,6144]{1,0:T(8,128)(2,1)}, bf16[192,6144]{1,0:T(8,128)(2,1)S(1)}, u32[]{:S(2)}) copy-start(bf16[192,6144]{1,0:T(8,128)(2,1)S(1)} %get-tuple-element.16) | copy-start | bytes 7077892
  205.4 126.2 %all-gather.9.cloned.1.call-start = ((), (), s32[]{:S(2)}) async-start(), calls=%async_computation.4 | async-start | bytes 3932160 | tf_op jit(solution)/shard_map/all_gather | solution.py:91
  205.6 9.6 %copy-start.4 = (f32[3,128,2,1024]{3,1,0,2:T(8,128)S(1)}, f32[3,128,2,1024]{3,1,0,2:T(8,128)}, u32[]{:S(2)}) copy-start(f32[3,128,2,1024]{3,1,0,2:T(8,128)} %copy-done.3) | copy-start | bytes 9437188
  205.6 9.6 %copy-start.9 = (bf16[192,6144]{1,0:T(8,128)(2,1)S(1)}, bf16[192,6144]{1,0:T(8,128)(2,1)}, u32[]{:S(2)}) copy-start(bf16[192,6144]{1,0:T(8,128)(2,1)} %copy-done.8) | copy-start | bytes 7077892
  205.6 9.6 %copy-start.11 = (bf16[192,6144]{1,0:T(8,128)(2,1)S(1)}, bf16[192,6144]{1,0:T(8,128)(2,1)}, u32[]{:S(2)}) copy-start(bf16[192,6144]{1,0:T(8,128)(2,1)} %copy-done.10) | copy-start | bytes 7077892
  226.0 148.0 %reduce-scatter.2.cloned.1.call-start = ((), (), s32[]{:S(2)}) async-start(), calls=%async_computation.6 | async-start | bytes 2949120 | tf_op jit(solution)/shard_map/reduce_scatter | solution.py:94
  331.6 44.3 %copy-start.1 = (bf16[8,2,64,1024]{3,2,1,0:T(8,128)(2,1)S(1)}, bf16[8,2,64,1024]{3,2,1,0:T(8,128)(2,1)}, u32[]{:S(2)}) copy-start(bf16[8,2,64,1024]{3,2,1,0:T(8,128)(2,1)} %param.21) | copy-start | bytes 6291460
Sparse Core Ops, SparseCore 0:
  8.9 22.3 all-gather.4
  34.6 50.4 all-gather.6
  90.4 88.7 all-reduce.1
  205.5 62.4 all-gather.10
  269.4 62.1 all-gather.8
  342.2 31.7 reduce-scatter.1

commit v3 on v2

--- a/solution.py
+++ b/solution.py
@@ -33,16 +33,47 @@
     cores = lax.axis_size("wc")
     wide_index = lax.axis_index(WIDE)
 
-    slots_q = lax.all_gather(prompts, WIDE, axis=0, tiled=True)
-    rows_q = jnp.take(slots_q, span_slot_owner[:nchunk], axis=0).reshape(tokens, quarter)
+    tile_count = tile_tenant_index.shape[0]
+    tile_rows = tokens // tile_count
+    resident_slots = adapter_down_weight.shape[0]
+    rank = adapter_down_weight.shape[3]
+    held = jnp.transpose(adapter_down_weight, (0, 1, 3, 2)).reshape(-1, quarter)
+    packed = jnp.concatenate([prompts.reshape(-1, quarter), held], axis=0)
+    gathered_q = lax.all_gather(packed, WIDE, axis=0, tiled=False)
+    wide_size = gathered_q.shape[0]
+    slot_rows = prompts.shape[0] * span
+    slots_q = gathered_q[:, :slot_rows]
+    adapters_q = gathered_q[:, slot_rows:].reshape(wide_size * resident_slots, window, rank, quarter)
+    slot_of_span = span_slot_owner[:nchunk]
+    rows_q = jnp.take(slots_q.reshape(-1, span, quarter), slot_of_span, axis=0).reshape(tokens, quarter)
+
+    tile_slot_index = jnp.take(tenant_adapter_slot, tile_tenant_index)
+    tile_adapters = jnp.take(adapters_q, tile_slot_index, axis=0)
+    partial_rank = jnp.einsum(
+        "ntd,nerd->nter",
+        rows_q.reshape(tile_count, tile_rows, quarter),
+        tile_adapters,
+        preferred_element_type=jnp.float32,
+    ).reshape(tokens, window * rank)
+    rank_hi = partial_rank.astype(jnp.bfloat16)
+    rank_lo = (partial_rank - rank_hi.astype(jnp.float32)).astype(jnp.bfloat16)
 
     half = tokens // cores
-    mine_q = lax.dynamic_slice_in_dim(rows_q, core * half, half, 0)
-    mine = lax.all_gather(mine_q, "expert", axis=1, tiled=True)
+    mine_q = jnp.concatenate([rows_q, rank_hi, rank_lo], axis=1)
+    mine_q = lax.dynamic_slice_in_dim(mine_q, core * half, half, 0)
+    expert_size = lax.axis_size("expert")
+    arrived = lax.all_gather(mine_q, "expert", axis=1, tiled=False)
+    mine = arrived[:, :, :quarter].reshape(half, expert_size * quarter)
+    pieces = arrived[:, :, quarter:].astype(jnp.float32)
+    summed = jnp.sum(pieces[:, :, : window * rank] + pieces[:, :, window * rank :], axis=1)
+    mine_rank = summed.astype(jnp.bfloat16)
+    mine = jnp.concatenate([mine, mine_rank], axis=1)
     other = lax.ppermute(mine, "wc", [(i, (i + 1) % cores) for i in range(cores)])
     first = jnp.where(core == 0, mine, other)
     second = jnp.where(core == 0, other, mine)
-    input_rows = jnp.concatenate([first, second], axis=0)
+    both = jnp.concatenate([first, second], axis=0)
+    input_rows = both[:, : expert_size * quarter]
+    lowrank = both[:, expert_size * quarter :].reshape(tile_count, tile_rows, window, rank)
 
     logits = jnp.dot(input_rows, router, preferred_element_type=jnp.float32)
     experts = jnp.arange(router.shape[1], dtype=jnp.int32)
@@ -54,26 +85,9 @@
         first_prob[:, None] * picked[:, 0, :window] + second_prob[:, None] * picked[:, 1, :window]
     )
 
-    tile_count = tile_tenant_index.shape[0]
-    tile_rows = tokens // tile_count
-    resident_slots = adapter_down_weight.shape[0]
-    tile_slot_index = jnp.take(tenant_adapter_slot, tile_tenant_index)
-    owners = tile_slot_index // resident_slots
-    local_index = tile_slot_index % resident_slots
-    held = jnp.take(adapter_down_weight, local_index, axis=0)
-    partial_rank = jnp.einsum(
-        "ntd,nedr->nter",
-        rows_q.reshape(tile_count, tile_rows, quarter),
-        held,
-        preferred_element_type=jnp.float32,
-    )
-    partial_rank = jnp.where(
-        (owners == wide_index)[:, None, None, None], partial_rank, jnp.zeros_like(partial_rank)
-    )
-    lowrank = lax.reduce_precision(lax.psum(partial_rank, GROUP), exponent_bits=8, mantissa_bits=7)
     tile_up = jnp.take(adapter_up_weight, tile_tenant_index, axis=0)
     adapted_hidden = jnp.einsum(
-        "nter,nerf->ntef", lowrank, tile_up.astype(jnp.float32), preferred_element_type=jnp.float32
+        "nter,nerf->ntef", lowrank, tile_up, preferred_element_type=jnp.float32
     ).reshape(tokens, window, tile_up.shape[3])
 
     running = None

time: 383 us -> 346 us (0.903)
  waiting for transfers between devices: 290 us -> 228 us
  local copies, waits for them, and re-layouts: 8.6 us -> 28.4 us
  other arithmetic: 6.66 us -> 12.3 us
    psum x1 -> x0, waiting for transfers between devices: 88.2 us -> none  [per_device(): lax.psum(partial_rank, GROUP)]
    all_gather x2, waiting for transfers between devices: 73.7 us -> 96.5 us  [the longest x1 57.1 us: per_device(): arrived = lax.all_gather(mine_q, 'expert', axis=1, tiled=False)]
    slice x0 -> x4, local copies, waits for them, and re-layouts: none -> 7.09 us  [the longest x1 3.72 us: per_device(): gathered_q[:, slot_rows:]]
    all_gather x0 -> x1, local copies, waits for them, and re-layouts: none -> 6.23 us  [per_device(): arrived = lax.all_gather(mine_q, 'expert', axis=1, tiled=False)]
    concatenate x0 -> x5, other arithmetic: none -> 5.89 us  [the longest x1 2.5 us: per_device(): packed = jnp.concatenate([prompts.reshape(-1, quarter), held], axis=0)]
    ppermute x1, waiting for transfers between devices: 0.01 us -> 4.31 us  [per_device(): lax.ppermute(mine, 'wc', [(i, (i + 1) % cores) for i in range(cores)])]
  transfers between devices with their start and end apart: 7 -> 6, of which waited for: 6 -> 6; matrix products, arithmetic and copies ran while one was open for 10% -> 9% of each run, Pallas kernels for 0% -> 0%
where the time goes in v3:
time: 346 us; the launch traced here: 345 us
  waiting for transfers between devices  228 us (66%)
  matrix products  62.5 us (18%)
  local copies, waits for them, and re-layouts  28.4 us (8%)
  between operations  13.4 us (4%)
  other arithmetic  12.3 us (4%)
    all_gather x2, waiting for transfers between devices, per_device(): gathered = lax.all_gather(hidden, 'expert', axis=1, tiled=True)  95.6 us
    all_gather x1, waiting for transfers between devices, per_device(): arrived = lax.all_gather(mine_q, 'expert', axis=1, tiled=False)  57.1 us
    all_gather x1, waiting for transfers between devices, per_device(): gathered_q = lax.all_gather(packed, WIDE, axis=0, tiled=False)  39.5 us
    reduce_scatter x1, waiting for transfers between devices, per_device(): lax.psum_scatter(running, WIDE, scatter_dimension=0, tiled=True)  31.9 us
    dot_general x2, matrix products, per_device(): jnp.dot(gathered, down_weight[expert_number], preferred_element_type=jnp....  20.6 us
    dot_general x2, matrix products, per_device(): jnp.dot(input_rows, up_weight[expert_number], preferred_element_type=jnp....  19.4 us
    dot_general x2, matrix products, per_device(): jnp.dot(input_rows, gate_weight[expert_number], preferred_element_type=jn...  18.7 us
  transfers between devices with their start and end apart: 6, of which 6 were waited for; matrix products, arithmetic and copies ran while one was open for 9% of the time, Pallas kernels for 0%

profile of v3, /device:TPU:0, one launch (start us, length us, event | category | flops | bytes accessed | tf_op | source)
XLA Modules:
  0.0 345.5 jit_solution(16391323644661182297)
XLA Ops:
  6.6 2.5 pad_maximum_fusion.1
  9.2 0.6 gather_fusion.1
  10.0 39.5 %all-gather.11.cloned.1.call-done = bf16[1536,1536]{1,0:T(8,128)(2,1)} async-done(((bf16[384,1536]{1,0:T(8,128)(2,1)}), bf16[1536,1536]{1,0:T(8,128)(2,1)}) %all-gather.11.cloned.1.call-update) | async-done | bytes 4718608 | tf_op jit(solution)/shard_map/all_gather | solution.py:42
  49.4 2.8 slice.102
  52.2 3.7 %slice.103 = bf16[4,256,1536]{2,1,0:T(8,128)(2,1)} slice(bf16[4,384,1536]{2,1,0:T(8,128)(2,1)} %bitcast.97), slice={[0:4], [128:384], [0:1536]} | slice | bytes 6291456 | tf_op jit(solution)/shard_map/slice | solution.py:46
  55.9 2.0 gather_fusion
  58.0 3.6 %gather_fusion.2 = bf16[3,2,64,1536]{3,2,1,0:T(8,128)(2,1)} fusion(bf16[8,2,64,1536]{3,2,1,0:T(8,128)(2,1)} %bitcast.95, s32[1024]{0:T(1024)S(1)} %pad_clamp_fusion), kind=kCustom, calls=%fused_computation.2 | custom fusion | bytes 2359308 | tf_op jit(solution)/shard_map/jit(_take)/gather | solution.py:51
  61.6 1.9 fusion.34
  63.6 0.7 fusion.48
  64.4 1.0 copy.24
  65.7 0.9 fusion.43
  66.6 57.1 %all-gather.13.cloned.1.call-done = bf16[192,7168]{1,0:T(8,128)(2,1)} async-done(((bf16[192,1792]{1,0:T(8,128)(2,1)}), bf16[192,7168]{1,0:T(8,128)(2,1)}) %all-gather.13.cloned.1.call-update) | async-done | bytes 2752528 | tf_op jit(solution)/shard_map/all_gather | solution.py:65
  123.7 6.2 %reshape.90 = bf16[192,4,1792]{2,1,0:T(4,128)(2,1)} reshape(bf16[192,7168]{1,0:T(8,128)(2,1)} %all-gather.13.cloned.1.call-done) | data formatting | bytes 5505024 | tf_op jit(solution)/shard_map/all_gather | solution.py:65
  129.9 1.8 copy-done.6
  133.3 1.8 pad_maximum_fusion
  135.7 4.3 %collective-permute-done = bf16[192,6272]{1,0:T(8,128)(2,1)} collective-permute-done((bf16[192,6272]{1,0:T(8,128)(2,1)}, bf16[192,6272]{1,0:T(8,128)(2,1)}, u32[]{:S(2)}, u32[]{:S(2)}) %collective-permute-start) | collective-permute-done | bytes 2408480 | tf_op jit(solution)/shard_map/ppermute | solution.py:71
  140.0 3.2 broadcast_select_fusion.1
  143.2 0.6 fusion.18
  143.9 2.1 copy-done.4
  146.0 1.3 fusion.56
  147.6 0.6 convolution_bitcast_fusion
  148.4 2.1 copy-done.5
  150.5 9.1 %fusion.4 = f32[384,1024]{1,0:T(8,128)S(1)} fusion(bf16[384,6144]{1,0:T(8,128)(2,1)S(1)} %copy-done.5, bf16[2,6144,1024]{2,1,0:T(8,128)(2,1)} %param.17), kind=kOutput, calls=%fused_computation.8 | convolution fusion | flops 4831838208 | bytes 18874368 | tf_op jit(solution)/shard_map/dot_general | solution.py:95
  159.7 9.0 %fusion.25 = bf16[384,1024]{1,0:T(8,128)(2,1)} fusion(f32[384,2,1024]{2,0,1:T(8,128)S(1)} %bitcast.98, f32[384,1024]{1,0:T(8,128)S(1)} %fusion.4, bf16[384,6144]{1,0:T(8,128)(2,1)S(1)} %copy-done.5, bf16[2,6144,1024]{2,1,0:T(8,128)(2,1)} %param.18, f32[384]{0:T(512)S(1)} %get-tuple-element.6), kind=kOutput, calls=%fused_computation.34 | convolution fusion | flops 4835377152 | bytes 21235200 | tf_op jit(solution)/shard_map/dot_general | solution.py:99
  168.9 9.5 %fusion.10 = f32[384,1024]{1,0:T(8,128)S(1)} fusion(bf16[384,6144]{1,0:T(8,128)(2,1)} %copy-done.4, bf16[2,6144,1024]{2,1,0:T(8,128)(2,1)} %param.17), kind=kOutput, calls=%fused_computation.14 | convolution fusion | flops 4831838208 | bytes 18874368 | tf_op jit(solution)/shard_map/dot_general | solution.py:95
  178.4 10.4 %fusion.29 = bf16[384,1024]{1,0:T(8,128)(2,1)} fusion(f32[384,2,1024]{2,0,1:T(8,128)S(1)} %bitcast.99, f32[384,1024]{1,0:T(8,128)S(1)} %fusion.10, bf16[384,6144]{1,0:T(8,128)(2,1)} %copy-done.4, bf16[2,6144,1024]{2,1,0:T(8,128)(2,1)} %param.18, f32[384]{0:T(512)S(1)} %get-tuple-element.5), kind=kOutput, calls=%fused_computation.39 | convolution fusion | flops 4835377152 | bytes 21235200 | tf_op jit(solution)/shard_map/dot_general | solution.py:99
  189.0 42.1 %all-gather.9.cloned.1.call-done = bf16[384,4096]{1,0:T(8,128)(2,1)} async-done(((bf16[384,1024]{1,0:T(8,128)(2,1)}), bf16[384,4096]{1,0:T(8,128)(2,1)}) %all-gather.9.cloned.1.call-update) | async-done | bytes 3145744 | tf_op jit(solution)/shard_map/all_gather | solution.py:105
  231.0 10.1 %fusion = f32[384,1536]{1,0:T(8,128)} fusion(bf16[384,4096]{1,0:T(8,128)(2,1)} %all-gather.9.cloned.1.call-done, bf16[2,4096,1536]{2,1,0:T(8,128)(2,1)} %param.19), kind=kOutput, calls=%fused_computation.4 | convolution fusion | flops 4831838208 | bytes 18087936 | tf_op jit(solution)/shard_map/dot_general | solution.py:106
  241.1 53.6 %all-gather.7.cloned.1.call-done = bf16[384,4096]{1,0:T(8,128)(2,1)} async-done(((bf16[384,1024]{1,0:T(8,128)(2,1)}), bf16[384,4096]{1,0:T(8,128)(2,1)}) %all-gather.7.cloned.1.call-update) | async-done | bytes 3145744 | tf_op jit(solution)/shard_map/all_gather | solution.py:105
  294.7 10.5 %fusion.19 = f32[384,1536]{1,0:T(8,128)} fusion(f32[384,1536]{1,0:T(8,128)} %fusion, bf16[384,4096]{1,0:T(8,128)(2,1)} %all-gather.7.cloned.1.call-done, bf16[2,4096,1536]{2,1,0:T(8,128)(2,1)} %param.19), kind=kOutput, calls=%fused_computation.25 | convolution fusion | flops 4832428032 | bytes 20447232 | tf_op jit(solution)/shard_map/dot_general | solution.py:106
  305.2 31.9 %reduce-scatter.2.cloned.1.call-done = f32[96,1536]{1,0:T(8,128)} async-done(((f32[384,1536]{1,0:T(8,128)}), f32[96,1536]{1,0:T(8,128)}) %reduce-scatter.2.cloned.1.call-update) | async-done | bytes 589840 | tf_op jit(solution)/shard_map/reduce_scatter | solution.py:108
  337.2 1.8 convert_element_type.35
  (58 shorter events, 3.7 us)
Async XLA Ops:
  6.5 128.6 %copy-start = (bf16[8,2,64,1024]{3,2,1,0:T(8,128)(2,1)S(1)}, bf16[8,2,64,1024]{3,2,1,0:T(8,128)(2,1)}, u32[]{:S(2)}) copy-start(bf16[8,2,64,1024]{3,2,1,0:T(8,128)(2,1)} %param.21) | copy-start | bytes 6291460
  6.5 2.6 copy-start.11
  6.5 2.7 copy-start.2
  6.5 3.3 copy-start.12
  6.5 42.9 %all-gather.11.cloned.1.call-start = ((), (), s32[]{:S(2)}) async-start(), calls=%async_computation.4 | async-start | bytes 5898240 | tf_op jit(solution)/shard_map/all_gather | solution.py:42
  9.1 114.6 %all-gather.13.cloned.1.call-start = ((), (), s32[]{:S(2)}) async-start(), calls=%async_computation.5 | async-start | bytes 3440640 | tf_op jit(solution)/shard_map/all_gather | solution.py:65
  66.6 164.5 %all-gather.9.cloned.1.call-start = ((), (), s32[]{:S(2)}) async-start(), calls=%async_computation.2 | async-start | bytes 3932160 | tf_op jit(solution)/shard_map/all_gather | solution.py:105
  129.9 1.8 copy-start.6
  129.9 2.5 slice-start
  133.0 2.1 copy-start.3
  133.2 2.5 copy-start.10
  135.1 4.9 %collective-permute-start = (bf16[192,6272]{1,0:T(8,128)(2,1)}, bf16[192,6272]{1,0:T(8,128)(2,1)}, u32[]{:S(2)}, u32[]{:S(2)}) collective-permute-start(bf16[192,6272]{1,0:T(8,128)(2,1)} %pad_maximum_fusion), channel_id=1, source_target_pairs={{0,4},{4,0},{1,5},{5,1},{2,6},{6,2},{3,7},{7,3},{8,12},{12,8},{9,1... | collective-permute-start | bytes 7225352 | tf_op jit(solution)/shard_map/ppermute | solution.py:71
  143.9 2.1 copy-start.4
  143.9 2.1 copy-start.9
  148.2 2.3 copy-start.5
  150.5 9.1 %copy-start.7 = (f32[3,128,2,1024]{3,1,0,2:T(8,128)}, f32[3,128,2,1024]{3,1,0,2:T(8,128)S(1)}, u32[]{:S(2)}) copy-start(f32[3,128,2,1024]{3,1,0,2:T(8,128)S(1)} %copy.27) | copy-start | bytes 9437188
  168.7 126.0 %all-gather.7.cloned.1.call-start = ((), (), s32[]{:S(2)}) async-start(), calls=%async_computation.1 | async-start | bytes 3932160 | tf_op jit(solution)/shard_map/all_gather | solution.py:105
  168.9 9.5 %copy-start.8 = (f32[3,128,2,1024]{3,1,0,2:T(8,128)S(1)}, f32[3,128,2,1024]{3,1,0,2:T(8,128)}, u32[]{:S(2)}) copy-start(f32[3,128,2,1024]{3,1,0,2:T(8,128)} %copy-done.7) | copy-start | bytes 9437188
  188.9 148.2 %reduce-scatter.2.cloned.1.call-start = ((), (), s32[]{:S(2)}) async-start(), calls=%async_computation.3 | async-start | bytes 2949120 | tf_op jit(solution)/shard_map/reduce_scatter | solution.py:108
  294.7 44.3 %copy-start.1 = (bf16[8,2,64,1024]{3,2,1,0:T(8,128)(2,1)S(1)}, bf16[8,2,64,1024]{3,2,1,0:T(8,128)(2,1)}, u32[]{:S(2)}) copy-start(bf16[8,2,64,1024]{3,2,1,0:T(8,128)(2,1)} %param.21) | copy-start | bytes 6291460
Sparse Core Ops, SparseCore 0:
  9.2 40.1 all-gather.10
  66.7 56.9 all-gather.12
  168.8 62.2 all-gather.8
  232.5 62.1 all-gather.6
  305.3 31.7 reduce-scatter.1

commit v4 on v3

--- a/solution.py
+++ b/solution.py
@@ -55,8 +55,9 @@
         tile_adapters,
         preferred_element_type=jnp.float32,
     ).reshape(tokens, window * rank)
-    rank_hi = partial_rank.astype(jnp.bfloat16)
-    rank_lo = (partial_rank - rank_hi.astype(jnp.float32)).astype(jnp.bfloat16)
+    rank_top = lax.reduce_precision(partial_rank, exponent_bits=8, mantissa_bits=7)
+    rank_hi = rank_top.astype(jnp.bfloat16)
+    rank_lo = (partial_rank - rank_top).astype(jnp.bfloat16)
 
     half = tokens // cores
     mine_q = jnp.concatenate([rows_q, rank_hi, rank_lo], axis=1)
@@ -90,23 +91,51 @@
         "nter,nerf->ntef", lowrank, tile_up, preferred_element_type=jnp.float32
     ).reshape(tokens, window, tile_up.shape[3])
 
-    running = None
+    pieces_per_expert = 2
+    units = gate_weight.shape[2]
+    piece = units // pieces_per_expert
+    expert_size = lax.axis_size("expert")
+    reduced = None
     for expert_number in range(window):
-        gate_pre = jnp.dot(
-            input_rows, gate_weight[expert_number], preferred_element_type=jnp.float32
-        )
-        up_value = (
-            jnp.dot(input_rows, up_weight[expert_number], preferred_element_type=jnp.float32)
-            + ADAPTER_SCALE * adapted_hidden[:, expert_number]
-        )
-        hidden = (
-            weight[:, expert_number, None] * jax.nn.silu(gate_pre) * up_value
-        ).astype(jnp.bfloat16)
-        gathered = lax.all_gather(hidden, "expert", axis=1, tiled=True)
-        part = jnp.dot(gathered, down_weight[expert_number], preferred_element_type=jnp.float32)
-        running = part if running is None else running + part
-    mixed_rows = lax.psum_scatter(running, WIDE, scatter_dimension=0, tiled=True)
-    return mixed_rows.astype(jnp.bfloat16)
+        running = None
+        for piece_number in range(pieces_per_expert):
+            cols = slice(piece_number * piece, (piece_number + 1) * piece)
+            gate_pre = jnp.dot(
+                input_rows, gate_weight[expert_number, :, cols], preferred_element_type=jnp.float32
+            )
+            up_value = (
+                jnp.dot(
+                    input_rows, up_weight[expert_number, :, cols], preferred_element_type=jnp.float32
+                )
+                + ADAPTER_SCALE * adapted_hidden[:, expert_number, cols]
+            )
+            hidden = (
+                weight[:, expert_number, None] * jax.nn.silu(gate_pre) * up_value
+            ).astype(jnp.bfloat16)
+            gathered = lax.all_gather(hidden, "expert", axis=1, tiled=False)
+            down_rows = down_weight[expert_number].reshape(expert_size, units, -1)[:, cols]
+            part = jnp.einsum(
+                "tef,efd->td", gathered, down_rows, preferred_element_type=jnp.float32
+            )
+            running = part if running is None else running + part
+        rows_sum = reduce_rows(running, core, cores)
+        reduced = rows_sum if reduced is None else reduced + rows_sum
+    return reduced.astype(jnp.bfloat16)
+
+
+def reduce_rows(running, core, cores):
+    chips = lax.axis_size("wy")
+    block = running.shape[0] // (chips * cores)
+    by_chip = running.reshape(chips, cores, block, running.shape[1])
+    keep = jnp.where(core == 0, by_chip[:, 0], by_chip[:, 1])
+    send = jnp.where(core == 0, by_chip[:, 1], by_chip[:, 0])
+    chip_sum = keep + lax.ppermute(send, "wc", [(i, (i + 1) % cores) for i in range(cores)])
+    if chips == 2:
+        chip = lax.axis_index("wy")
+        mine = jnp.where(chip == 0, chip_sum[0], chip_sum[1])
+        away = jnp.where(chip == 0, chip_sum[1], chip_sum[0])
+        return mine + lax.ppermute(away, "wy", [(0, 1), (1, 0)])
+    return lax.psum_scatter(chip_sum, "wy", scatter_dimension=0, tiled=True).reshape(block, -1)
 
 
 def solution(mesh):

time: 346 us -> 363 us (1.049)
  waiting for transfers between devices: 228 us -> 191 us
  matrix products: 62.5 us -> 86.7 us
  local copies, waits for them, and re-layouts: 28.4 us -> 49 us
  other arithmetic: 12.3 us -> 18.4 us
    reduce_scatter x1 -> x0, waiting for transfers between devices: 31.9 us -> none  [per_device(): lax.psum_scatter(running, WIDE, scatter_dimension=0, tiled=True)]
    all_gather x2 -> x4, waiting for transfers between devices: 95.6 us -> 64.6 us  [per_device(): gathered = lax.all_gather(hidden, 'expert', axis=1, tiled=False)]
    ppermute x0 -> x4, waiting for transfers between devices: none -> 25.6 us  [the longest x2 25.6 us: reduce_rows(): return mine + lax.ppermute(away, 'wy', [(0, 1), (1, 0)])]
    dot_general x6 -> x12, matrix products: 58.7 us -> 82.6 us  [the longest x4 30 us: per_device(): jnp.dot(input_rows, up_weight[expert_number, :, cols], preferred_element_...]
    slice x0 -> x1, local copies, waits for them, and re-layouts: none -> 17.2 us  [per_device(): down_weight[expert_number].reshape(expert_size, units, -1)[:, cols]]
    unnamed x28 -> x29, local copies, waits for them, and re-layouts: 6.55 us -> 8.05 us
  transfers between devices with their start and end apart: 6 -> 11, of which waited for: 6 -> 8; matrix products, arithmetic and copies ran while one was open for 9% -> 26% of each run, Pallas kernels for 0% -> 0%
where the time goes in v4:
time: 363 us; the launch traced here: 362 us
  waiting for transfers between devices  191 us (53%)
  matrix products  86.7 us (24%)
  local copies, waits for them, and re-layouts  49 us (13%)
  other arithmetic  18.4 us (5%)
  between operations  13.8 us (4%)
    all_gather x4, waiting for transfers between devices, per_device(): gathered = lax.all_gather(hidden, 'expert', axis=1, tiled=False)  64.6 us
    all_gather x1, waiting for transfers between devices, per_device(): arrived = lax.all_gather(mine_q, 'expert', axis=1, tiled=False)  57.1 us
    all_gather x1, waiting for transfers between devices, per_device(): gathered_q = lax.all_gather(packed, WIDE, axis=0, tiled=False)  39.5 us
    dot_general x4, matrix products, per_device(): jnp.dot(input_rows, up_weight[expert_number, :, cols], preferred_element_...  30 us
    dot_general x4, matrix products, per_device(): jnp.einsum('tef,efd->td', gathered, down_rows, preferred_element_type=jnp...  27.8 us
    ppermute x2, waiting for transfers between devices, reduce_rows(): return mine + lax.ppermute(away, 'wy', [(0, 1), (1, 0)])  25.6 us
    dot_general x4, matrix products, per_device(): jnp.dot(input_rows, gate_weight[expert_number, :, cols], preferred_elemen...  24.8 us
    slice x1, local copies, waits for them, and re-layouts, per_device(): down_weight[expert_number].reshape(expert_size, units, -1)[:, cols]  17.2 us
  transfers between devices with their start and end apart: 11, of which 8 were waited for; matrix products, arithmetic and copies ran while one was open for 26% of the time, Pallas kernels for 0%

profile of v4, /device:TPU:0, one launch (start us, length us, event | category | flops | bytes accessed | tf_op | source)
XLA Modules:
  0.0 362.0 jit_solution(9896356941073778303)
XLA Ops:
  6.6 2.5 pad_maximum_fusion.1
  10.0 39.5 %all-gather.13.cloned.1.call-done = bf16[1536,1536]{1,0:T(8,128)(2,1)} async-done(((bf16[384,1536]{1,0:T(8,128)(2,1)}), bf16[1536,1536]{1,0:T(8,128)(2,1)}) %all-gather.13.cloned.1.call-update) | async-done | bytes 4718608 | tf_op jit(solution)/shard_map/all_gather | solution.py:42
  49.4 2.8 slice.186
  52.2 3.7 %slice.187 = bf16[4,256,1536]{2,1,0:T(8,128)(2,1)} slice(bf16[4,384,1536]{2,1,0:T(8,128)(2,1)} %bitcast.204), slice={[0:4], [128:384], [0:1536]} | slice | bytes 6291456 | tf_op jit(solution)/shard_map/slice | solution.py:46
  55.9 3.1 gather_fusion
  59.1 3.6 gather_fusion.2
  64.1 2.2 fusion.71
  69.3 57.1 %all-gather.15.cloned.1.call-done = bf16[192,7168]{1,0:T(8,128)(2,1)} async-done(((bf16[192,1792]{1,0:T(8,128)(2,1)}), bf16[192,7168]{1,0:T(8,128)(2,1)}) %all-gather.15.cloned.1.call-update) | async-done | bytes 2752528 | tf_op jit(solution)/shard_map/all_gather | solution.py:66
  126.3 6.2 %reshape.118 = bf16[192,4,1792]{2,1,0:T(4,128)(2,1)} reshape(bf16[192,7168]{1,0:T(8,128)(2,1)} %all-gather.15.cloned.1.call-done) | data formatting | bytes 5505024 | tf_op jit(solution)/shard_map/all_gather | solution.py:66
  135.9 1.8 pad_maximum_fusion
  138.7 4.3 %collective-permute-done = bf16[192,6272]{1,0:T(8,128)(2,1)} collective-permute-done((bf16[192,6272]{1,0:T(8,128)(2,1)}, bf16[192,6272]{1,0:T(8,128)(2,1)}, u32[]{:S(2)}, u32[]{:S(2)}) %collective-permute-start) | collective-permute-done | bytes 2408480 | tf_op jit(solution)/shard_map/ppermute | solution.py:72
  143.0 3.2 broadcast_select_fusion
  149.5 6.2 %fusion.14 = f32[384,512]{1,0:T(8,128)S(1)} fusion(bf16[384,6144]{1,0:T(8,128)(2,1)} %copy-done.4, bf16[2,6144,1024]{2,1,0:T(8,128)(2,1)} %param.17), kind=kOutput, calls=%fused_computation.18 | convolution fusion | flops 2415919104 | bytes 11796480 | tf_op jit(solution)/shard_map/dot_general | solution.py:103
  156.6 1.6 copy-done.9
  159.8 6.4 %multiply_convert_fusion.1 = bf16[384,512]{1,0:T(8,128)(2,1)} fusion(f32[384,512]{1,0:T(8,128)S(1)} %fusion.14, f32[384]{0:T(512)S(1)} %get-tuple-element.6, f32[384,2,1024]{2,0,1:T(8,128)S(1)} %bitcast.205, bf16[384,6144]{1,0:T(8,128)(2,1)S(1)} %copy-done.5, bf16[2,6144,1024]{2,1,0:T(8,128)(2,1)} %param.18), kind=kOutput, calls=%fused_computation.89 | convolution fusion | flops 2417688576 | bytes 12977664 | tf_op jit(solution)/shard_map/dot_general | solution.py:107
  166.5 6.2 %fusion.10 = f32[384,512]{1,0:T(8,128)S(1)} fusion(bf16[384,6144]{1,0:T(8,128)(2,1)} %copy-done.4, bf16[2,6144,1024]{2,1,0:T(8,128)(2,1)} %param.17), kind=kOutput, calls=%fused_computation.14 | convolution fusion | flops 2415919104 | bytes 11796480 | tf_op jit(solution)/shard_map/dot_general | solution.py:103
  172.7 7.9 %multiply_convert_fusion = bf16[384,512]{1,0:T(8,128)(2,1)} fusion(f32[384,512]{1,0:T(8,128)S(1)} %fusion.10, f32[384]{0:T(512)S(1)} %get-tuple-element.6, f32[384,2,1024]{2,0,1:T(8,128)} %bitcast.206, bf16[384,6144]{1,0:T(8,128)(2,1)} %copy-done.4, bf16[2,6144,1024]{2,1,0:T(8,128)(2,1)} %param.18), kind=kOutput, calls=%fused_computation.88 | convolution fusion | flops 2417688576 | bytes 12977664 | tf_op jit(solution)/shard_map/dot_general | solution.py:107
  180.6 6.2 %fusion.22 = f32[384,512]{1,0:T(8,128)S(1)} fusion(bf16[384,6144]{1,0:T(8,128)(2,1)} %copy-done.4, bf16[2,6144,1024]{2,1,0:T(8,128)(2,1)} %param.17), kind=kOutput, calls=%fused_computation.26 | convolution fusion | flops 2415919104 | bytes 11796480 | tf_op jit(solution)/shard_map/dot_general | solution.py:103
  186.9 7.8 %multiply_convert_fusion.3 = bf16[384,512]{1,0:T(8,128)(2,1)} fusion(f32[384,512]{1,0:T(8,128)S(1)} %fusion.22, f32[384,2,1024]{2,0,1:T(8,128)} %bitcast.207, bf16[384,6144]{1,0:T(8,128)(2,1)} %copy-done.4, bf16[2,6144,1024]{2,1,0:T(8,128)(2,1)} %param.18, f32[384]{0:T(512)S(1)} %get-tuple-element.5), kind=kOutput, calls=%fused_computation.91 | convolution fusion | flops 2417688576 | bytes 12977664 | tf_op jit(solution)/shard_map/dot_general | solution.py:107
  194.8 17.2 %fusion.107 = (bf16[1,4096,1536]{2,1,0:T(8,128)(2,1)}, bf16[1,4096,1536]{2,1,0:T(8,128)(2,1)}) fusion(bf16[2,4096,1536]{2,1,0:T(8,128)(2,1)} %param.19), kind=kLoop, calls=%fused_computation.137 | loop fusion | bytes 50331648 | tf_op jit(solution)/shard_map/slice | solution.py:116
  212.0 6.2 %fusion.18 = f32[384,512]{1,0:T(8,128)S(1)} fusion(bf16[384,6144]{1,0:T(8,128)(2,1)} %copy-done.4, bf16[2,6144,1024]{2,1,0:T(8,128)(2,1)} %param.17), kind=kOutput, calls=%fused_computation.22 | convolution fusion | flops 2415919104 | bytes 11796480 | tf_op jit(solution)/shard_map/dot_general | solution.py:103
  218.2 7.9 %multiply_convert_fusion.2 = bf16[384,512]{1,0:T(8,128)(2,1)} fusion(f32[384,512]{1,0:T(8,128)S(1)} %fusion.18, f32[384,2,1024]{2,0,1:T(8,128)} %bitcast.208, bf16[384,6144]{1,0:T(8,128)(2,1)} %copy-done.4, bf16[2,6144,1024]{2,1,0:T(8,128)(2,1)} %param.18, f32[384]{0:T(512)S(1)} %get-tuple-element.5), kind=kOutput, calls=%fused_computation.90 | convolution fusion | flops 2417688576 | bytes 12977664 | tf_op jit(solution)/shard_map/dot_general | solution.py:107
  226.1 7.4 %fusion.39 = f32[384,1536]{1,0:T(8,128)} fusion(bf16[4,1024,1536]{2,1,0:T(8,128)(2,1)} %bitcast.195, bf16[48,4,8,512]{3,2,1,0:T(8,128)(2,1)} %bitcast.212), kind=kOutput, calls=%fused_computation.41 | convolution fusion | flops 2415919104 | bytes 10223616 | tf_op jit(solution)/shard_map/tef,efd->td/dot_general | solution.py:117
  233.5 6.2 %all-gather.23.cloned.1.call-done = bf16[384,2048]{1,0:T(8,128)(2,1)} async-done(((bf16[384,512]{1,0:T(8,128)(2,1)}), bf16[384,2048]{1,0:T(8,128)(2,1)}) %all-gather.23.cloned.1.call-update) | async-done | bytes 1572880 | tf_op jit(solution)/shard_map/all_gather | solution.py:115
  239.7 6.6 %fusion.45 = f32[384,1536]{1,0:T(8,128)S(1)} fusion(f32[384,1536]{1,0:T(8,128)} %fusion.39, bf16[4,1024,1536]{2,1,0:T(8,128)(2,1)} %bitcast.196, bf16[48,4,8,512]{3,2,1,0:T(8,128)(2,1)} %bitcast.213), kind=kOutput, calls=%fused_computation.43 | convolution fusion | flops 2416508928 | bytes 12582912 | tf_op jit(solution)/shard_map/tef,efd->td/dot_general | solution.py:117
  248.9 28.2 %all-gather.17.cloned.1.call-done = bf16[384,2048]{1,0:T(8,128)(2,1)} async-done(((bf16[384,512]{1,0:T(8,128)(2,1)}), bf16[384,2048]{1,0:T(8,128)(2,1)}) %all-gather.17.cloned.1.call-update) | async-done | bytes 1572880 | tf_op jit(solution)/shard_map/all_gather | solution.py:115
  277.1 7.2 %fusion.33 = f32[384,1536]{1,0:T(8,128)} fusion(bf16[4,1024,1536]{2,1,0:T(8,128)(2,1)} %bitcast.193, bf16[48,4,8,512]{3,2,1,0:T(8,128)(2,1)} %bitcast.214), kind=kOutput, calls=%fused_computation.39 | convolution fusion | flops 2415919104 | bytes 10223616 | tf_op jit(solution)/shard_map/tef,efd->td/dot_general | solution.py:117
  284.4 30.2 %all-gather.19.cloned.1.call-done = bf16[384,2048]{1,0:T(8,128)(2,1)} async-done(((bf16[384,512]{1,0:T(8,128)(2,1)}), bf16[384,2048]{1,0:T(8,128)(2,1)}) %all-gather.19.cloned.1.call-update) | async-done | bytes 1572880 | tf_op jit(solution)/shard_map/all_gather | solution.py:115
  314.5 6.5 %fusion.48 = f32[384,1536]{1,0:T(8,128)S(1)} fusion(f32[384,1536]{1,0:T(8,128)} %fusion.33, bf16[4,1024,1536]{2,1,0:T(8,128)(2,1)} %bitcast.194, bf16[48,4,8,512]{3,2,1,0:T(8,128)(2,1)} %bitcast.215), kind=kOutput, calls=%fused_computation.44 | convolution fusion | flops 2416508928 | bytes 12582912 | tf_op jit(solution)/shard_map/tef,efd->td/dot_general | solution.py:117
  323.7 2.0 bitcast_add_fusion
  328.6 13.4 %collective-permute-done.4 = f32[96,1536]{1,0:T(8,128)S(1)} collective-permute-done((f32[96,1536]{1,0:T(8,128)S(1)}, f32[96,1536]{1,0:T(8,128)S(1)}, u32[]{:S(2)}, u32[]{:S(2)}) %collective-permute-start.4) | collective-permute-done | bytes 589856 | tf_op jit(solution)/shard_map/ppermute | solution.py:137
  342.0 12.2 %collective-permute-done.2 = f32[96,1536]{1,0:T(8,128)S(1)} collective-permute-done((f32[96,1536]{1,0:T(8,128)S(1)}, f32[96,1536]{1,0:T(8,128)S(1)}, u32[]{:S(2)}, u32[]{:S(2)}) %collective-permute-start.2) | collective-permute-done | bytes 589856 | tf_op jit(solution)/shard_map/ppermute | solution.py:137
  (83 shorter events, 24.6 us)
Async XLA Ops:
  6.5 131.5 %copy-start = (bf16[8,2,64,1024]{3,2,1,0:T(8,128)(2,1)S(1)}, bf16[8,2,64,1024]{3,2,1,0:T(8,128)(2,1)}, u32[]{:S(2)}) copy-start(bf16[8,2,64,1024]{3,2,1,0:T(8,128)(2,1)} %param.21) | copy-start | bytes 6291460
  6.5 2.6 copy-start.12
  6.5 2.6 copy-start.2
  6.5 3.3 copy-start.13
  6.5 42.9 %all-gather.13.cloned.1.call-start = ((), (), s32[]{:S(2)}) async-start(), calls=%async_computation | async-start | bytes 5898240 | tf_op jit(solution)/shard_map/all_gather | solution.py:42
  9.1 117.2 %all-gather.15.cloned.1.call-start = ((), (), s32[]{:S(2)}) async-start(), calls=%async_computation.1 | async-start | bytes 3440640 | tf_op jit(solution)/shard_map/all_gather | solution.py:66
  69.2 156.9 %all-gather.21.cloned.1.call-start = ((), (), s32[]{:S(2)}) async-start(), calls=%async_computation.4 | async-start | bytes 1966080 | tf_op jit(solution)/shard_map/all_gather | solution.py:115
  133.7 1.7 slice-start
  135.9 2.2 copy-start.3
  135.9 2.8 copy-start.11
  138.0 4.9 %collective-permute-start = (bf16[192,6272]{1,0:T(8,128)(2,1)}, bf16[192,6272]{1,0:T(8,128)(2,1)}, u32[]{:S(2)}, u32[]{:S(2)}) collective-permute-start(bf16[192,6272]{1,0:T(8,128)(2,1)} %pad_maximum_fusion), channel_id=1, source_target_pairs={{0,4},{4,0},{1,5},{5,1},{2,6},{6,2},{3,7},{7,3},{8,12},{12,8},{9,1... | collective-permute-start | bytes 7225352 | tf_op jit(solution)/shard_map/ppermute | solution.py:72
  146.2 0.9 copy-start.10
  147.1 2.2 copy-start.4
  156.3 3.5 copy-start.5
  156.6 1.6 copy-start.9
  166.3 73.4 %all-gather.23.cloned.1.call-start = ((), (), s32[]{:S(2)}) async-start(), calls=%async_computation.5 | async-start | bytes 1966080 | tf_op jit(solution)/shard_map/all_gather | solution.py:115
  180.6 96.5 %all-gather.17.cloned.1.call-start = ((), (), s32[]{:S(2)}) async-start(), calls=%async_computation.2 | async-start | bytes 1966080 | tf_op jit(solution)/shard_map/all_gather | solution.py:115
  194.7 119.8 %all-gather.19.cloned.1.call-start = ((), (), s32[]{:S(2)}) async-start(), calls=%async_computation.3 | async-start | bytes 1966080 | tf_op jit(solution)/shard_map/all_gather | solution.py:115
  246.3 1.4 copy-start.6
  248.9 74.7 %collective-permute-start.3 = (f32[2,96,1536]{2,1,0:T(8,128)}, f32[2,96,1536]{2,1,0:T(8,128)S(1)}, u32[]{:S(2)}, u32[]{:S(2)}) collective-permute-start(f32[2,96,1536]{2,1,0:T(8,128)} %select_bitcast_fusion), channel_id=1, source_target_pairs={{0,4},{4,0},{1,5},{5,1},{2,6},{6,2},{3,7},{7,3},{8,12},{12,8},{9,1... | collective-permute-start | bytes 3538952 | tf_op jit(solution)/shard_map/ppermute | solution.py:132
  321.1 1.4 copy-start.7
  323.7 3.7 %collective-permute-start.1 = (f32[2,96,1536]{2,1,0:T(8,128)}, f32[2,96,1536]{2,1,0:T(8,128)S(1)}, u32[]{:S(2)}, u32[]{:S(2)}) collective-permute-start(f32[2,96,1536]{2,1,0:T(8,128)} %select_bitcast_fusion.1), channel_id=1, source_target_pairs={{0,4},{4,0},{1,5},{5,1},{2,6},{6,2},{3,7},{7,3},{8,12},{12,8},{9,1... | collective-permute-start | bytes 3538952 | tf_op jit(solution)/shard_map/ppermute | solution.py:132
  323.7 3.7 %copy-start.8 = (f32[384,1536]{1,0:T(8,128)S(1)}, f32[384,1536]{1,0:T(8,128)}, u32[]{:S(2)}) copy-start(f32[384,1536]{1,0:T(8,128)} %copy-done.7) | copy-start | bytes 7077892
  325.8 16.2 %collective-permute-start.4 = (f32[96,1536]{1,0:T(8,128)S(1)}, f32[96,1536]{1,0:T(8,128)S(1)}, u32[]{:S(2)}, u32[]{:S(2)}) collective-permute-start(f32[96,1536]{1,0:T(8,128)S(1)} %select_bitcast_fusion.2), channel_id=1, source_target_pairs={{0,8},{8,0},{1,9},{9,1},{2,10},{10,2},{3,11},{11,3},{4,12},{12,4},... | collective-permute-start | bytes 1769480 | tf_op jit(solution)/shard_map/ppermute | solution.py:137
  327.3 27.8 %copy-start.1 = (bf16[8,2,64,1024]{3,2,1,0:T(8,128)(2,1)S(1)}, bf16[8,2,64,1024]{3,2,1,0:T(8,128)(2,1)}, u32[]{:S(2)}) copy-start(bf16[8,2,64,1024]{3,2,1,0:T(8,128)(2,1)} %param.21) | copy-start | bytes 6291460
  327.7 26.5 %collective-permute-start.2 = (f32[96,1536]{1,0:T(8,128)S(1)}, f32[96,1536]{1,0:T(8,128)S(1)}, u32[]{:S(2)}, u32[]{:S(2)}) collective-permute-start(f32[96,1536]{1,0:T(8,128)S(1)} %select_bitcast_fusion.3), channel_id=1, source_target_pairs={{0,8},{8,0},{1,9},{9,1},{2,10},{10,2},{3,11},{11,3},{4,12},{12,4},... | collective-permute-start | bytes 1769480 | tf_op jit(solution)/shard_map/ppermute | solution.py:137
Sparse Core Ops, SparseCore 0:
  9.2 40.1 all-gather.12
  69.3 56.9 all-gather.14
  166.4 35.8 all-gather.20
  203.7 35.9 all-gather.22
  241.1 35.9 all-gather.16
  278.6 35.9 all-gather.18

commit v5 on v3

--- a/solution.py
+++ b/solution.py
@@ -55,8 +55,9 @@
         tile_adapters,
         preferred_element_type=jnp.float32,
     ).reshape(tokens, window * rank)
-    rank_hi = partial_rank.astype(jnp.bfloat16)
-    rank_lo = (partial_rank - rank_hi.astype(jnp.float32)).astype(jnp.bfloat16)
+    rank_top = lax.reduce_precision(partial_rank, exponent_bits=8, mantissa_bits=7)
+    rank_hi = rank_top.astype(jnp.bfloat16)
+    rank_lo = (partial_rank - rank_top).astype(jnp.bfloat16)
 
     half = tokens // cores
     mine_q = jnp.concatenate([rows_q, rank_hi, rank_lo], axis=1)
@@ -105,8 +106,22 @@
         gathered = lax.all_gather(hidden, "expert", axis=1, tiled=True)
         part = jnp.dot(gathered, down_weight[expert_number], preferred_element_type=jnp.float32)
         running = part if running is None else running + part
-    mixed_rows = lax.psum_scatter(running, WIDE, scatter_dimension=0, tiled=True)
-    return mixed_rows.astype(jnp.bfloat16)
+    return reduce_rows(running, core, cores).astype(jnp.bfloat16)
+
+
+def reduce_rows(running, core, cores):
+    chips = lax.axis_size("wy")
+    block = running.shape[0] // (chips * cores)
+    by_chip = running.reshape(chips, cores, block, running.shape[1])
+    keep = jnp.where(core == 0, by_chip[:, 0], by_chip[:, 1])
+    send = jnp.where(core == 0, by_chip[:, 1], by_chip[:, 0])
+    chip_sum = keep + lax.ppermute(send, "wc", [(i, (i + 1) % cores) for i in range(cores)])
+    if chips == 2:
+        chip = lax.axis_index("wy")
+        mine = jnp.where(chip == 0, chip_sum[0], chip_sum[1])
+        away = jnp.where(chip == 0, chip_sum[1], chip_sum[0])
+        return mine + lax.ppermute(away, "wy", [(0, 1), (1, 0)])
+    return lax.psum_scatter(chip_sum, "wy", scatter_dimension=0, tiled=True).reshape(block, -1)
 
 
 def solution(mesh):

time: 346 us -> 334 us (0.965)
  waiting for transfers between devices: 228 us -> 213 us
    reduce_scatter x1 -> x0, waiting for transfers between devices: 31.9 us -> none  [per_device(): lax.psum_scatter(running, WIDE, scatter_dimension=0, tiled=True)]
    ppermute x0 -> x2, waiting for transfers between devices: none -> 16.7 us  [the longest x1 13.9 us: reduce_rows(): return mine + lax.ppermute(away, 'wy', [(0, 1), (1, 0)])]
    unnamed x28 -> x29, local copies, waits for them, and re-layouts: 6.55 us -> 7.95 us
  transfers between devices with their start and end apart: 6 -> 7, of which waited for: 6 -> 7; matrix products, arithmetic and copies ran while one was open for 9% -> 9% of each run, Pallas kernels for 0% -> 0%
where the time goes in v5:
time: 334 us; the launch traced here: 333 us
  waiting for transfers between devices  213 us (64%)
  matrix products  61.1 us (18%)
  local copies, waits for them, and re-layouts  29.9 us (9%)
  other arithmetic  13.6 us (4%)
  between operations  13.5 us (4%)
    all_gather x2, waiting for transfers between devices, per_device(): gathered = lax.all_gather(hidden, 'expert', axis=1, tiled=True)  95.8 us
    all_gather x1, waiting for transfers between devices, per_device(): arrived = lax.all_gather(mine_q, 'expert', axis=1, tiled=False)  57.1 us
    all_gather x1, waiting for transfers between devices, per_device(): gathered_q = lax.all_gather(packed, WIDE, axis=0, tiled=False)  39.5 us
    dot_general x2, matrix products, per_device(): jnp.dot(input_rows, up_weight[expert_number], preferred_element_type=jnp....  19.4 us
    dot_general x2, matrix products, per_device(): jnp.dot(gathered, down_weight[expert_number], preferred_element_type=jnp....  19.3 us
    dot_general x2, matrix products, per_device(): jnp.dot(input_rows, gate_weight[expert_number], preferred_element_type=jn...  18.7 us
    ppermute x1, waiting for transfers between devices, reduce_rows(): return mine + lax.ppermute(away, 'wy', [(0, 1), (1, 0)])  13.9 us
    unnamed x29, local copies, waits for them, and re-layouts  7.95 us
  transfers between devices with their start and end apart: 7, of which 7 were waited for; matrix products, arithmetic and copies ran while one was open for 9% of the time, Pallas kernels for 0%

profile of v5, /device:TPU:0, one launch (start us, length us, event | category | flops | bytes accessed | tf_op | source)
XLA Modules:
  0.0 333.4 jit_solution(11744506258537552692)
XLA Ops:
  6.6 2.5 pad_maximum_fusion.1
  10.0 39.5 %all-gather.11.cloned.1.call-done = bf16[1536,1536]{1,0:T(8,128)(2,1)} async-done(((bf16[384,1536]{1,0:T(8,128)(2,1)}), bf16[1536,1536]{1,0:T(8,128)(2,1)}) %all-gather.11.cloned.1.call-update) | async-done | bytes 4718608 | tf_op jit(solution)/shard_map/all_gather | solution.py:42
  49.4 2.7 slice.122
  52.2 3.7 %slice.123 = bf16[4,256,1536]{2,1,0:T(8,128)(2,1)} slice(bf16[4,384,1536]{2,1,0:T(8,128)(2,1)} %bitcast.117), slice={[0:4], [128:384], [0:1536]} | slice | bytes 6291456 | tf_op jit(solution)/shard_map/slice | solution.py:46
  55.9 2.0 gather_fusion
  57.9 3.6 %gather_fusion.2 = bf16[3,2,64,1536]{3,2,1,0:T(8,128)(2,1)} fusion(bf16[8,2,64,1536]{3,2,1,0:T(8,128)(2,1)} %bitcast.115, s32[1024]{0:T(1024)S(1)} %pad_clamp_fusion), kind=kCustom, calls=%fused_computation.2 | custom fusion | bytes 2359308 | tf_op jit(solution)/shard_map/jit(_take)/gather | solution.py:51
  61.5 1.9 fusion.34
  64.3 1.0 copy.28
  65.6 0.9 fusion.43
  66.6 57.1 %all-gather.13.cloned.1.call-done = bf16[192,7168]{1,0:T(8,128)(2,1)} async-done(((bf16[192,1792]{1,0:T(8,128)(2,1)}), bf16[192,7168]{1,0:T(8,128)(2,1)}) %all-gather.13.cloned.1.call-update) | async-done | bytes 2752528 | tf_op jit(solution)/shard_map/all_gather | solution.py:66
  123.7 6.2 %reshape.102 = bf16[192,4,1792]{2,1,0:T(4,128)(2,1)} reshape(bf16[192,7168]{1,0:T(8,128)(2,1)} %all-gather.13.cloned.1.call-done) | data formatting | bytes 5505024 | tf_op jit(solution)/shard_map/all_gather | solution.py:66
  129.9 1.8 copy-done.6
  133.3 1.8 pad_maximum_fusion
  135.8 4.3 %collective-permute-done = bf16[192,6272]{1,0:T(8,128)(2,1)} collective-permute-done((bf16[192,6272]{1,0:T(8,128)(2,1)}, bf16[192,6272]{1,0:T(8,128)(2,1)}, u32[]{:S(2)}, u32[]{:S(2)}) %collective-permute-start) | collective-permute-done | bytes 2408480 | tf_op jit(solution)/shard_map/ppermute | solution.py:72
  140.1 3.2 broadcast_select_fusion.1
  144.0 2.1 copy-done.4
  146.1 1.3 fusion.57
  148.5 2.1 copy-done.5
  150.6 9.1 %fusion.4 = f32[384,1024]{1,0:T(8,128)S(1)} fusion(bf16[384,6144]{1,0:T(8,128)(2,1)S(1)} %copy-done.5, bf16[2,6144,1024]{2,1,0:T(8,128)(2,1)} %param.17), kind=kOutput, calls=%fused_computation.8 | convolution fusion | flops 4831838208 | bytes 18874368 | tf_op jit(solution)/shard_map/dot_general | solution.py:96
  159.7 9.0 %fusion.25 = bf16[384,1024]{1,0:T(8,128)(2,1)} fusion(f32[384,2,1024]{2,0,1:T(8,128)S(1)} %bitcast.118, f32[384,1024]{1,0:T(8,128)S(1)} %fusion.4, bf16[384,6144]{1,0:T(8,128)(2,1)S(1)} %copy-done.5, bf16[2,6144,1024]{2,1,0:T(8,128)(2,1)} %param.18, f32[384]{0:T(512)S(1)} %get-tuple-element.6), kind=kOutput, calls=%fused_computation.34 | convolution fusion | flops 4835377152 | bytes 21235200 | tf_op jit(solution)/shard_map/dot_general | solution.py:100
  169.0 9.5 %fusion.10 = f32[384,1024]{1,0:T(8,128)S(1)} fusion(bf16[384,6144]{1,0:T(8,128)(2,1)} %copy-done.4, bf16[2,6144,1024]{2,1,0:T(8,128)(2,1)} %param.17), kind=kOutput, calls=%fused_computation.14 | convolution fusion | flops 4831838208 | bytes 18874368 | tf_op jit(solution)/shard_map/dot_general | solution.py:96
  178.5 10.4 %fusion.29 = bf16[384,1024]{1,0:T(8,128)(2,1)} fusion(f32[384,2,1024]{2,0,1:T(8,128)S(1)} %bitcast.119, f32[384,1024]{1,0:T(8,128)S(1)} %fusion.10, bf16[384,6144]{1,0:T(8,128)(2,1)} %copy-done.4, bf16[2,6144,1024]{2,1,0:T(8,128)(2,1)} %param.18, f32[384]{0:T(512)S(1)} %get-tuple-element.5), kind=kOutput, calls=%fused_computation.39 | convolution fusion | flops 4835377152 | bytes 21235200 | tf_op jit(solution)/shard_map/dot_general | solution.py:100
  189.0 42.1 %all-gather.9.cloned.1.call-done = bf16[384,4096]{1,0:T(8,128)(2,1)} async-done(((bf16[384,1024]{1,0:T(8,128)(2,1)}), bf16[384,4096]{1,0:T(8,128)(2,1)}) %all-gather.9.cloned.1.call-update) | async-done | bytes 3145744 | tf_op jit(solution)/shard_map/all_gather | solution.py:106
  231.1 10.0 %fusion = f32[384,1536]{1,0:T(8,128)} fusion(bf16[384,4096]{1,0:T(8,128)(2,1)} %all-gather.9.cloned.1.call-done, bf16[2,4096,1536]{2,1,0:T(8,128)(2,1)} %param.19), kind=kOutput, calls=%fused_computation.4 | convolution fusion | flops 4831838208 | bytes 18087936 | tf_op jit(solution)/shard_map/dot_general | solution.py:107
  241.1 53.6 %all-gather.7.cloned.1.call-done = bf16[384,4096]{1,0:T(8,128)(2,1)} async-done(((bf16[384,1024]{1,0:T(8,128)(2,1)}), bf16[384,4096]{1,0:T(8,128)(2,1)}) %all-gather.7.cloned.1.call-update) | async-done | bytes 3145744 | tf_op jit(solution)/shard_map/all_gather | solution.py:106
  294.7 9.3 %fusion.19 = f32[384,1536]{1,0:T(8,128)S(1)} fusion(f32[384,1536]{1,0:T(8,128)} %fusion, bf16[384,4096]{1,0:T(8,128)(2,1)} %all-gather.7.cloned.1.call-done, bf16[2,4096,1536]{2,1,0:T(8,128)(2,1)} %param.19), kind=kOutput, calls=%fused_computation.25 | convolution fusion | flops 4832428032 | bytes 20447232 | tf_op jit(solution)/shard_map/dot_general | solution.py:107
  304.0 1.4 copy-done.7
  305.7 2.8 collective-permute-done.1
  308.5 2.0 bitcast_add_fusion
  310.6 1.5 collective-permute-start.2
  312.1 13.9 %collective-permute-done.2 = f32[96,1536]{1,0:T(8,128)S(1)} collective-permute-done((f32[96,1536]{1,0:T(8,128)S(1)}, f32[96,1536]{1,0:T(8,128)S(1)}, u32[]{:S(2)}, u32[]{:S(2)}) %collective-permute-start.2) | collective-permute-done | bytes 589856 | tf_op jit(solution)/shard_map/ppermute | solution.py:123
  326.0 0.8 fusion.44
  (63 shorter events, 6.6 us)
Async XLA Ops:
  6.5 128.6 %copy-start = (bf16[8,2,64,1024]{3,2,1,0:T(8,128)(2,1)S(1)}, bf16[8,2,64,1024]{3,2,1,0:T(8,128)(2,1)}, u32[]{:S(2)}) copy-start(bf16[8,2,64,1024]{3,2,1,0:T(8,128)(2,1)} %param.21) | copy-start | bytes 6291460
  6.5 2.6 copy-start.12
  6.5 2.6 copy-start.2
  6.5 3.3 copy-start.13
  6.5 42.9 %all-gather.11.cloned.1.call-start = ((), (), s32[]{:S(2)}) async-start(), calls=%async_computation.2 | async-start | bytes 5898240 | tf_op jit(solution)/shard_map/all_gather | solution.py:42
  9.1 114.6 %all-gather.13.cloned.1.call-start = ((), (), s32[]{:S(2)}) async-start(), calls=%async_computation.3 | async-start | bytes 3440640 | tf_op jit(solution)/shard_map/all_gather | solution.py:66
  66.6 164.6 %all-gather.9.cloned.1.call-start = ((), (), s32[]{:S(2)}) async-start(), calls=%async_computation.1 | async-start | bytes 3932160 | tf_op jit(solution)/shard_map/all_gather | solution.py:106
  129.9 1.8 copy-start.6
  129.9 2.6 slice-start
  133.0 2.2 copy-start.3
  133.3 2.5 copy-start.11
  135.1 4.9 %collective-permute-start = (bf16[192,6272]{1,0:T(8,128)(2,1)}, bf16[192,6272]{1,0:T(8,128)(2,1)}, u32[]{:S(2)}, u32[]{:S(2)}) collective-permute-start(bf16[192,6272]{1,0:T(8,128)(2,1)} %pad_maximum_fusion), channel_id=1, source_target_pairs={{0,4},{4,0},{1,5},{5,1},{2,6},{6,2},{3,7},{7,3},{8,12},{12,8},{9,1... | collective-permute-start | bytes 7225352 | tf_op jit(solution)/shard_map/ppermute | solution.py:72
  143.9 2.1 copy-start.4
  143.9 2.1 copy-start.10
  148.2 2.3 copy-start.5
  150.6 9.1 %copy-start.8 = (f32[3,128,2,1024]{3,1,0,2:T(8,128)}, f32[3,128,2,1024]{3,1,0,2:T(8,128)S(1)}, u32[]{:S(2)}) copy-start(f32[3,128,2,1024]{3,1,0,2:T(8,128)S(1)} %copy.31) | copy-start | bytes 9437188
  168.7 126.0 %all-gather.7.cloned.1.call-start = ((), (), s32[]{:S(2)}) async-start(), calls=%async_computation | async-start | bytes 3932160 | tf_op jit(solution)/shard_map/all_gather | solution.py:106
  169.0 9.5 %copy-start.9 = (f32[3,128,2,1024]{3,1,0,2:T(8,128)S(1)}, f32[3,128,2,1024]{3,1,0,2:T(8,128)}, u32[]{:S(2)}) copy-start(f32[3,128,2,1024]{3,1,0,2:T(8,128)} %copy-done.8) | copy-start | bytes 9437188
  304.0 1.4 copy-start.7
  305.6 2.9 collective-permute-start.1
  308.5 18.4 %copy-start.1 = (bf16[8,2,64,1024]{3,2,1,0:T(8,128)(2,1)S(1)}, bf16[8,2,64,1024]{3,2,1,0:T(8,128)(2,1)}, u32[]{:S(2)}) copy-start(bf16[8,2,64,1024]{3,2,1,0:T(8,128)(2,1)} %param.21) | copy-start | bytes 6291460
  310.6 15.4 %collective-permute-start.2 = (f32[96,1536]{1,0:T(8,128)S(1)}, f32[96,1536]{1,0:T(8,128)S(1)}, u32[]{:S(2)}, u32[]{:S(2)}) collective-permute-start(f32[96,1536]{1,0:T(8,128)S(1)} %select_bitcast_fusion.1), channel_id=1, source_target_pairs={{0,8},{8,0},{1,9},{9,1},{2,10},{10,2},{3,11},{11,3},{4,12},{12,4},... | collective-permute-start | bytes 1769480 | tf_op jit(solution)/shard_map/ppermute | solution.py:123
Sparse Core Ops, SparseCore 0:
  9.2 40.1 all-gather.10
  66.7 56.9 all-gather.12
  168.9 62.2 all-gather.8
  232.5 62.1 all-gather.6

commit v6 on v5

--- a/solution.py
+++ b/solution.py
@@ -37,20 +37,29 @@
     tile_rows = tokens // tile_count
     resident_slots = adapter_down_weight.shape[0]
     rank = adapter_down_weight.shape[3]
-    held = jnp.transpose(adapter_down_weight, (0, 1, 3, 2)).reshape(-1, quarter)
-    packed = jnp.concatenate([prompts.reshape(-1, quarter), held], axis=0)
-    gathered_q = lax.all_gather(packed, WIDE, axis=0, tiled=False)
-    wide_size = gathered_q.shape[0]
-    slot_rows = prompts.shape[0] * span
-    slots_q = gathered_q[:, :slot_rows]
-    adapters_q = gathered_q[:, slot_rows:].reshape(wide_size * resident_slots, window, rank, quarter)
+    slots_q = lax.all_gather(prompts, WIDE, axis=0, tiled=True)
     slot_of_span = span_slot_owner[:nchunk]
-    rows_q = jnp.take(slots_q.reshape(-1, span, quarter), slot_of_span, axis=0).reshape(tokens, quarter)
+    rows_q = jnp.take(slots_q, slot_of_span, axis=0).reshape(tokens, quarter)
 
+    chips = lax.axis_size("wy")
     tile_slot_index = jnp.take(tenant_adapter_slot, tile_tenant_index)
-    tile_adapters = jnp.take(adapters_q, tile_slot_index, axis=0)
+    holder = tile_slot_index // resident_slots
+    local_slot = tile_slot_index % resident_slots
+    if chips == 2 and cores == 2:
+        swap = [(0, 1), (1, 0)]
+        from_chip = lax.ppermute(adapter_down_weight, "wy", swap)
+        from_core = lax.ppermute(adapter_down_weight, "wc", swap)
+        from_both = lax.ppermute(from_chip, "wc", swap)
+        stacked = jnp.stack([adapter_down_weight, from_core, from_chip, from_both])
+        source = jnp.bitwise_xor(holder, wide_index)
+    else:
+        stacked = lax.all_gather(adapter_down_weight, WIDE, axis=0, tiled=False)
+        source = holder
+    flat_held = stacked.reshape((-1,) + adapter_down_weight.shape[1:])
+    tile_adapters = jnp.take(flat_held, source * resident_slots + local_slot, axis=0)
+
     partial_rank = jnp.einsum(
-        "ntd,nerd->nter",
+        "ntd,nedr->nter",
         rows_q.reshape(tile_count, tile_rows, quarter),
         tile_adapters,
         preferred_element_type=jnp.float32,

time: 334 us -> 321 us (0.961)
  waiting for transfers between devices: 213 us -> 200 us
  local copies, waits for them, and re-layouts: 29.9 us -> 23 us
  other arithmetic: 13.6 us -> 17.3 us
    all_gather x1, waiting for transfers between devices: 39.5 us -> 0.01 us  [per_device(): slots_q = lax.all_gather(prompts, WIDE, axis=0, tiled=True)]
    ppermute x0 -> x3, waiting for transfers between devices: none -> 24.2 us  [the longest x1 23.3 us: per_device(): from_chip = lax.ppermute(adapter_down_weight, 'wy', swap)]
    slice x2 -> x0, local copies, waits for them, and re-layouts: 6.46 us -> none  [the longest x1 3.72 us: per_device(): gathered_q[:, slot_rows:]]
    unnamed x29 -> x23, local copies, waits for them, and re-layouts: 7.95 us -> 7.94 us
  transfers between devices with their start and end apart: 7 -> 10, of which waited for: 7 -> 8; matrix products, arithmetic and copies ran while one was open for 9% -> 13% of each run, Pallas kernels for 0% -> 0%
where the time goes in v6:
time: 321 us; the launch traced here: 320 us
  waiting for transfers between devices  200 us (62%)
  matrix products  61.1 us (19%)
  local copies, waits for them, and re-layouts  23 us (7%)
  other arithmetic  17.3 us (5%)
  between operations  13.4 us (4%)
  starting transfers between devices  4.97 us (2%)
    all_gather x2, waiting for transfers between devices, per_device(): gathered = lax.all_gather(hidden, 'expert', axis=1, tiled=True)  95.7 us
    all_gather x1, waiting for transfers between devices, per_device(): arrived = lax.all_gather(mine_q, 'expert', axis=1, tiled=False)  59.3 us
    ppermute x1, waiting for transfers between devices, per_device(): from_chip = lax.ppermute(adapter_down_weight, 'wy', swap)  23.3 us
    dot_general x2, matrix products, per_device(): jnp.dot(input_rows, up_weight[expert_number], preferred_element_type=jnp....  19.4 us
    dot_general x2, matrix products, per_device(): jnp.dot(gathered, down_weight[expert_number], preferred_element_type=jnp....  19.3 us
    dot_general x2, matrix products, per_device(): jnp.dot(input_rows, gate_weight[expert_number], preferred_element_type=jn...  18.7 us
    ppermute x1, waiting for transfers between devices, reduce_rows(): return mine + lax.ppermute(away, 'wy', [(0, 1), (1, 0)])  13.9 us
    unnamed x23, local copies, waits for them, and re-layouts  7.94 us
  transfers between devices with their start and end apart: 10, of which 8 were waited for; matrix products, arithmetic and copies ran while one was open for 13% of the time, Pallas kernels for 0%

profile of v6, /device:TPU:0, one launch (start us, length us, event | category | flops | bytes accessed | tf_op | source)
XLA Modules:
  0.0 320.1 jit_solution(7276344345402028918)
XLA Ops:
  6.5 3.0 collective-permute-start.1
  10.3 1.3 gather_fusion.1
  11.6 23.3 %collective-permute-done.1 = bf16[2,2,1536,64]{2,3,1,0:T(8,128)(2,1)S(1)} collective-permute-done((bf16[2,2,1536,64]{2,3,1,0:T(8,128)(2,1)}, bf16[2,2,1536,64]{2,3,1,0:T(8,128)(2,1)S(1)}, u32[]{:S(2)}, u32[]{:S(2)}) %collective-permute-start.1) | collective-permute-done | bytes 786464 | tf_op jit(solution)/shard_map/ppermute | solution.py:50
  37.2 3.0 pad_maximum_fusion
  40.2 2.5 gather_fusion.2
  42.8 1.2 broadcast_select_fusion.2
  44.0 2.0 gather_fusion
  46.0 1.8 fusion.34
  48.8 1.0 copy.28
  50.0 0.9 fusion.40
  51.0 59.3 %all-gather.12.cloned.1.call-done = bf16[192,7168]{1,0:T(8,128)(2,1)} async-done(((bf16[192,1792]{1,0:T(8,128)(2,1)}), bf16[192,7168]{1,0:T(8,128)(2,1)}) %all-gather.12.cloned.1.call-update) | async-done | bytes 2752528 | tf_op jit(solution)/shard_map/all_gather | solution.py:75
  110.3 6.2 %reshape.122 = bf16[192,4,1792]{2,1,0:T(4,128)(2,1)} reshape(bf16[192,7168]{1,0:T(8,128)(2,1)} %all-gather.12.cloned.1.call-done) | data formatting | bytes 5505024 | tf_op jit(solution)/shard_map/all_gather | solution.py:75
  116.5 1.8 copy-done.5
  119.9 1.9 pad_maximum_fusion.1
  122.4 4.3 %collective-permute-done.3 = bf16[192,6272]{1,0:T(8,128)(2,1)} collective-permute-done((bf16[192,6272]{1,0:T(8,128)(2,1)}, bf16[192,6272]{1,0:T(8,128)(2,1)}, u32[]{:S(2)}, u32[]{:S(2)}) %collective-permute-start.3) | collective-permute-done | bytes 2408480 | tf_op jit(solution)/shard_map/ppermute | solution.py:81
  126.8 3.2 broadcast_select_fusion.1
  130.6 2.1 copy-done.3
  132.7 1.3 fusion.54
  135.1 2.1 copy-done.4
  137.2 9.1 %fusion.4 = f32[384,1024]{1,0:T(8,128)S(1)} fusion(bf16[384,6144]{1,0:T(8,128)(2,1)S(1)} %copy-done.4, bf16[2,6144,1024]{2,1,0:T(8,128)(2,1)} %param.17), kind=kOutput, calls=%fused_computation.8 | convolution fusion | flops 4831838208 | bytes 18874368 | tf_op jit(solution)/shard_map/dot_general | solution.py:105
  146.4 9.0 %fusion.25 = bf16[384,1024]{1,0:T(8,128)(2,1)} fusion(f32[384,2,1024]{2,0,1:T(8,128)S(1)} %bitcast.115, f32[384,1024]{1,0:T(8,128)S(1)} %fusion.4, bf16[384,6144]{1,0:T(8,128)(2,1)S(1)} %copy-done.4, bf16[2,6144,1024]{2,1,0:T(8,128)(2,1)} %param.18, f32[384]{0:T(512)S(1)} %get-tuple-element.6), kind=kOutput, calls=%fused_computation.35 | convolution fusion | flops 4835377152 | bytes 21235200 | tf_op jit(solution)/shard_map/dot_general | solution.py:109
  155.6 9.5 %fusion.10 = f32[384,1024]{1,0:T(8,128)S(1)} fusion(bf16[384,6144]{1,0:T(8,128)(2,1)} %copy-done.3, bf16[2,6144,1024]{2,1,0:T(8,128)(2,1)} %param.17), kind=kOutput, calls=%fused_computation.14 | convolution fusion | flops 4831838208 | bytes 18874368 | tf_op jit(solution)/shard_map/dot_general | solution.py:105
  165.2 10.4 %fusion.29 = bf16[384,1024]{1,0:T(8,128)(2,1)} fusion(f32[384,2,1024]{2,0,1:T(8,128)S(1)} %bitcast.116, f32[384,1024]{1,0:T(8,128)S(1)} %fusion.10, bf16[384,6144]{1,0:T(8,128)(2,1)} %copy-done.3, bf16[2,6144,1024]{2,1,0:T(8,128)(2,1)} %param.18, f32[384]{0:T(512)S(1)} %get-tuple-element.5), kind=kOutput, calls=%fused_computation.40 | convolution fusion | flops 4835377152 | bytes 21235200 | tf_op jit(solution)/shard_map/dot_general | solution.py:109
  175.6 42.1 %all-gather.10.cloned.1.call-done = bf16[384,4096]{1,0:T(8,128)(2,1)} async-done(((bf16[384,1024]{1,0:T(8,128)(2,1)}), bf16[384,4096]{1,0:T(8,128)(2,1)}) %all-gather.10.cloned.1.call-update) | async-done | bytes 3145744 | tf_op jit(solution)/shard_map/all_gather | solution.py:115
  217.8 10.0 %fusion = f32[384,1536]{1,0:T(8,128)} fusion(bf16[384,4096]{1,0:T(8,128)(2,1)} %all-gather.10.cloned.1.call-done, bf16[2,4096,1536]{2,1,0:T(8,128)(2,1)} %param.19), kind=kOutput, calls=%fused_computation.4 | convolution fusion | flops 4831838208 | bytes 18087936 | tf_op jit(solution)/shard_map/dot_general | solution.py:116
  227.8 53.6 %all-gather.8.cloned.1.call-done = bf16[384,4096]{1,0:T(8,128)(2,1)} async-done(((bf16[384,1024]{1,0:T(8,128)(2,1)}), bf16[384,4096]{1,0:T(8,128)(2,1)}) %all-gather.8.cloned.1.call-update) | async-done | bytes 3145744 | tf_op jit(solution)/shard_map/all_gather | solution.py:115
  281.4 9.3 %fusion.19 = f32[384,1536]{1,0:T(8,128)S(1)} fusion(f32[384,1536]{1,0:T(8,128)} %fusion, bf16[384,4096]{1,0:T(8,128)(2,1)} %all-gather.8.cloned.1.call-done, bf16[2,4096,1536]{2,1,0:T(8,128)(2,1)} %param.19), kind=kOutput, calls=%fused_computation.26 | convolution fusion | flops 4832428032 | bytes 20447232 | tf_op jit(solution)/shard_map/dot_general | solution.py:116
  290.7 1.4 copy-done.6
  292.3 2.8 collective-permute-done.4
  295.2 2.0 bitcast_add_fusion
  297.3 1.5 collective-permute-start.5
  298.8 13.9 %collective-permute-done.5 = f32[96,1536]{1,0:T(8,128)S(1)} collective-permute-done((f32[96,1536]{1,0:T(8,128)S(1)}, f32[96,1536]{1,0:T(8,128)S(1)}, u32[]{:S(2)}, u32[]{:S(2)}) %collective-permute-start.5) | collective-permute-done | bytes 589856 | tf_op jit(solution)/shard_map/ppermute | solution.py:132
  (63 shorter events, 9.6 us)
Async XLA Ops:
  6.5 115.3 %copy-start = (bf16[8,2,64,1024]{3,2,1,0:T(8,128)(2,1)S(1)}, bf16[8,2,64,1024]{3,2,1,0:T(8,128)(2,1)}, u32[]{:S(2)}) copy-start(bf16[8,2,64,1024]{3,2,1,0:T(8,128)(2,1)} %param.21) | copy-start | bytes 6291460
  6.5 37.5 %all-gather.6.cloned.1.call-start = ((), (), s32[]{:S(2)}) async-start(), calls=%async_computation | async-start | bytes 1966080 | tf_op jit(solution)/shard_map/all_gather | solution.py:40
  6.5 28.4 %collective-permute-start.1 = (bf16[2,2,1536,64]{2,3,1,0:T(8,128)(2,1)}, bf16[2,2,1536,64]{2,3,1,0:T(8,128)(2,1)S(1)}, u32[]{:S(2)}, u32[]{:S(2)}) collective-permute-start(bf16[2,2,1536,64]{2,3,1,0:T(8,128)(2,1)} %param.20), channel_id=1, source_target_pairs={{0,8},{8,0},{1,9},{9,1},{2,10},{10,2},{3,11},{11,3},{4,12},{12,4},... | collective-permute-start | bytes 2359304 | tf_op jit(solution)/shard_map/ppermute | solution.py:50
  9.5 100.8 %all-gather.12.cloned.1.call-start = ((), (), s32[]{:S(2)}) async-start(), calls=%async_computation.3 | async-start | bytes 3440640 | tf_op jit(solution)/shard_map/all_gather | solution.py:75
  9.6 26.8 %collective-permute-start = (bf16[2,2,1536,64]{2,3,1,0:T(8,128)(2,1)}, bf16[2,2,1536,64]{2,3,1,0:T(8,128)(2,1)}, u32[]{:S(2)}, u32[]{:S(2)}) collective-permute-start(bf16[2,2,1536,64]{2,3,1,0:T(8,128)(2,1)} %param.20), channel_id=1, source_target_pairs={{0,4},{4,0},{1,5},{5,1},{2,6},{6,2},{3,7},{7,3},{8,12},{12,8},{9,1... | collective-permute-start | bytes 2359304 | tf_op jit(solution)/shard_map/ppermute | solution.py:51
  34.9 2.3 collective-permute-start.2
  51.0 166.8 %all-gather.10.cloned.1.call-start = ((), (), s32[]{:S(2)}) async-start(), calls=%async_computation.2 | async-start | bytes 3932160 | tf_op jit(solution)/shard_map/all_gather | solution.py:115
  116.5 1.8 copy-start.5
  116.5 2.6 slice-start
  119.6 2.2 copy-start.2
  119.9 2.5 copy-start.10
  121.8 4.9 %collective-permute-start.3 = (bf16[192,6272]{1,0:T(8,128)(2,1)}, bf16[192,6272]{1,0:T(8,128)(2,1)}, u32[]{:S(2)}, u32[]{:S(2)}) collective-permute-start(bf16[192,6272]{1,0:T(8,128)(2,1)} %pad_maximum_fusion.1), channel_id=1, source_target_pairs={{0,4},{4,0},{1,5},{5,1},{2,6},{6,2},{3,7},{7,3},{8,12},{12,8},{9,1... | collective-permute-start | bytes 7225352 | tf_op jit(solution)/shard_map/ppermute | solution.py:81
  130.6 2.1 copy-start.3
  130.6 2.1 copy-start.9
  134.9 2.3 copy-start.4
  137.2 9.1 %copy-start.7 = (f32[3,128,2,1024]{3,1,0,2:T(8,128)}, f32[3,128,2,1024]{3,1,0,2:T(8,128)S(1)}, u32[]{:S(2)}) copy-start(f32[3,128,2,1024]{3,1,0,2:T(8,128)S(1)} %copy.31) | copy-start | bytes 9437188
  155.4 126.0 %all-gather.8.cloned.1.call-start = ((), (), s32[]{:S(2)}) async-start(), calls=%async_computation.1 | async-start | bytes 3932160 | tf_op jit(solution)/shard_map/all_gather | solution.py:115
  155.6 9.5 %copy-start.8 = (f32[3,128,2,1024]{3,1,0,2:T(8,128)S(1)}, f32[3,128,2,1024]{3,1,0,2:T(8,128)}, u32[]{:S(2)}) copy-start(f32[3,128,2,1024]{3,1,0,2:T(8,128)} %copy-done.7) | copy-start | bytes 9437188
  290.7 1.4 copy-start.6
  292.2 2.9 collective-permute-start.4
  295.2 18.4 %copy-start.1 = (bf16[8,2,64,1024]{3,2,1,0:T(8,128)(2,1)S(1)}, bf16[8,2,64,1024]{3,2,1,0:T(8,128)(2,1)}, u32[]{:S(2)}) copy-start(bf16[8,2,64,1024]{3,2,1,0:T(8,128)(2,1)} %param.21) | copy-start | bytes 6291460
  297.3 15.4 %collective-permute-start.5 = (f32[96,1536]{1,0:T(8,128)S(1)}, f32[96,1536]{1,0:T(8,128)S(1)}, u32[]{:S(2)}, u32[]{:S(2)}) collective-permute-start(f32[96,1536]{1,0:T(8,128)S(1)} %select_bitcast_fusion.1), channel_id=1, source_target_pairs={{0,8},{8,0},{1,9},{9,1},{2,10},{10,2},{3,11},{11,3},{4,12},{12,4},... | collective-permute-start | bytes 1769480 | tf_op jit(solution)/shard_map/ppermute | solution.py:132
Sparse Core Ops, SparseCore 0:
  9.7 27.7 all-gather.5
  51.1 59.1 all-gather.11
  155.5 62.2 all-gather.9
  219.2 62.1 all-gather.7

commit v7 on v6

--- a/solution.py
+++ b/solution.py
@@ -73,49 +73,88 @@
     mine_q = lax.dynamic_slice_in_dim(mine_q, core * half, half, 0)
     expert_size = lax.axis_size("expert")
     arrived = lax.all_gather(mine_q, "expert", axis=1, tiled=False)
-    mine = arrived[:, :, :quarter].reshape(half, expert_size * quarter)
-    pieces = arrived[:, :, quarter:].astype(jnp.float32)
-    summed = jnp.sum(pieces[:, :, : window * rank] + pieces[:, :, window * rank :], axis=1)
-    mine_rank = summed.astype(jnp.bfloat16)
-    mine = jnp.concatenate([mine, mine_rank], axis=1)
-    other = lax.ppermute(mine, "wc", [(i, (i + 1) % cores) for i in range(cores)])
-    first = jnp.where(core == 0, mine, other)
-    second = jnp.where(core == 0, other, mine)
-    both = jnp.concatenate([first, second], axis=0)
-    input_rows = both[:, : expert_size * quarter]
-    lowrank = both[:, expert_size * quarter :].reshape(tile_count, tile_rows, window, rank)
-
-    logits = jnp.dot(input_rows, router, preferred_element_type=jnp.float32)
+    swap = [(i, (i + 1) % cores) for i in range(cores)]
+    halves = (arrived, lax.ppermute(arrived, "wc", swap))
+
+    def true_order(mine, other):
+        return jnp.where(
+            core == 0, jnp.concatenate([mine, other], axis=0), jnp.concatenate([other, mine], axis=0)
+        )
+
+    def local_halves(whole):
+        return tuple(
+            lax.dynamic_slice_in_dim(whole, start * half, half, 0) for start in (core, 1 - core)
+        )
+
+    rows = []
+    ranks = []
+    for piece in halves:
+        rows.append(piece[:, :, :quarter].reshape(half, expert_size * quarter))
+        parts = piece[:, :, quarter:].astype(jnp.float32)
+        ranks.append(
+            jnp.sum(parts[:, :, : window * rank] + parts[:, :, window * rank :], axis=1).astype(
+                jnp.bfloat16
+            )
+        )
+    tile_up = jnp.take(adapter_up_weight, tile_tenant_index, axis=0)
     experts = jnp.arange(router.shape[1], dtype=jnp.int32)
-    picked = (row_expert_index[:, :, None] == experts[None, None, :]).astype(jnp.float32)
-    chosen = jnp.sum(picked * logits[:, None, :], axis=2)
-    first_prob = jax.nn.sigmoid(chosen[:, 0] - chosen[:, 1])
-    second_prob = jax.nn.sigmoid(chosen[:, 1] - chosen[:, 0])
-    weight = (
-        first_prob[:, None] * picked[:, 0, :window] + second_prob[:, None] * picked[:, 1, :window]
-    )
-
-    tile_up = jnp.take(adapter_up_weight, tile_tenant_index, axis=0)
-    adapted_hidden = jnp.einsum(
-        "nter,nerf->ntef", lowrank, tile_up, preferred_element_type=jnp.float32
-    ).reshape(tokens, window, tile_up.shape[3])
-
-    running = None
+    index_halves = local_halves(row_expert_index)
+    weights = []
+    adapted = []
+    for h in range(2):
+        logits = jnp.dot(rows[h], router, preferred_element_type=jnp.float32)
+        picked = (index_halves[h][:, :, None] == experts[None, None, :]).astype(jnp.float32)
+        chosen = jnp.sum(picked * logits[:, None, :], axis=2)
+        first_prob = jax.nn.sigmoid(chosen[:, 0] - chosen[:, 1])
+        second_prob = jax.nn.sigmoid(chosen[:, 1] - chosen[:, 0])
+        weights.append(
+            first_prob[:, None] * picked[:, 0, :window]
+            + second_prob[:, None] * picked[:, 1, :window]
+        )
+        blank = jnp.zeros_like(ranks[h])
+        placed = true_order(ranks[h], blank) if h == 0 else true_order(blank, ranks[h])
+        adapted_all = jnp.einsum(
+            "nter,nerf->ntef",
+            placed.reshape(tile_count, tile_rows, window, rank),
+            tile_up,
+            preferred_element_type=jnp.float32,
+        ).reshape(tokens, window, tile_up.shape[3])
+        adapted.append(local_halves(adapted_all)[h])
+
+    running = [None, None]
+    previous = None
     for expert_number in range(window):
-        gate_pre = jnp.dot(
-            input_rows, gate_weight[expert_number], preferred_element_type=jnp.float32
-        )
-        up_value = (
-            jnp.dot(input_rows, up_weight[expert_number], preferred_element_type=jnp.float32)
-            + ADAPTER_SCALE * adapted_hidden[:, expert_number]
-        )
-        hidden = (
-            weight[:, expert_number, None] * jax.nn.silu(gate_pre) * up_value
-        ).astype(jnp.bfloat16)
-        gathered = lax.all_gather(hidden, "expert", axis=1, tiled=True)
-        part = jnp.dot(gathered, down_weight[expert_number], preferred_element_type=jnp.float32)
-        running = part if running is None else running + part
-    return reduce_rows(running, core, cores).astype(jnp.bfloat16)
+        hidden = []
+        for h in range(2):
+            gate_pre = jnp.dot(
+                rows[h], gate_weight[expert_number], preferred_element_type=jnp.float32
+            )
+            up_value = (
+                jnp.dot(rows[h], up_weight[expert_number], preferred_element_type=jnp.float32)
+                + ADAPTER_SCALE * adapted[h][:, expert_number]
+            )
+            hidden.append(
+                (weights[h][:, expert_number, None] * jax.nn.silu(gate_pre) * up_value).astype(
+                    jnp.bfloat16
+                )
+            )
+        if expert_number == 0:
+            parts = []
+            for hd in hidden:
+                if previous is not None:
+                    hd, _ = lax.optimization_barrier((hd, previous))
+                previous = lax.all_gather(hd, "expert", axis=1, tiled=True)
+                parts.append(
+                    jnp.dot(previous, down_weight[expert_number], preferred_element_type=jnp.float32)
+                )
+        else:
+            joined = jnp.concatenate(hidden, axis=0)
+            joined, _ = lax.optimization_barrier((joined, previous))
+            previous = lax.all_gather(joined, "expert", axis=1, tiled=True)
+            part = jnp.dot(previous, down_weight[expert_number], preferred_element_type=jnp.float32)
+            parts = [part[:half], part[half:]]
+        running = [p if r is None else r + p for r, p in zip(running, parts)]
+    return reduce_rows(true_order(*running), core, cores).astype(jnp.bfloat16)
 
 
 def reduce_rows(running, core, cores):

time: 321 us -> 355 us (1.11)
  matrix products: 61.1 us -> 87.4 us
  local copies, waits for them, and re-layouts: 23 us -> 28.9 us
  waiting for transfers between devices: 200 us -> 204 us
    dot_general x8 -> x15, matrix products: 59.3 us -> 85.6 us  [the longest x4 32.4 us: per_device(): jnp.dot(rows[h], up_weight[expert_number], preferred_element_type=jnp.flo...]
    all_gather x2 -> x3, waiting for transfers between devices: 95.7 us -> 105 us  [the longest x1 63.8 us: per_device(): previous = lax.all_gather(joined, 'expert', axis=1, tiled=True)]
    ppermute x1, waiting for transfers between devices: 4.31 us -> 0.01 us  [per_device(): halves = (arrived, lax.ppermute(arrived, 'wc', swap))]
    slice x3 -> x4, local copies, waits for them, and re-layouts: 0.7 us -> 4.96 us  [the longest x2 4.95 us: per_device(): rows.append(piece[:, :, :quarter].reshape(half, expert_size * quarter))]
    unnamed x23 -> x30, local copies, waits for them, and re-layouts: 7.94 us -> 5.89 us
  transfers between devices with their start and end apart: 10 -> 11, of which waited for: 8 -> 8; matrix products, arithmetic and copies ran while one was open for 13% -> 19% of each run, Pallas kernels for 0% -> 0%
where the time goes in v7:
time: 355 us; the launch traced here: 354 us
  waiting for transfers between devices  204 us (57%)
  matrix products  87.4 us (25%)
  local copies, waits for them, and re-layouts  28.9 us (8%)
  other arithmetic  15.1 us (4%)
  between operations  13.6 us (4%)
  starting transfers between devices  5.05 us (1%)
    all_gather x1, waiting for transfers between devices, per_device(): previous = lax.all_gather(joined, 'expert', axis=1, tiled=True)  63.8 us
    all_gather x1, waiting for transfers between devices, per_device(): arrived = lax.all_gather(mine_q, 'expert', axis=1, tiled=False)  58.5 us
    all_gather x2, waiting for transfers between devices, per_device(): previous = lax.all_gather(hd, 'expert', axis=1, tiled=True)  41.2 us
    dot_general x4, matrix products, per_device(): jnp.dot(rows[h], up_weight[expert_number], preferred_element_type=jnp.flo...  32.4 us
    dot_general x4, matrix products, per_device(): jnp.dot(rows[h], gate_weight[expert_number], preferred_element_type=jnp.f...  29.3 us
    ppermute x1, waiting for transfers between devices, per_device(): from_chip = lax.ppermute(adapter_down_weight, 'wy', swap)  23.3 us
    dot_general x3, matrix products, per_device(): jnp.dot(previous, down_weight[expert_number], preferred_element_type=jnp....  21.2 us
    ppermute x1, waiting for transfers between devices, reduce_rows(): return mine + lax.ppermute(away, 'wy', [(0, 1), (1, 0)])  13.9 us
  transfers between devices with their start and end apart: 11, of which 8 were waited for; matrix products, arithmetic and copies ran while one was open for 19% of the time, Pallas kernels for 0%

profile of v7, /device:TPU:0, one launch (start us, length us, event | category | flops | bytes accessed | tf_op | source)
XLA Modules:
  0.0 354.4 jit_solution(15834963004559741849)
XLA Ops:
  6.5 3.0 collective-permute-start.1
  11.6 23.3 %collective-permute-done.1 = bf16[2,2,1536,64]{2,3,1,0:T(8,128)(2,1)S(1)} collective-permute-done((bf16[2,2,1536,64]{2,3,1,0:T(8,128)(2,1)}, bf16[2,2,1536,64]{2,3,1,0:T(8,128)(2,1)S(1)}, u32[]{:S(2)}, u32[]{:S(2)}) %collective-permute-start.1) | collective-permute-done | bytes 786464 | tf_op jit(solution)/shard_map/ppermute | solution.py:50
  37.2 2.9 pad_maximum_fusion
  40.2 2.5 gather_fusion.2
  43.9 2.0 gather_fusion
  45.9 1.8 fusion.75
  51.7 58.5 %all-gather.15.cloned.1.call-done = bf16[192,7168]{1,0:T(8,128)(2,1)} async-done(((bf16[192,1792]{1,0:T(8,128)(2,1)}), bf16[192,7168]{1,0:T(8,128)(2,1)}) %all-gather.15.cloned.1.call-update) | async-done | bytes 2752528 | tf_op jit(solution)/shard_map/all_gather | solution.py:75
  110.2 6.2 %reshape.141 = bf16[192,4,1792]{2,1,0:T(4,128)(2,1)} reshape(bf16[192,7168]{1,0:T(8,128)(2,1)} %all-gather.15.cloned.1.call-done) | data formatting | bytes 5505024 | tf_op jit(solution)/shard_map/all_gather | solution.py:75
  117.9 2.5 slice.169
  120.3 1.9 copy.49
  123.1 1.9 copy.36
  126.5 6.2 %fusion.8 = f32[192,1024]{1,0:T(8,128)S(1)} fusion(bf16[192,6144]{1,0:T(8,128)(2,1)S(1)} %bitcast.183, bf16[2,6144,1024]{2,1,0:T(8,128)(2,1)} %param.17), kind=kOutput, calls=%fused_computation.12 | convolution fusion | flops 2415919104 | bytes 15728640 | tf_op jit(solution)/shard_map/dot_general | solution.py:129
  132.8 8.1 %fusion.20 = f32[192,1024]{1,0:T(8,128)} fusion(bf16[192,6144]{1,0:T(8,128)(2,1)S(1)} %bitcast.184, bf16[2,6144,1024]{2,1,0:T(8,128)(2,1)} %param.17), kind=kOutput, calls=%fused_computation.24 | convolution fusion | flops 2415919104 | bytes 15728640 | tf_op jit(solution)/shard_map/dot_general | solution.py:129
  140.8 2.5 slice.179
  144.6 8.1 %fusion.18 = f32[192,1024]{1,0:T(8,128)} fusion(bf16[192,6144]{1,0:T(8,128)(2,1)S(1)} %bitcast.177, bf16[2,6144,1024]{2,1,0:T(8,128)(2,1)} %param.17), kind=kOutput, calls=%fused_computation.22 | convolution fusion | flops 2415919104 | bytes 15728640 | tf_op jit(solution)/shard_map/dot_general | solution.py:129
  155.0 1.9 copy.39
  158.0 8.2 %fusion.72 = bf16[192,1024]{1,0:T(8,128)(2,1)} fusion(bf16[192,6144]{1,0:T(8,128)(2,1)S(1)} %bitcast.185, bf16[2,6144,1024]{2,1,0:T(8,128)(2,1)} %param.18, f32[384,2,1024]{2,0,1:T(8,128)} %bitcast.188, s32[]{:T(128)S(6)} %select_n.135, f32[192,1024]{1,0:T(8,128)S(1)} %copy-done.13, f32[192]{0:T(256)S(1)} %bitcast.205), kind=kOutput, calls=%fused_computation.57 | convolution fusion | flops 2417688576 | bytes 16909060 | tf_op jit(solution)/shard_map/dot_general | solution.py:133
  166.5 8.3 %fusion.66 = bf16[192,1024]{1,0:T(8,128)(2,1)S(1)} fusion(bf16[192,6144]{1,0:T(8,128)(2,1)} %bitcast.181, bf16[2,6144,1024]{2,1,0:T(8,128)(2,1)} %param.18, f32[384,2,1024]{2,0,1:T(8,128)} %bitcast.189, s32[]{:T(128)S(6)} %select_n.135, s32[]{:T(128)S(6)} %add.153, f32[192,1024]{1,0:T(8,128)S(1)} %fusion.8, f32[192]{0:T(256)S(1)} %bitcast.203), kind=kOutput, calls=%fused_computation.55 | convolution fusion | flops 2417688576 | bytes 16909064 | tf_op jit(solution)/shard_map/dot_general | solution.py:133
  174.9 8.2 %fusion.69 = bf16[192,1024]{1,0:T(8,128)(2,1)} fusion(bf16[192,6144]{1,0:T(8,128)(2,1)S(1)} %bitcast.179, bf16[2,6144,1024]{2,1,0:T(8,128)(2,1)} %param.18, f32[384,2,1024]{2,0,1:T(8,128)} %bitcast.190, s32[]{:T(128)S(6)} %select_n.149, f32[192,1024]{1,0:T(8,128)S(1)} %copy-done.12, f32[192]{0:T(256)S(1)} %bitcast.204), kind=kOutput, calls=%fused_computation.56 | convolution fusion | flops 2417688576 | bytes 16909060 | tf_op jit(solution)/shard_map/dot_general | solution.py:133
  183.1 19.3 %all-gather.9.cloned.1.call-done = bf16[192,4096]{1,0:T(8,128)(2,1)} async-done(((bf16[192,1024]{1,0:T(8,128)(2,1)}), bf16[192,4096]{1,0:T(8,128)(2,1)}) %all-gather.9.cloned.1.call-update) | async-done | bytes 1572880 | tf_op jit(solution)/shard_map/all_gather | solution.py:146
  202.5 6.8 %fusion.6 = f32[192,1024]{1,0:T(8,128)S(1)} fusion(bf16[192,6144]{1,0:T(8,128)(2,1)} %bitcast.178, bf16[2,6144,1024]{2,1,0:T(8,128)(2,1)} %param.17), kind=kOutput, calls=%fused_computation.10 | convolution fusion | flops 2415919104 | bytes 15728640 | tf_op jit(solution)/shard_map/dot_general | solution.py:129
  209.3 7.7 %fusion.63 = bf16[192,1024]{1,0:T(8,128)(2,1)S(1)} fusion(bf16[192,6144]{1,0:T(8,128)(2,1)S(1)} %bitcast.180, bf16[2,6144,1024]{2,1,0:T(8,128)(2,1)} %param.18, f32[384,2,1024]{2,0,1:T(8,128)} %bitcast.191, s32[]{:T(128)S(6)} %select_n.149, s32[]{:T(128)S(6)} %add.153, f32[192,1024]{1,0:T(8,128)S(1)} %fusion.6, f32[192]{0:T(256)S(1)} %bitcast.202), kind=kOutput, calls=%fused_computation.54 | convolution fusion | flops 2417688576 | bytes 16909064 | tf_op jit(solution)/shard_map/dot_general | solution.py:133
  217.9 21.9 %all-gather.11.cloned.1.call-done = bf16[192,4096]{1,0:T(8,128)(2,1)} async-done(((bf16[192,1024]{1,0:T(8,128)(2,1)}), bf16[192,4096]{1,0:T(8,128)(2,1)}) %all-gather.11.cloned.1.call-update) | async-done | bytes 1572880 | tf_op jit(solution)/shard_map/all_gather | solution.py:146
  239.8 63.8 %all-gather.13.cloned.1.call-done = bf16[384,4096]{1,0:T(8,128)(2,1)} async-done(((bf16[384,1024]{1,0:T(8,128)(2,1)}), bf16[384,4096]{1,0:T(8,128)(2,1)}) %all-gather.13.cloned.1.call-update) | async-done | bytes 3145744 | tf_op jit(solution)/shard_map/all_gather | solution.py:153
  303.6 9.0 %fusion = f32[384,1536]{1,0:T(8,128)S(1)} fusion(bf16[384,4096]{1,0:T(8,128)(2,1)} %all-gather.13.cloned.1.call-done, bf16[2,4096,1536]{2,1,0:T(8,128)(2,1)} %param.19), kind=kOutput, calls=%fused_computation.4 | convolution fusion | flops 4831838208 | bytes 18087936 | tf_op jit(solution)/shard_map/dot_general | solution.py:154
  312.6 6.1 %fusion.33 = f32[192,1536]{1,0:T(8,128)S(1)} fusion(bf16[192,4096]{1,0:T(8,128)(2,1)S(1)} %copy-done.10, bf16[2,4096,1536]{2,1,0:T(8,128)(2,1)} %param.19, f32[384,1536]{1,0:T(8,128)S(1)} %fusion), kind=kOutput, calls=%fused_computation.38 | convolution fusion | flops 2416214016 | bytes 16515072 | tf_op jit(solution)/shard_map/dot_general | solution.py:148
  318.8 6.0 %fusion.36 = f32[192,1536]{1,0:T(8,128)S(1)} fusion(bf16[192,4096]{1,0:T(8,128)(2,1)S(1)} %copy-done.11, bf16[2,4096,1536]{2,1,0:T(8,128)(2,1)} %param.19, f32[384,1536]{1,0:T(8,128)S(1)} %fusion), kind=kOutput, calls=%fused_computation.39 | convolution fusion | flops 2416214016 | bytes 16515072 | tf_op jit(solution)/shard_map/dot_general | solution.py:148
  325.1 1.4 copy-done.2
  326.7 2.8 collective-permute-done.4
  329.5 2.0 bitcast_add_fusion
  331.6 1.6 collective-permute-start.5
  333.2 13.9 %collective-permute-done.5 = f32[96,1536]{1,0:T(8,128)S(1)} collective-permute-done((f32[96,1536]{1,0:T(8,128)S(1)}, f32[96,1536]{1,0:T(8,128)S(1)}, u32[]{:S(2)}, u32[]{:S(2)}) %collective-permute-start.5) | collective-permute-done | bytes 589856 | tf_op jit(solution)/shard_map/ppermute | solution.py:171
  (88 shorter events, 20.4 us)
Async XLA Ops:
  6.5 44.4 %copy-start = (bf16[8,2,64,1024]{3,2,1,0:T(8,128)(2,1)S(1)}, bf16[8,2,64,1024]{3,2,1,0:T(8,128)(2,1)}, u32[]{:S(2)}) copy-start(bf16[8,2,64,1024]{3,2,1,0:T(8,128)(2,1)} %param.21) | copy-start | bytes 6291460
  6.5 37.4 %all-gather.7.cloned.1.call-start = ((), (), s32[]{:S(2)}) async-start(), calls=%async_computation | async-start | bytes 1966080 | tf_op jit(solution)/shard_map/all_gather | solution.py:40
  6.5 28.4 %collective-permute-start.1 = (bf16[2,2,1536,64]{2,3,1,0:T(8,128)(2,1)}, bf16[2,2,1536,64]{2,3,1,0:T(8,128)(2,1)S(1)}, u32[]{:S(2)}, u32[]{:S(2)}) collective-permute-start(bf16[2,2,1536,64]{2,3,1,0:T(8,128)(2,1)} %param.20), channel_id=1, source_target_pairs={{0,8},{8,0},{1,9},{9,1},{2,10},{10,2},{3,11},{11,3},{4,12},{12,4},... | collective-permute-start | bytes 2359304 | tf_op jit(solution)/shard_map/ppermute | solution.py:50
  9.5 100.7 %all-gather.15.cloned.1.call-start = ((), (), s32[]{:S(2)}) async-start(), calls=%async_computation.4 | async-start | bytes 3440640 | tf_op jit(solution)/shard_map/all_gather | solution.py:75
  9.6 26.8 %collective-permute-start = (bf16[2,2,1536,64]{2,3,1,0:T(8,128)(2,1)}, bf16[2,2,1536,64]{2,3,1,0:T(8,128)(2,1)}, u32[]{:S(2)}, u32[]{:S(2)}) collective-permute-start(bf16[2,2,1536,64]{2,3,1,0:T(8,128)(2,1)} %param.20), channel_id=1, source_target_pairs={{0,4},{4,0},{1,5},{5,1},{2,6},{6,2},{3,7},{7,3},{8,12},{12,8},{9,1... | collective-permute-start | bytes 2359304 | tf_op jit(solution)/shard_map/ppermute | solution.py:51
  34.9 2.3 collective-permute-start.2
  49.9 1.6 copy-start.9
  50.9 151.5 %all-gather.9.cloned.1.call-start = ((), (), s32[]{:S(2)}) async-start(), calls=%async_computation.1 | async-start | bytes 1966080 | tf_op jit(solution)/shard_map/all_gather | solution.py:146
  116.5 24.4 %collective-permute-start.3 = (bf16[192,4,1792]{2,1,0:T(4,128)(2,1)}, bf16[192,4,1792]{2,1,0:T(4,128)(2,1)}, u32[]{:S(2)}, u32[]{:S(2)}) collective-permute-start(bf16[192,4,1792]{2,1,0:T(4,128)(2,1)} %reshape.141), channel_id=1, source_target_pairs={{0,4},{4,0},{1,5},{5,1},{2,6},{6,2},{3,7},{7,3},{8,12},{12,8},{9,1... | collective-permute-start | bytes 8257544 | tf_op jit(solution)/shard_map/ppermute | solution.py:77
  123.0 2.8 copy-start.6
  123.0 2.8 copy-start.8
  143.9 8.9 %copy-start.3 = (bf16[24,8,4,1536]{3,1,2,0:T(8,128)(2,1)}, bf16[24,8,4,1536]{3,1,2,0:T(8,128)(2,1)S(1)}, u32[]{:S(2)}) copy-start(bf16[24,8,4,1536]{3,1,2,0:T(8,128)(2,1)S(1)} %copy.50) | copy-start | bytes 7077892
  155.0 2.8 copy-start.7
  155.0 3.0 copy-start.13
  166.2 73.6 %all-gather.11.cloned.1.call-start = ((), (), s32[]{:S(2)}) async-start(), calls=%async_computation.2 | async-start | bytes 1966080 | tf_op jit(solution)/shard_map/all_gather | solution.py:146
  166.5 8.4 %copy-start.4 = (bf16[24,8,4,1536]{3,1,2,0:T(8,128)(2,1)S(1)}, bf16[24,8,4,1536]{3,1,2,0:T(8,128)(2,1)}, u32[]{:S(2)}) copy-start(bf16[24,8,4,1536]{3,1,2,0:T(8,128)(2,1)} %copy-done.3) | copy-start | bytes 7077892
  166.5 8.4 %copy-start.12 = (f32[192,1024]{1,0:T(8,128)S(1)}, f32[192,1024]{1,0:T(8,128)}, u32[]{:S(2)}) copy-start(f32[192,1024]{1,0:T(8,128)} %fusion.18) | copy-start | bytes 2359300
  202.4 101.2 %all-gather.13.cloned.1.call-start = ((), (), s32[]{:S(2)}) async-start(), calls=%async_computation.3 | async-start | bytes 3932160 | tf_op jit(solution)/shard_map/all_gather | solution.py:153
  202.4 6.9 %copy-start.5 = (bf16[24,8,4,1536]{3,1,2,0:T(8,128)(2,1)S(1)}, bf16[24,8,4,1536]{3,1,2,0:T(8,128)(2,1)}, u32[]{:S(2)}) copy-start(bf16[24,8,4,1536]{3,1,2,0:T(8,128)(2,1)} %copy-done.3) | copy-start | bytes 7077892
  303.6 9.1 %copy-start.10 = (bf16[192,4096]{1,0:T(8,128)(2,1)S(1)}, bf16[192,4096]{1,0:T(8,128)(2,1)}, u32[]{:S(2)}) copy-start(bf16[192,4096]{1,0:T(8,128)(2,1)} %all-gather.9.cloned.1.call-done) | copy-start | bytes 4718596
  312.6 6.2 %copy-start.11 = (bf16[192,4096]{1,0:T(8,128)(2,1)S(1)}, bf16[192,4096]{1,0:T(8,128)(2,1)}, u32[]{:S(2)}) copy-start(bf16[192,4096]{1,0:T(8,128)(2,1)} %all-gather.11.cloned.1.call-done) | copy-start | bytes 4718596
  325.1 1.4 copy-start.2
  326.6 2.9 collective-permute-start.4
  329.5 18.4 %copy-start.1 = (bf16[8,2,64,1024]{3,2,1,0:T(8,128)(2,1)S(1)}, bf16[8,2,64,1024]{3,2,1,0:T(8,128)(2,1)}, u32[]{:S(2)}) copy-start(bf16[8,2,64,1024]{3,2,1,0:T(8,128)(2,1)} %param.21) | copy-start | bytes 6291460
  331.6 15.4 %collective-permute-start.5 = (f32[96,1536]{1,0:T(8,128)S(1)}, f32[96,1536]{1,0:T(8,128)S(1)}, u32[]{:S(2)}, u32[]{:S(2)}) collective-permute-start(f32[96,1536]{1,0:T(8,128)S(1)} %select_bitcast_fusion.1), channel_id=1, source_target_pairs={{0,8},{8,0},{1,9},{9,1},{2,10},{10,2},{3,11},{11,3},{4,12},{12,4},... | collective-permute-start | bytes 1769480 | tf_op jit(solution)/shard_map/ppermute | solution.py:171
Sparse Core Ops, SparseCore 0:
  9.7 27.7 all-gather.6
  51.0 59.1 all-gather.14
  166.3 36.0 all-gather.8
  203.8 35.9 all-gather.10
  241.2 62.3 all-gather.12

commit v8 on v6

--- a/solution.py
+++ b/solution.py
@@ -69,21 +69,27 @@
     rank_lo = (partial_rank - rank_top).astype(jnp.bfloat16)
 
     half = tokens // cores
-    mine_q = jnp.concatenate([rows_q, rank_hi, rank_lo], axis=1)
-    mine_q = lax.dynamic_slice_in_dim(mine_q, core * half, half, 0)
     expert_size = lax.axis_size("expert")
-    arrived = lax.all_gather(mine_q, "expert", axis=1, tiled=False)
-    mine = arrived[:, :, :quarter].reshape(half, expert_size * quarter)
-    pieces = arrived[:, :, quarter:].astype(jnp.float32)
-    summed = jnp.sum(pieces[:, :, : window * rank] + pieces[:, :, window * rank :], axis=1)
-    mine_rank = summed.astype(jnp.bfloat16)
-    mine = jnp.concatenate([mine, mine_rank], axis=1)
-    other = lax.ppermute(mine, "wc", [(i, (i + 1) % cores) for i in range(cores)])
-    first = jnp.where(core == 0, mine, other)
-    second = jnp.where(core == 0, other, mine)
-    both = jnp.concatenate([first, second], axis=0)
-    input_rows = both[:, : expert_size * quarter]
-    lowrank = both[:, expert_size * quarter :].reshape(tile_count, tile_rows, window, rank)
+    swap = [(i, (i + 1) % cores) for i in range(cores)]
+    mine_q = lax.dynamic_slice_in_dim(rows_q, core * half, half, 0)
+    mine = lax.all_gather(mine_q, "expert", axis=1, tiled=True)
+    rank_q = lax.dynamic_slice_in_dim(
+        jnp.concatenate([rank_hi, rank_lo], axis=1), core * half, half, 0
+    )
+    rank_q, _ = lax.optimization_barrier((rank_q, mine))
+    pieces = lax.all_gather(rank_q, "expert", axis=1, tiled=False).astype(jnp.float32)
+    mine_rank = jnp.sum(pieces[:, :, : window * rank] + pieces[:, :, window * rank :], axis=1)
+    mine_rank = mine_rank.astype(jnp.bfloat16)
+    other = lax.ppermute(mine, "wc", swap)
+    other_rank = lax.ppermute(mine_rank, "wc", swap)
+    input_rows = jnp.where(
+        core == 0, jnp.concatenate([mine, other], axis=0), jnp.concatenate([other, mine], axis=0)
+    )
+    lowrank = jnp.where(
+        core == 0,
+        jnp.concatenate([mine_rank, other_rank], axis=0),
+        jnp.concatenate([other_rank, mine_rank], axis=0),
+    ).reshape(tile_count, tile_rows, window, rank)
 
     logits = jnp.dot(input_rows, router, preferred_element_type=jnp.float32)
     experts = jnp.arange(router.shape[1], dtype=jnp.int32)

time: 321 us -> 303 us (0.944)
  waiting for transfers between devices: 200 us -> 174 us
  blocking collectives: 0 us -> 16.2 us
  matrix products: 61.1 us -> 76.6 us
  local copies, waits for them, and re-layouts: 23 us -> 10.4 us
  other arithmetic: 17.3 us -> 9.81 us
    all_gather x1, waiting for transfers between devices: 59.3 us -> 22.1 us  [per_device(): mine = lax.all_gather(mine_q, 'expert', axis=1, tiled=True)]
    all_gather x1, waiting for transfers between devices: 0.01 us -> 23.2 us  [per_device(): slots_q = lax.all_gather(prompts, WIDE, axis=0, tiled=True)]
    all_gather x0 -> x1, blocking collectives: none -> 16.2 us  [per_device(): lax.all_gather(rank_q, 'expert', axis=1, tiled=False).astype(jnp.float32)]
    dot_general x2, matrix products: 19.4 us -> 27.1 us  [per_device(): jnp.dot(input_rows, up_weight[expert_number], preferred_element_type=jnp....]
    all_gather x2, waiting for transfers between devices: 95.7 us -> 88.4 us  [per_device(): gathered = lax.all_gather(hidden, 'expert', axis=1, tiled=True)]
    all_gather x1 -> x0, local copies, waits for them, and re-layouts: 6.24 us -> none  [per_device(): arrived = lax.all_gather(mine_q, 'expert', axis=1, tiled=False)]
    dot_general x2, matrix products: 18.7 us -> 24.3 us  [per_device(): jnp.dot(input_rows, gate_weight[expert_number], preferred_element_type=jn...]
    unnamed x23 -> x22, local copies, waits for them, and re-layouts: 7.94 us -> 3.98 us
  transfers between devices with their start and end apart: 10 -> 11, of which waited for: 8 -> 9; matrix products, arithmetic and copies ran while one was open for 13% -> 16% of each run, Pallas kernels for 0% -> 0%
where the time goes in v8:
time: 303 us; the launch traced here: 302 us
  waiting for transfers between devices  174 us (57%)
  matrix products  76.6 us (25%)
  blocking collectives  16.2 us (5%)
  between operations  13.4 us (4%)
  local copies, waits for them, and re-layouts  10.4 us (3%)
  other arithmetic  9.81 us (3%)
    all_gather x2, waiting for transfers between devices, per_device(): gathered = lax.all_gather(hidden, 'expert', axis=1, tiled=True)  88.4 us
    dot_general x2, matrix products, per_device(): jnp.dot(input_rows, up_weight[expert_number], preferred_element_type=jnp....  27.1 us
    dot_general x2, matrix products, per_device(): jnp.dot(input_rows, gate_weight[expert_number], preferred_element_type=jn...  24.3 us
    all_gather x1, waiting for transfers between devices, per_device(): slots_q = lax.all_gather(prompts, WIDE, axis=0, tiled=True)  23.2 us
    all_gather x1, waiting for transfers between devices, per_device(): mine = lax.all_gather(mine_q, 'expert', axis=1, tiled=True)  22.1 us
    ppermute x1, waiting for transfers between devices, per_device(): from_chip = lax.ppermute(adapter_down_weight, 'wy', swap)  19.7 us
    dot_general x2, matrix products, per_device(): jnp.dot(gathered, down_weight[expert_number], preferred_element_type=jnp....  19.4 us
    all_gather x1, blocking collectives, per_device(): lax.all_gather(rank_q, 'expert', axis=1, tiled=False).astype(jnp.float32)  16.2 us
  transfers between devices with their start and end apart: 11, of which 9 were waited for; matrix products, arithmetic and copies ran while one was open for 16% of the time, Pallas kernels for 0%

profile of v8, /device:TPU:0, one launch (start us, length us, event | category | flops | bytes accessed | tf_op | source)
XLA Modules:
  0.0 302.2 jit_solution(2042875579103111808)
XLA Ops:
  6.5 0.7 all-gather.6.cloned.1.call-update
  7.3 0.7 compare_and_fusion.2
  8.1 23.2 %all-gather.6.cloned.1.call-done = bf16[4,128,1536]{2,1,0:T(8,128)(2,1)} async-done(((bf16[1,128,1536]{2,1,0:T(8,128)(2,1)}), bf16[4,128,1536]{2,1,0:T(8,128)(2,1)}) %all-gather.6.cloned.1.call-update) | async-done | bytes 1572880 | tf_op jit(solution)/shard_map/all_gather | solution.py:40
  31.3 2.0 gather_fusion
  33.4 1.2 dynamic-slice_select_fusion
  35.0 19.7 %collective-permute-done.2 = bf16[2,2,1536,64]{2,3,1,0:T(8,128)(2,1)} collective-permute-done((bf16[2,2,1536,64]{2,3,1,0:T(8,128)(2,1)}, bf16[2,2,1536,64]{2,3,1,0:T(8,128)(2,1)}, u32[]{:S(2)}, u32[]{:S(2)}) %collective-permute-start.2) | collective-permute-done | bytes 786464 | tf_op jit(solution)/shard_map/ppermute | solution.py:50
  54.7 0.6 gather_fusion.2
  55.4 1.9 collective-permute-done.3
  57.3 3.2 %pad_maximum_fusion = bf16[4,2,2,1536,64]{3,4,2,1,0:T(8,128)(2,1)} fusion(bf16[1,2,2,1536,64]{3,4,2,1,0:T(8,128)(2,1)} %bitcast.9, bf16[1,2,2,1536,64]{3,4,2,1,0:T(8,128)(2,1)} %bitcast.8, bf16[1,2,2,1536,64]{3,4,2,1,0:T(8,128)(2,1)} %bitcast.7, bf16[1,2,2,1536,64]{3,4,2,1,0:T(8,128)(2,1)} %bitcast.114), kind=kLoop, calls=%fused_computation.23 | loop fusion | flops 4718592 | bytes 6291456 | tf_op jit(solution)/shard_map/stack | solution.py:53
  60.5 2.5 gather_fusion.3
  63.1 22.1 %all-gather.8.cloned.1.call-done = bf16[192,6144]{1,0:T(8,128)(2,1)} async-done(((bf16[192,1536]{1,0:T(8,128)(2,1)}), bf16[192,6144]{1,0:T(8,128)(2,1)}) %all-gather.8.cloned.1.call-update) | async-done | bytes 2359312 | tf_op jit(solution)/shard_map/all_gather | solution.py:75
  85.3 1.8 fusion.33
  87.6 16.2 %all-gather = bf16[192,1024]{0,1:T(8,128)(2,1)S(1)} all-gather(bf16[192,256]{0,1:T(8,128)(2,1)S(1)} %fusion.43), channel_id=2, replica_groups=mesh['groups'=2,'wy'=2,'wc'=2,'expert'=4] {'expert'}, dimensions={1}, use_global_device_ids=true | all-gather | bytes 491520 | tf_op jit(solution)/shard_map/all_gather | solution.py:80
  104.0 0.6 gather_fusion.1
  105.4 0.6 convolution_bitcast_fusion
  106.3 2.5 copy-done.9
  108.8 3.3 %fusion.52 = f32[384,8]{0,1:T(8,128)S(1)} fusion(bf16[6144,8]{0,1:T(8,128)(2,1)S(1)} %copy-done.10, bf16[192,6144]{1,0:T(8,128)(2,1)} %collective-permute-done, bf16[192,6144]{1,0:T(8,128)(2,1)S(1)} %copy-done.9, pred[]{:T(512)S(6)} %eq.13), kind=kOutput, calls=%fused_computation.93 | convolution fusion | flops 58982400 | bytes 4829185 | tf_op jit(solution)/shard_map/dot_general | solution.py:94
  112.2 11.1 %fusion.4 = f32[384,1024]{1,0:T(8,128)S(1)} fusion(bf16[2,6144,1024]{2,1,0:T(8,128)(2,1)} %param.17, bf16[192,6144]{1,0:T(8,128)(2,1)} %collective-permute-done, bf16[192,6144]{1,0:T(8,128)(2,1)S(1)} %copy-done.9, pred[]{:T(512)S(6)} %eq.13), kind=kOutput, calls=%fused_computation.8 | convolution fusion | flops 4853071872 | bytes 18874368 | tf_op jit(solution)/shard_map/dot_general | solution.py:111
  123.3 13.5 %fusion.24 = bf16[384,1024]{1,0:T(8,128)(2,1)} fusion(f32[384,2,1024]{2,0,1:T(8,128)S(1)} %bitcast.109, f32[384,1024]{1,0:T(8,128)S(1)} %fusion.4, bf16[2,6144,1024]{2,1,0:T(8,128)(2,1)} %param.18, f32[384]{0:T(512)S(1)} %get-tuple-element.8, bf16[192,6144]{1,0:T(8,128)(2,1)} %collective-permute-done, bf16[192,6144]{1,0:T(8,128)(2,1)} %all-gather.8.cloned.1.call-done, ...), kind=kOutput, calls=%fused_computation.30 | convolution fusion | flops 4856610816 | bytes 21235200 | tf_op jit(solution)/shard_map/dot_general | solution.py:115
  137.1 13.2 %fusion.10 = f32[384,1024]{1,0:T(8,128)S(1)} fusion(bf16[2,6144,1024]{2,1,0:T(8,128)(2,1)} %param.17, bf16[192,6144]{1,0:T(8,128)(2,1)} %collective-permute-done, bf16[192,6144]{1,0:T(8,128)(2,1)} %all-gather.8.cloned.1.call-done, pred[]{:T(512)S(6)} %eq.13), kind=kOutput, calls=%fused_computation.14 | convolution fusion | flops 4853071872 | bytes 18874368 | tf_op jit(solution)/shard_map/dot_general | solution.py:111
  150.3 13.6 %fusion.28 = bf16[384,1024]{1,0:T(8,128)(2,1)} fusion(f32[384,2,1024]{2,0,1:T(8,128)S(1)} %bitcast.110, f32[384,1024]{1,0:T(8,128)S(1)} %fusion.10, bf16[2,6144,1024]{2,1,0:T(8,128)(2,1)} %param.18, f32[384]{0:T(512)S(1)} %get-tuple-element.7, bf16[192,6144]{1,0:T(8,128)(2,1)} %collective-permute-done, bf16[192,6144]{1,0:T(8,128)(2,1)} %all-gather.8.cloned.1.call-done, ...), kind=kOutput, calls=%fused_computation.35 | convolution fusion | flops 4856610816 | bytes 21235200 | tf_op jit(solution)/shard_map/dot_general | solution.py:115
  164.0 34.9 %all-gather.12.cloned.1.call-done = bf16[384,4096]{1,0:T(8,128)(2,1)} async-done(((bf16[384,1024]{1,0:T(8,128)(2,1)}), bf16[384,4096]{1,0:T(8,128)(2,1)}) %all-gather.12.cloned.1.call-update) | async-done | bytes 3145744 | tf_op jit(solution)/shard_map/all_gather | solution.py:121
  198.9 10.1 %fusion = f32[384,1536]{1,0:T(8,128)} fusion(bf16[384,4096]{1,0:T(8,128)(2,1)} %all-gather.12.cloned.1.call-done, bf16[2,4096,1536]{2,1,0:T(8,128)(2,1)} %param.19), kind=kOutput, calls=%fused_computation.4 | convolution fusion | flops 4831838208 | bytes 18087936 | tf_op jit(solution)/shard_map/dot_general | solution.py:122
  209.0 53.5 %all-gather.10.cloned.1.call-done = bf16[384,4096]{1,0:T(8,128)(2,1)} async-done(((bf16[384,1024]{1,0:T(8,128)(2,1)}), bf16[384,4096]{1,0:T(8,128)(2,1)}) %all-gather.10.cloned.1.call-update) | async-done | bytes 3145744 | tf_op jit(solution)/shard_map/all_gather | solution.py:121
  262.5 9.3 %fusion.18 = f32[384,1536]{1,0:T(8,128)S(1)} fusion(f32[384,1536]{1,0:T(8,128)} %fusion, bf16[384,4096]{1,0:T(8,128)(2,1)} %all-gather.10.cloned.1.call-done, bf16[2,4096,1536]{2,1,0:T(8,128)(2,1)} %param.19), kind=kOutput, calls=%fused_computation.24 | convolution fusion | flops 4832428032 | bytes 20447232 | tf_op jit(solution)/shard_map/dot_general | solution.py:122
  271.8 1.4 copy-done.3
  273.2 1.2 select_bitcast_fusion
  274.4 3.1 %collective-permute-done.5 = f32[2,96,1536]{2,1,0:T(8,128)S(1)} collective-permute-done((f32[2,96,1536]{2,1,0:T(8,128)}, f32[2,96,1536]{2,1,0:T(8,128)S(1)}, u32[]{:S(2)}, u32[]{:S(2)}) %collective-permute-start.5) | collective-permute-done | bytes 1179680 | tf_op jit(solution)/shard_map/ppermute | solution.py:133
  277.4 1.9 bitcast_add_fusion
  279.4 1.5 collective-permute-start.6
  280.9 13.9 %collective-permute-done.6 = f32[96,1536]{1,0:T(8,128)S(1)} collective-permute-done((f32[96,1536]{1,0:T(8,128)S(1)}, f32[96,1536]{1,0:T(8,128)S(1)}, u32[]{:S(2)}, u32[]{:S(2)}) %collective-permute-start.6) | collective-permute-done | bytes 589856 | tf_op jit(solution)/shard_map/ppermute | solution.py:138
  294.8 0.8 fusion.38
  (58 shorter events, 2.9 us)
Async XLA Ops:
  6.5 97.5 %copy-start = (bf16[8,2,64,1024]{3,2,1,0:T(8,128)(2,1)S(1)}, bf16[8,2,64,1024]{3,2,1,0:T(8,128)(2,1)}, u32[]{:S(2)}) copy-start(bf16[8,2,64,1024]{3,2,1,0:T(8,128)(2,1)} %param.21) | copy-start | bytes 6291460
  6.5 48.1 %copy-start.8 = (s32[3]{0:T(128)S(1)}, s32[3]{0:T(128)}, u32[]{:S(2)}) copy-start(s32[3]{0:T(128)} %param.14) | copy-start | bytes 40
  6.5 48.2 %copy-start.2 = (s32[8]{0:T(128)S(1)}, s32[8]{0:T(128)}, u32[]{:S(2)}) copy-start(s32[8]{0:T(128)} %param.15) | copy-start | bytes 100
  6.5 24.8 %all-gather.6.cloned.1.call-start = ((), (), s32[]{:S(2)}) async-start(), calls=%async_computation | async-start | bytes 1966080 | tf_op jit(solution)/shard_map/all_gather | solution.py:40
  7.3 77.9 %all-gather.8.cloned.1.call-start = ((), (), s32[]{:S(2)}) async-start(), calls=%async_computation.1 | async-start | bytes 2949120 | tf_op jit(solution)/shard_map/all_gather | solution.py:75
  33.4 27.2 %copy-start.6 = (bf16[3,128,1536]{2,1,0:T(8,128)(2,1)}, bf16[3,128,1536]{2,1,0:T(8,128)(2,1)S(1)}, u32[]{:S(2)}) copy-start(bf16[3,128,1536]{2,1,0:T(8,128)(2,1)S(1)} %gather_fusion) | copy-start | bytes 3538948
  34.6 164.3 %all-gather.12.cloned.1.call-start = ((), (), s32[]{:S(2)}) async-start(), calls=%async_computation.3 | async-start | bytes 3932160 | tf_op jit(solution)/shard_map/all_gather | solution.py:121
  34.6 20.1 %collective-permute-start.2 = (bf16[2,2,1536,64]{2,3,1,0:T(8,128)(2,1)}, bf16[2,2,1536,64]{2,3,1,0:T(8,128)(2,1)}, u32[]{:S(2)}, u32[]{:S(2)}) collective-permute-start(bf16[2,2,1536,64]{2,3,1,0:T(8,128)(2,1)} %param.20), channel_id=1, source_target_pairs={{0,8},{8,0},{1,9},{9,1},{2,10},{10,2},{3,11},{11,3},{4,12},{12,4},... | collective-permute-start | bytes 2359304 | tf_op jit(solution)/shard_map/ppermute | solution.py:50
  35.0 20.4 %collective-permute-start.1 = (bf16[2,2,1536,64]{2,3,1,0:T(8,128)(2,1)}, bf16[2,2,1536,64]{2,3,1,0:T(8,128)(2,1)}, u32[]{:S(2)}, u32[]{:S(2)}) collective-permute-start(bf16[2,2,1536,64]{2,3,1,0:T(8,128)(2,1)} %param.20), channel_id=1, source_target_pairs={{0,4},{4,0},{1,5},{5,1},{2,6},{6,2},{3,7},{7,3},{8,12},{12,8},{9,1... | collective-permute-start | bytes 2359304 | tf_op jit(solution)/shard_map/ppermute | solution.py:51
  54.7 2.6 collective-permute-start.3
  85.2 21.1 %collective-permute-start = (bf16[192,6144]{1,0:T(8,128)(2,1)}, bf16[192,6144]{1,0:T(8,128)(2,1)}, u32[]{:S(2)}, u32[]{:S(2)}) collective-permute-start(bf16[192,6144]{1,0:T(8,128)(2,1)} %all-gather.8.cloned.1.call-done), channel_id=1, source_target_pairs={{0,4},{4,0},{1,5},{5,1},{2,6},{6,2},{3,7},{7,3},{8,12},{12,8},{9,1... | collective-permute-start | bytes 7077896 | tf_op jit(solution)/shard_map/ppermute | solution.py:83
  87.2 16.8 %copy-start.7 = (s32[384,2]{0,1:T(2,128)S(1)}, s32[384,2]{0,1:T(2,128)}, u32[]{:S(2)}) copy-start(s32[384,2]{0,1:T(2,128)} %param.13) | copy-start | bytes 9220
  103.9 1.3 collective-permute-start.4
  106.0 2.8 copy-start.9
  106.0 2.8 copy-start.10
  106.3 17.0 %copy-start.4 = (f32[3,128,2,1024]{3,1,0,2:T(8,128)}, f32[3,128,2,1024]{3,1,0,2:T(8,128)S(1)}, u32[]{:S(2)}) copy-start(f32[3,128,2,1024]{3,1,0,2:T(8,128)S(1)} %copy.25) | copy-start | bytes 9437188
  136.9 125.6 %all-gather.10.cloned.1.call-start = ((), (), s32[]{:S(2)}) async-start(), calls=%async_computation.2 | async-start | bytes 3932160 | tf_op jit(solution)/shard_map/all_gather | solution.py:121
  137.1 13.2 %copy-start.5 = (f32[3,128,2,1024]{3,1,0,2:T(8,128)S(1)}, f32[3,128,2,1024]{3,1,0,2:T(8,128)}, u32[]{:S(2)}) copy-start(f32[3,128,2,1024]{3,1,0,2:T(8,128)} %copy-done.4) | copy-start | bytes 9437188
  271.8 1.4 copy-start.3
  274.4 3.1 %collective-permute-start.5 = (f32[2,96,1536]{2,1,0:T(8,128)}, f32[2,96,1536]{2,1,0:T(8,128)S(1)}, u32[]{:S(2)}, u32[]{:S(2)}) collective-permute-start(f32[2,96,1536]{2,1,0:T(8,128)} %select_bitcast_fusion), channel_id=1, source_target_pairs={{0,4},{4,0},{1,5},{5,1},{2,6},{6,2},{3,7},{7,3},{8,12},{12,8},{9,1... | collective-permute-start | bytes 3538952 | tf_op jit(solution)/shard_map/ppermute | solution.py:133
  274.4 21.3 %copy-start.1 = (bf16[8,2,64,1024]{3,2,1,0:T(8,128)(2,1)S(1)}, bf16[8,2,64,1024]{3,2,1,0:T(8,128)(2,1)}, u32[]{:S(2)}) copy-start(bf16[8,2,64,1024]{3,2,1,0:T(8,128)(2,1)} %param.21) | copy-start | bytes 6291460
  279.4 15.4 %collective-permute-start.6 = (f32[96,1536]{1,0:T(8,128)S(1)}, f32[96,1536]{1,0:T(8,128)S(1)}, u32[]{:S(2)}, u32[]{:S(2)}) collective-permute-start(f32[96,1536]{1,0:T(8,128)S(1)} %select_bitcast_fusion.1), channel_id=1, source_target_pairs={{0,8},{8,0},{1,9},{9,1},{2,10},{10,2},{3,11},{11,3},{4,12},{12,4},... | collective-permute-start | bytes 1769480 | tf_op jit(solution)/shard_map/ppermute | solution.py:138
Sparse Core Ops, SparseCore 0:
  8.9 22.3 all-gather.5
  34.7 50.4 all-gather.7
  137.0 61.8 all-gather.11
  200.3 62.1 all-gather.9

commit v9 on v8

--- a/solution.py
+++ b/solution.py
@@ -77,8 +77,15 @@
         jnp.concatenate([rank_hi, rank_lo], axis=1), core * half, half, 0
     )
     rank_q, _ = lax.optimization_barrier((rank_q, mine))
-    pieces = lax.all_gather(rank_q, "expert", axis=1, tiled=False).astype(jnp.float32)
-    mine_rank = jnp.sum(pieces[:, :, : window * rank] + pieces[:, :, window * rank :], axis=1)
+    arrivals = [rank_q] + [
+        lax.ppermute(rank_q, "expert", [(i, (i + shift) % expert_size) for i in range(expert_size)])
+        for shift in range(1, expert_size)
+    ]
+    mine_rank = None
+    for piece in arrivals:
+        piece = piece.astype(jnp.float32)
+        piece = piece[:, : window * rank] + piece[:, window * rank :]
+        mine_rank = piece if mine_rank is None else mine_rank + piece
     mine_rank = mine_rank.astype(jnp.bfloat16)
     other = lax.ppermute(mine, "wc", swap)
     other_rank = lax.ppermute(mine_rank, "wc", swap)

time: 303 us -> 308 us (1.017)
  waiting for transfers between devices: 174 us -> 192 us
  blocking collectives: 16.2 us -> 0 us
  starting transfers between devices: 2.3 us -> 5.69 us
    all_gather x1 -> x0, blocking collectives: 16.2 us -> none  [per_device(): lax.all_gather(rank_q, 'expert', axis=1, tiled=False).astype(jnp.float32)]
    ppermute x0 -> x3, waiting for transfers between devices: none -> 10.5 us  [per_device(): lax.ppermute(rank_q, 'expert', [(i, (i + shift) % expert_size) for i in r...]
    all_gather x1, waiting for transfers between devices: 22.1 us -> 29.8 us  [per_device(): mine = lax.all_gather(mine_q, 'expert', axis=1, tiled=True)]
    ppermute x0 -> x3, starting transfers between devices: none -> 3.34 us  [per_device(): lax.ppermute(rank_q, 'expert', [(i, (i + shift) % expert_size) for i in r...]
  transfers between devices with their start and end apart: 11 -> 14, of which waited for: 9 -> 10; matrix products, arithmetic and copies ran while one was open for 16% -> 16% of each run, Pallas kernels for 0% -> 0%
where the time goes in v9:
time: 308 us; the launch traced here: 307 us
  waiting for transfers between devices  192 us (62%)
  matrix products  76.1 us (25%)
  between operations  13.5 us (4%)
  local copies, waits for them, and re-layouts  10.3 us (3%)
  other arithmetic  9.88 us (3%)
  starting transfers between devices  5.69 us (2%)
    all_gather x2, waiting for transfers between devices, per_device(): gathered = lax.all_gather(hidden, 'expert', axis=1, tiled=True)  90.5 us
    all_gather x1, waiting for transfers between devices, per_device(): mine = lax.all_gather(mine_q, 'expert', axis=1, tiled=True)  29.8 us
    dot_general x2, matrix products, per_device(): jnp.dot(input_rows, up_weight[expert_number], preferred_element_type=jnp....  27.3 us
    dot_general x2, matrix products, per_device(): jnp.dot(input_rows, gate_weight[expert_number], preferred_element_type=jn...  23.9 us
    all_gather x1, waiting for transfers between devices, per_device(): slots_q = lax.all_gather(prompts, WIDE, axis=0, tiled=True)  23.2 us
    ppermute x1, waiting for transfers between devices, per_device(): from_chip = lax.ppermute(adapter_down_weight, 'wy', swap)  19.7 us
    dot_general x2, matrix products, per_device(): jnp.dot(gathered, down_weight[expert_number], preferred_element_type=jnp....  19.3 us
    ppermute x1, waiting for transfers between devices, reduce_rows(): return mine + lax.ppermute(away, 'wy', [(0, 1), (1, 0)])  13.9 us
  transfers between devices with their start and end apart: 14, of which 10 were waited for; matrix products, arithmetic and copies ran while one was open for 16% of the time, Pallas kernels for 0%

profile of v9, /device:TPU:0, one launch (start us, length us, event | category | flops | bytes accessed | tf_op | source)
XLA Modules:
  0.0 307.4 jit_solution(1044081617725553556)
XLA Ops:
  6.5 0.7 all-gather.5.cloned.1.call-update
  7.3 0.7 compare_and_fusion.2
  8.1 23.2 %all-gather.5.cloned.1.call-done = bf16[4,128,1536]{2,1,0:T(8,128)(2,1)} async-done(((bf16[1,128,1536]{2,1,0:T(8,128)(2,1)}), bf16[4,128,1536]{2,1,0:T(8,128)(2,1)}) %all-gather.5.cloned.1.call-update) | async-done | bytes 1572880 | tf_op jit(solution)/shard_map/all_gather | solution.py:40
  31.3 2.0 gather_fusion
  33.4 1.2 dynamic-slice_select_fusion
  35.0 19.7 %collective-permute-done.2 = bf16[2,2,1536,64]{2,3,1,0:T(8,128)(2,1)} collective-permute-done((bf16[2,2,1536,64]{2,3,1,0:T(8,128)(2,1)}, bf16[2,2,1536,64]{2,3,1,0:T(8,128)(2,1)}, u32[]{:S(2)}, u32[]{:S(2)}) %collective-permute-start.2) | collective-permute-done | bytes 786464 | tf_op jit(solution)/shard_map/ppermute | solution.py:50
  54.8 0.6 gather_fusion.2
  55.4 29.8 %all-gather.7.cloned.1.call-done = bf16[192,6144]{1,0:T(8,128)(2,1)} async-done(((bf16[192,1536]{1,0:T(8,128)(2,1)}), bf16[192,6144]{1,0:T(8,128)(2,1)}) %all-gather.7.cloned.1.call-update) | async-done | bytes 2359312 | tf_op jit(solution)/shard_map/all_gather | solution.py:75
  85.2 3.3 %pad_maximum_fusion = bf16[4,2,2,1536,64]{3,4,2,1,0:T(8,128)(2,1)} fusion(bf16[1,2,2,1536,64]{3,4,2,1,0:T(8,128)(2,1)} %bitcast.9, bf16[1,2,2,1536,64]{3,4,2,1,0:T(8,128)(2,1)} %bitcast.8, bf16[1,2,2,1536,64]{3,4,2,1,0:T(8,128)(2,1)} %bitcast.7, bf16[1,2,2,1536,64]{3,4,2,1,0:T(8,128)(2,1)} %bitcast.111), kind=kLoop, calls=%fused_computation.23 | loop fusion | flops 4718592 | bytes 6291456 | tf_op jit(solution)/shard_map/stack | solution.py:53
  88.5 2.5 gather_fusion.3
  91.2 1.8 fusion.33
  93.4 1.0 collective-permute-start.6
  94.8 1.9 collective-permute-start.4
  96.8 3.9 %collective-permute-done.6 = bf16[192,256]{0,1:T(8,128)(2,1)S(1)} collective-permute-done((bf16[192,256]{0,1:T(8,128)(2,1)S(1)}, bf16[192,256]{0,1:T(8,128)(2,1)S(1)}, u32[]{:S(2)}, u32[]{:S(2)}) %collective-permute-start.6) | collective-permute-done | bytes 98336 | tf_op jit(solution)/shard_map/ppermute | solution.py:81
  100.7 6.7 %collective-permute-done.5 = bf16[192,256]{0,1:T(8,128)(2,1)S(1)} collective-permute-done((bf16[192,256]{0,1:T(8,128)(2,1)S(1)}, bf16[192,256]{0,1:T(8,128)(2,1)S(1)}, u32[]{:S(2)}, u32[]{:S(2)}) %collective-permute-start.5) | collective-permute-done | bytes 98336 | tf_op jit(solution)/shard_map/ppermute | solution.py:81
  109.9 2.5 copy-done.9
  112.4 3.2 %fusion.55 = f32[384,8]{0,1:T(8,128)S(1)} fusion(bf16[6144,8]{0,1:T(8,128)(2,1)S(1)} %copy-done.10, bf16[192,6144]{1,0:T(8,128)(2,1)} %collective-permute-done, bf16[192,6144]{1,0:T(8,128)(2,1)S(1)} %copy-done.9, pred[]{:T(512)S(6)} %eq.13), kind=kOutput, calls=%fused_computation.98 | convolution fusion | flops 58982400 | bytes 4829185 | tf_op jit(solution)/shard_map/dot_general | solution.py:101
  115.6 11.1 %fusion.4 = f32[384,1024]{1,0:T(8,128)S(1)} fusion(bf16[2,6144,1024]{2,1,0:T(8,128)(2,1)} %param.17, bf16[192,6144]{1,0:T(8,128)(2,1)} %collective-permute-done, bf16[192,6144]{1,0:T(8,128)(2,1)S(1)} %copy-done.9, pred[]{:T(512)S(6)} %eq.13), kind=kOutput, calls=%fused_computation.8 | convolution fusion | flops 4853071872 | bytes 18874368 | tf_op jit(solution)/shard_map/dot_general | solution.py:118
  126.8 13.6 %fusion.24 = bf16[384,1024]{1,0:T(8,128)(2,1)} fusion(f32[384,2,1024]{2,0,1:T(8,128)S(1)} %bitcast.106, f32[384,1024]{1,0:T(8,128)S(1)} %fusion.4, bf16[2,6144,1024]{2,1,0:T(8,128)(2,1)} %param.18, f32[384]{0:T(512)S(1)} %get-tuple-element.8, bf16[192,6144]{1,0:T(8,128)(2,1)} %collective-permute-done, bf16[192,6144]{1,0:T(8,128)(2,1)} %all-gather.7.cloned.1.call-done, ...), kind=kOutput, calls=%fused_computation.30 | convolution fusion | flops 4856610816 | bytes 21235200 | tf_op jit(solution)/shard_map/dot_general | solution.py:122
  140.6 12.8 %fusion.10 = f32[384,1024]{1,0:T(8,128)S(1)} fusion(bf16[2,6144,1024]{2,1,0:T(8,128)(2,1)} %param.17, bf16[192,6144]{1,0:T(8,128)(2,1)} %collective-permute-done, bf16[192,6144]{1,0:T(8,128)(2,1)} %all-gather.7.cloned.1.call-done, pred[]{:T(512)S(6)} %eq.13), kind=kOutput, calls=%fused_computation.14 | convolution fusion | flops 4853071872 | bytes 18874368 | tf_op jit(solution)/shard_map/dot_general | solution.py:118
  153.5 13.7 %fusion.28 = bf16[384,1024]{1,0:T(8,128)(2,1)} fusion(f32[384,2,1024]{2,0,1:T(8,128)S(1)} %bitcast.107, f32[384,1024]{1,0:T(8,128)S(1)} %fusion.10, bf16[2,6144,1024]{2,1,0:T(8,128)(2,1)} %param.18, f32[384]{0:T(512)S(1)} %get-tuple-element.7, bf16[192,6144]{1,0:T(8,128)(2,1)} %collective-permute-done, bf16[192,6144]{1,0:T(8,128)(2,1)} %all-gather.7.cloned.1.call-done, ...), kind=kOutput, calls=%fused_computation.35 | convolution fusion | flops 4856610816 | bytes 21235200 | tf_op jit(solution)/shard_map/dot_general | solution.py:122
  167.2 36.9 %all-gather.11.cloned.1.call-done = bf16[384,4096]{1,0:T(8,128)(2,1)} async-done(((bf16[384,1024]{1,0:T(8,128)(2,1)}), bf16[384,4096]{1,0:T(8,128)(2,1)}) %all-gather.11.cloned.1.call-update) | async-done | bytes 3145744 | tf_op jit(solution)/shard_map/all_gather | solution.py:128
  204.1 10.0 %fusion = f32[384,1536]{1,0:T(8,128)} fusion(bf16[384,4096]{1,0:T(8,128)(2,1)} %all-gather.11.cloned.1.call-done, bf16[2,4096,1536]{2,1,0:T(8,128)(2,1)} %param.19), kind=kOutput, calls=%fused_computation.4 | convolution fusion | flops 4831838208 | bytes 18087936 | tf_op jit(solution)/shard_map/dot_general | solution.py:129
  214.0 53.6 %all-gather.9.cloned.1.call-done = bf16[384,4096]{1,0:T(8,128)(2,1)} async-done(((bf16[384,1024]{1,0:T(8,128)(2,1)}), bf16[384,4096]{1,0:T(8,128)(2,1)}) %all-gather.9.cloned.1.call-update) | async-done | bytes 3145744 | tf_op jit(solution)/shard_map/all_gather | solution.py:128
  267.7 9.3 %fusion.18 = f32[384,1536]{1,0:T(8,128)S(1)} fusion(f32[384,1536]{1,0:T(8,128)} %fusion, bf16[384,4096]{1,0:T(8,128)(2,1)} %all-gather.9.cloned.1.call-done, bf16[2,4096,1536]{2,1,0:T(8,128)(2,1)} %param.19), kind=kOutput, calls=%fused_computation.24 | convolution fusion | flops 4832428032 | bytes 20447232 | tf_op jit(solution)/shard_map/dot_general | solution.py:129
  277.0 1.4 copy-done.3
  278.4 1.2 select_bitcast_fusion
  279.6 3.1 collective-permute-done.8
  282.6 1.9 bitcast_add_fusion
  284.6 1.5 collective-permute-start.9
  286.1 13.9 %collective-permute-done.9 = f32[96,1536]{1,0:T(8,128)S(1)} collective-permute-done((f32[96,1536]{1,0:T(8,128)S(1)}, f32[96,1536]{1,0:T(8,128)S(1)}, u32[]{:S(2)}, u32[]{:S(2)}) %collective-permute-start.9) | collective-permute-done | bytes 589856 | tf_op jit(solution)/shard_map/ppermute | solution.py:145
  300.0 0.8 fusion.38
  (66 shorter events, 4.5 us)
Async XLA Ops:
  6.5 101.0 %copy-start = (bf16[8,2,64,1024]{3,2,1,0:T(8,128)(2,1)S(1)}, bf16[8,2,64,1024]{3,2,1,0:T(8,128)(2,1)}, u32[]{:S(2)}) copy-start(bf16[8,2,64,1024]{3,2,1,0:T(8,128)(2,1)} %param.21) | copy-start | bytes 6291460
  6.5 48.2 %copy-start.8 = (s32[3]{0:T(128)S(1)}, s32[3]{0:T(128)}, u32[]{:S(2)}) copy-start(s32[3]{0:T(128)} %param.14) | copy-start | bytes 40
  6.5 48.2 %copy-start.2 = (s32[8]{0:T(128)S(1)}, s32[8]{0:T(128)}, u32[]{:S(2)}) copy-start(s32[8]{0:T(128)} %param.15) | copy-start | bytes 100
  6.5 24.8 %all-gather.5.cloned.1.call-start = ((), (), s32[]{:S(2)}) async-start(), calls=%async_computation | async-start | bytes 1966080 | tf_op jit(solution)/shard_map/all_gather | solution.py:40
  7.3 77.9 %all-gather.7.cloned.1.call-start = ((), (), s32[]{:S(2)}) async-start(), calls=%async_computation.1 | async-start | bytes 2949120 | tf_op jit(solution)/shard_map/all_gather | solution.py:75
  33.4 55.1 %copy-start.6 = (bf16[3,128,1536]{2,1,0:T(8,128)(2,1)}, bf16[3,128,1536]{2,1,0:T(8,128)(2,1)S(1)}, u32[]{:S(2)}) copy-start(bf16[3,128,1536]{2,1,0:T(8,128)(2,1)S(1)} %gather_fusion) | copy-start | bytes 3538948
  34.6 169.5 %all-gather.11.cloned.1.call-start = ((), (), s32[]{:S(2)}) async-start(), calls=%async_computation.3 | async-start | bytes 3932160 | tf_op jit(solution)/shard_map/all_gather | solution.py:128
  34.7 20.1 %collective-permute-start.2 = (bf16[2,2,1536,64]{2,3,1,0:T(8,128)(2,1)}, bf16[2,2,1536,64]{2,3,1,0:T(8,128)(2,1)}, u32[]{:S(2)}, u32[]{:S(2)}) collective-permute-start(bf16[2,2,1536,64]{2,3,1,0:T(8,128)(2,1)} %param.20), channel_id=1, source_target_pairs={{0,8},{8,0},{1,9},{9,1},{2,10},{10,2},{3,11},{11,3},{4,12},{12,4},... | collective-permute-start | bytes 2359304 | tf_op jit(solution)/shard_map/ppermute | solution.py:50
  35.0 50.2 %collective-permute-start.1 = (bf16[2,2,1536,64]{2,3,1,0:T(8,128)(2,1)}, bf16[2,2,1536,64]{2,3,1,0:T(8,128)(2,1)}, u32[]{:S(2)}, u32[]{:S(2)}) collective-permute-start(bf16[2,2,1536,64]{2,3,1,0:T(8,128)(2,1)} %param.20), channel_id=1, source_target_pairs={{0,4},{4,0},{1,5},{5,1},{2,6},{6,2},{3,7},{7,3},{8,12},{12,8},{9,1... | collective-permute-start | bytes 2359304 | tf_op jit(solution)/shard_map/ppermute | solution.py:51
  54.7 30.5 %collective-permute-start.3 = (bf16[2,2,1536,64]{2,3,1,0:T(8,128)(2,1)}, bf16[2,2,1536,64]{2,3,1,0:T(8,128)(2,1)}, u32[]{:S(2)}, u32[]{:S(2)}) collective-permute-start(bf16[2,2,1536,64]{2,3,1,0:T(8,128)(2,1)} %collective-permute-done.2), channel_id=1, source_target_pairs={{0,4},{4,0},{1,5},{5,1},{2,6},{6,2},{3,7},{7,3},{8,12},{12,8},{9,1... | collective-permute-start | bytes 2359304 | tf_op jit(solution)/shard_map/ppermute | solution.py:52
  85.2 24.6 %collective-permute-start = (bf16[192,6144]{1,0:T(8,128)(2,1)}, bf16[192,6144]{1,0:T(8,128)(2,1)}, u32[]{:S(2)}, u32[]{:S(2)}) collective-permute-start(bf16[192,6144]{1,0:T(8,128)(2,1)} %all-gather.7.cloned.1.call-done), channel_id=1, source_target_pairs={{0,4},{4,0},{1,5},{5,1},{2,6},{6,2},{3,7},{7,3},{8,12},{12,8},{9,1... | collective-permute-start | bytes 7077896 | tf_op jit(solution)/shard_map/ppermute | solution.py:90
  91.2 16.4 %copy-start.7 = (s32[384,2]{0,1:T(2,128)S(1)}, s32[384,2]{0,1:T(2,128)}, u32[]{:S(2)}) copy-start(s32[384,2]{0,1:T(2,128)} %param.13) | copy-start | bytes 9220
  93.4 7.2 %collective-permute-start.6 = (bf16[192,256]{0,1:T(8,128)(2,1)S(1)}, bf16[192,256]{0,1:T(8,128)(2,1)S(1)}, u32[]{:S(2)}, u32[]{:S(2)}) collective-permute-start(bf16[192,256]{0,1:T(8,128)(2,1)S(1)} %fusion.42), channel_id=1, source_target_pairs={{0,3},{1,0},{2,1},{3,2},{4,7},{5,4},{6,5},{7,6},{8,11},{9,8},{10,9... | collective-permute-start | bytes 294920 | tf_op jit(solution)/shard_map/ppermute | solution.py:81
  94.4 12.9 %collective-permute-start.5 = (bf16[192,256]{0,1:T(8,128)(2,1)S(1)}, bf16[192,256]{0,1:T(8,128)(2,1)S(1)}, u32[]{:S(2)}, u32[]{:S(2)}) collective-permute-start(bf16[192,256]{0,1:T(8,128)(2,1)S(1)} %fusion.42), channel_id=1, source_target_pairs={{0,2},{1,3},{2,0},{3,1},{4,6},{5,7},{6,4},{7,5},{8,10},{9,11},{10,... | collective-permute-start | bytes 294920 | tf_op jit(solution)/shard_map/ppermute | solution.py:81
  94.8 12.5 %collective-permute-start.4 = (bf16[192,256]{0,1:T(8,128)(2,1)S(1)}, bf16[192,256]{0,1:T(8,128)(2,1)S(1)}, u32[]{:S(2)}, u32[]{:S(2)}) collective-permute-start(bf16[192,256]{0,1:T(8,128)(2,1)S(1)} %fusion.42), channel_id=1, source_target_pairs={{0,1},{1,2},{2,3},{3,0},{4,5},{5,6},{6,7},{7,4},{8,9},{9,10},{10,1... | collective-permute-start | bytes 294920 | tf_op jit(solution)/shard_map/ppermute | solution.py:81
  107.5 1.3 collective-permute-start.7
  109.6 2.8 copy-start.9
  109.6 2.8 copy-start.10
  109.8 16.9 %copy-start.4 = (f32[3,128,2,1024]{3,1,0,2:T(8,128)}, f32[3,128,2,1024]{3,1,0,2:T(8,128)S(1)}, u32[]{:S(2)}) copy-start(f32[3,128,2,1024]{3,1,0,2:T(8,128)S(1)} %copy.25) | copy-start | bytes 9437188
  140.4 127.3 %all-gather.9.cloned.1.call-start = ((), (), s32[]{:S(2)}) async-start(), calls=%async_computation.2 | async-start | bytes 3932160 | tf_op jit(solution)/shard_map/all_gather | solution.py:128
  140.6 12.8 %copy-start.5 = (f32[3,128,2,1024]{3,1,0,2:T(8,128)S(1)}, f32[3,128,2,1024]{3,1,0,2:T(8,128)}, u32[]{:S(2)}) copy-start(f32[3,128,2,1024]{3,1,0,2:T(8,128)} %copy-done.4) | copy-start | bytes 9437188
  277.0 1.4 copy-start.3
  279.6 3.1 collective-permute-start.8
  279.6 21.3 %copy-start.1 = (bf16[8,2,64,1024]{3,2,1,0:T(8,128)(2,1)S(1)}, bf16[8,2,64,1024]{3,2,1,0:T(8,128)(2,1)}, u32[]{:S(2)}) copy-start(bf16[8,2,64,1024]{3,2,1,0:T(8,128)(2,1)} %param.21) | copy-start | bytes 6291460
  284.6 15.4 %collective-permute-start.9 = (f32[96,1536]{1,0:T(8,128)S(1)}, f32[96,1536]{1,0:T(8,128)S(1)}, u32[]{:S(2)}, u32[]{:S(2)}) collective-permute-start(f32[96,1536]{1,0:T(8,128)S(1)} %select_bitcast_fusion.1), channel_id=1, source_target_pairs={{0,8},{8,0},{1,9},{9,1},{2,10},{10,2},{3,11},{11,3},{4,12},{12,4},... | collective-permute-start | bytes 1769480 | tf_op jit(solution)/shard_map/ppermute | solution.py:145
Sparse Core Ops, SparseCore 0:
  8.9 22.3 all-gather.4
  34.7 50.4 all-gather.6
  140.5 63.5 all-gather.10
  205.5 62.1 all-gather.8

commit v10 on v8

--- a/solution.py
+++ b/solution.py
@@ -85,6 +85,7 @@
     input_rows = jnp.where(
         core == 0, jnp.concatenate([mine, other], axis=0), jnp.concatenate([other, mine], axis=0)
     )
+    input_rows = lax.optimization_barrier(input_rows)
     lowrank = jnp.where(
         core == 0,
         jnp.concatenate([mine_rank, other_rank], axis=0),

time: 303 us -> 296 us (0.977)
  matrix products: 76.6 us -> 59.1 us
  waiting for transfers between devices: 174 us -> 180 us
  other arithmetic: 9.81 us -> 13 us
    dot_general x2, matrix products: 27.1 us -> 18.1 us  [per_device(): jnp.dot(input_rows, up_weight[expert_number], preferred_element_type=jnp....]
    all_gather x2, waiting for transfers between devices: 88.4 us -> 95.1 us  [per_device(): gathered = lax.all_gather(hidden, 'expert', axis=1, tiled=True)]
    dot_general x2, matrix products: 24.3 us -> 19.2 us  [per_device(): jnp.dot(input_rows, gate_weight[expert_number], preferred_element_type=jn...]
    select_n x0 -> x1, other arithmetic: none -> 4 us  [per_device(): jnp.where(core == 0, jnp.concatenate([mine, other], axis=0), jnp.concaten...]
  transfers between devices with their start and end apart: 11 -> 11, of which waited for: 9 -> 9; matrix products, arithmetic and copies ran while one was open for 16% -> 14% of each run, Pallas kernels for 0% -> 0%
where the time goes in v10:
time: 296 us; the launch traced here: 295 us
  waiting for transfers between devices  180 us (61%)
  matrix products  59.1 us (20%)
  blocking collectives  15.9 us (5%)
  between operations  13.5 us (5%)
  other arithmetic  13 us (4%)
  local copies, waits for them, and re-layouts  11.5 us (4%)
    all_gather x2, waiting for transfers between devices, per_device(): gathered = lax.all_gather(hidden, 'expert', axis=1, tiled=True)  95.1 us
    all_gather x1, waiting for transfers between devices, per_device(): slots_q = lax.all_gather(prompts, WIDE, axis=0, tiled=True)  23.2 us
    all_gather x1, waiting for transfers between devices, per_device(): mine = lax.all_gather(mine_q, 'expert', axis=1, tiled=True)  22.1 us
    ppermute x1, waiting for transfers between devices, per_device(): from_chip = lax.ppermute(adapter_down_weight, 'wy', swap)  19.7 us
    dot_general x2, matrix products, per_device(): jnp.dot(gathered, down_weight[expert_number], preferred_element_type=jnp....  19.3 us
    dot_general x2, matrix products, per_device(): jnp.dot(input_rows, gate_weight[expert_number], preferred_element_type=jn...  19.2 us
    dot_general x2, matrix products, per_device(): jnp.dot(input_rows, up_weight[expert_number], preferred_element_type=jnp....  18.1 us
    all_gather x1, blocking collectives, per_device(): lax.all_gather(rank_q, 'expert', axis=1, tiled=False).astype(jnp.float32)  15.9 us
  transfers between devices with their start and end apart: 11, of which 9 were waited for; matrix products, arithmetic and copies ran while one was open for 14% of the time, Pallas kernels for 0%

profile of v10, /device:TPU:0, one launch (start us, length us, event | category | flops | bytes accessed | tf_op | source)
XLA Modules:
  0.0 295.3 jit_solution(13277670761311684568)
XLA Ops:
  6.5 0.7 all-gather.6.cloned.1.call-update
  7.3 0.7 compare_and_fusion.2
  8.1 23.2 %all-gather.6.cloned.1.call-done = bf16[4,128,1536]{2,1,0:T(8,128)(2,1)} async-done(((bf16[1,128,1536]{2,1,0:T(8,128)(2,1)}), bf16[4,128,1536]{2,1,0:T(8,128)(2,1)}) %all-gather.6.cloned.1.call-update) | async-done | bytes 1572880 | tf_op jit(solution)/shard_map/all_gather | solution.py:40
  31.3 2.0 gather_fusion
  33.4 1.2 dynamic-slice_select_fusion
  35.0 19.7 %collective-permute-done.2 = bf16[2,2,1536,64]{2,3,1,0:T(8,128)(2,1)} collective-permute-done((bf16[2,2,1536,64]{2,3,1,0:T(8,128)(2,1)}, bf16[2,2,1536,64]{2,3,1,0:T(8,128)(2,1)}, u32[]{:S(2)}, u32[]{:S(2)}) %collective-permute-start.2) | collective-permute-done | bytes 786464 | tf_op jit(solution)/shard_map/ppermute | solution.py:50
  54.7 0.6 gather_fusion.2
  55.4 1.9 collective-permute-done.3
  57.3 3.2 %pad_maximum_fusion = bf16[4,2,2,1536,64]{3,4,2,1,0:T(8,128)(2,1)} fusion(bf16[1,2,2,1536,64]{3,4,2,1,0:T(8,128)(2,1)} %bitcast.9, bf16[1,2,2,1536,64]{3,4,2,1,0:T(8,128)(2,1)} %bitcast.8, bf16[1,2,2,1536,64]{3,4,2,1,0:T(8,128)(2,1)} %bitcast.7, bf16[1,2,2,1536,64]{3,4,2,1,0:T(8,128)(2,1)} %bitcast.119), kind=kLoop, calls=%fused_computation.23 | loop fusion | flops 4718592 | bytes 6291456 | tf_op jit(solution)/shard_map/stack | solution.py:53
  60.6 2.5 gather_fusion.3
  63.1 22.1 %all-gather.8.cloned.1.call-done = bf16[192,6144]{1,0:T(8,128)(2,1)} async-done(((bf16[192,1536]{1,0:T(8,128)(2,1)}), bf16[192,6144]{1,0:T(8,128)(2,1)}) %all-gather.8.cloned.1.call-update) | async-done | bytes 2359312 | tf_op jit(solution)/shard_map/all_gather | solution.py:75
  85.4 1.1 copy-done.9
  87.4 15.9 %all-gather = bf16[192,1024]{0,1:T(8,128)(2,1)S(1)} all-gather(bf16[192,256]{0,1:T(8,128)(2,1)S(1)} %fusion.43), channel_id=2, replica_groups=mesh['groups'=2,'wy'=2,'wc'=2,'expert'=4] {'expert'}, dimensions={1}, use_global_device_ids=true | all-gather | bytes 491520 | tf_op jit(solution)/shard_map/all_gather | solution.py:80
  103.6 0.6 gather_fusion.1
  105.0 0.6 convolution_bitcast_fusion
  105.9 2.5 copy-done.10
  108.4 4.0 %maximum_select_fusion = bf16[384,6144]{1,0:T(8,128)(2,1)S(1)} fusion(bf16[192,6144]{1,0:T(8,128)(2,1)} %collective-permute-done, bf16[192,6144]{1,0:T(8,128)(2,1)S(1)} %copy-done.10, pred[]{:T(512)S(6)} %eq.13), kind=kLoop, calls=%fused_computation.22 | loop fusion | flops 21233664 | bytes 9437185 | tf_op jit(solution)/shard_map/jit(_where)/select_n | solution.py:85
  112.4 1.3 fusion.52
  113.8 8.1 %fusion.4 = f32[384,1024]{1,0:T(8,128)S(1)} fusion(bf16[384,6144]{1,0:T(8,128)(2,1)S(1)} %maximum_select_fusion, bf16[2,6144,1024]{2,1,0:T(8,128)(2,1)} %param.17), kind=kOutput, calls=%fused_computation.8 | convolution fusion | flops 4831838208 | bytes 18874368 | tf_op jit(solution)/shard_map/dot_general | solution.py:112
  122.0 9.0 %fusion.24 = bf16[384,1024]{1,0:T(8,128)(2,1)} fusion(f32[384,2,1024]{2,0,1:T(8,128)S(1)} %bitcast.114, f32[384,1024]{1,0:T(8,128)S(1)} %fusion.4, bf16[384,6144]{1,0:T(8,128)(2,1)S(1)} %maximum_select_fusion, bf16[2,6144,1024]{2,1,0:T(8,128)(2,1)} %param.18, f32[384]{0:T(512)S(1)} %get-tuple-element.8), kind=kOutput, calls=%fused_computation.30 | convolution fusion | flops 4835377152 | bytes 21235200 | tf_op jit(solution)/shard_map/dot_general | solution.py:116
  131.3 11.1 %fusion.10 = f32[384,1024]{1,0:T(8,128)S(1)} fusion(bf16[384,6144]{1,0:T(8,128)(2,1)} %copy-done.3, bf16[2,6144,1024]{2,1,0:T(8,128)(2,1)} %param.17), kind=kOutput, calls=%fused_computation.14 | convolution fusion | flops 4831838208 | bytes 18874368 | tf_op jit(solution)/shard_map/dot_general | solution.py:112
  142.4 9.1 %fusion.28 = bf16[384,1024]{1,0:T(8,128)(2,1)} fusion(f32[384,2,1024]{2,0,1:T(8,128)S(1)} %bitcast.115, f32[384,1024]{1,0:T(8,128)S(1)} %fusion.10, bf16[384,6144]{1,0:T(8,128)(2,1)S(1)} %copy-done.4, bf16[2,6144,1024]{2,1,0:T(8,128)(2,1)} %param.18, f32[384]{0:T(512)S(1)} %get-tuple-element.7), kind=kOutput, calls=%fused_computation.35 | convolution fusion | flops 4835377152 | bytes 21235200 | tf_op jit(solution)/shard_map/dot_general | solution.py:116
  151.5 41.5 %all-gather.12.cloned.1.call-done = bf16[384,4096]{1,0:T(8,128)(2,1)} async-done(((bf16[384,1024]{1,0:T(8,128)(2,1)}), bf16[384,4096]{1,0:T(8,128)(2,1)}) %all-gather.12.cloned.1.call-update) | async-done | bytes 3145744 | tf_op jit(solution)/shard_map/all_gather | solution.py:122
  193.0 10.0 %fusion = f32[384,1536]{1,0:T(8,128)} fusion(bf16[384,4096]{1,0:T(8,128)(2,1)} %all-gather.12.cloned.1.call-done, bf16[2,4096,1536]{2,1,0:T(8,128)(2,1)} %param.19), kind=kOutput, calls=%fused_computation.4 | convolution fusion | flops 4831838208 | bytes 18087936 | tf_op jit(solution)/shard_map/dot_general | solution.py:123
  203.1 53.6 %all-gather.10.cloned.1.call-done = bf16[384,4096]{1,0:T(8,128)(2,1)} async-done(((bf16[384,1024]{1,0:T(8,128)(2,1)}), bf16[384,4096]{1,0:T(8,128)(2,1)}) %all-gather.10.cloned.1.call-update) | async-done | bytes 3145744 | tf_op jit(solution)/shard_map/all_gather | solution.py:122
  256.6 9.3 %fusion.18 = f32[384,1536]{1,0:T(8,128)S(1)} fusion(f32[384,1536]{1,0:T(8,128)} %fusion, bf16[384,4096]{1,0:T(8,128)(2,1)} %all-gather.10.cloned.1.call-done, bf16[2,4096,1536]{2,1,0:T(8,128)(2,1)} %param.19), kind=kOutput, calls=%fused_computation.24 | convolution fusion | flops 4832428032 | bytes 20447232 | tf_op jit(solution)/shard_map/dot_general | solution.py:123
  265.9 1.4 copy-done.5
  267.6 2.8 collective-permute-done.5
  270.4 2.0 bitcast_add_fusion
  272.5 1.5 collective-permute-start.6
  274.0 13.9 %collective-permute-done.6 = f32[96,1536]{1,0:T(8,128)S(1)} collective-permute-done((f32[96,1536]{1,0:T(8,128)S(1)}, f32[96,1536]{1,0:T(8,128)S(1)}, u32[]{:S(2)}, u32[]{:S(2)}) %collective-permute-start.6) | collective-permute-done | bytes 589856 | tf_op jit(solution)/shard_map/ppermute | solution.py:139
  287.9 0.8 fusion.38
  (65 shorter events, 3.6 us)
Async XLA Ops:
  6.5 97.1 %copy-start = (bf16[8,2,64,1024]{3,2,1,0:T(8,128)(2,1)S(1)}, bf16[8,2,64,1024]{3,2,1,0:T(8,128)(2,1)}, u32[]{:S(2)}) copy-start(bf16[8,2,64,1024]{3,2,1,0:T(8,128)(2,1)} %param.21) | copy-start | bytes 6291460
  6.5 48.2 %copy-start.13 = (s32[3]{0:T(128)S(1)}, s32[3]{0:T(128)}, u32[]{:S(2)}) copy-start(s32[3]{0:T(128)} %param.14) | copy-start | bytes 40
  6.5 48.2 %copy-start.2 = (s32[8]{0:T(128)S(1)}, s32[8]{0:T(128)}, u32[]{:S(2)}) copy-start(s32[8]{0:T(128)} %param.15) | copy-start | bytes 100
  6.5 24.8 %all-gather.6.cloned.1.call-start = ((), (), s32[]{:S(2)}) async-start(), calls=%async_computation | async-start | bytes 1966080 | tf_op jit(solution)/shard_map/all_gather | solution.py:40
  7.3 77.9 %all-gather.8.cloned.1.call-start = ((), (), s32[]{:S(2)}) async-start(), calls=%async_computation.1 | async-start | bytes 2949120 | tf_op jit(solution)/shard_map/all_gather | solution.py:75
  33.4 27.2 %copy-start.8 = (bf16[3,128,1536]{2,1,0:T(8,128)(2,1)}, bf16[3,128,1536]{2,1,0:T(8,128)(2,1)S(1)}, u32[]{:S(2)}) copy-start(bf16[3,128,1536]{2,1,0:T(8,128)(2,1)S(1)} %gather_fusion) | copy-start | bytes 3538948
  34.6 158.4 %all-gather.12.cloned.1.call-start = ((), (), s32[]{:S(2)}) async-start(), calls=%async_computation.3 | async-start | bytes 3932160 | tf_op jit(solution)/shard_map/all_gather | solution.py:122
  34.6 20.1 %collective-permute-start.2 = (bf16[2,2,1536,64]{2,3,1,0:T(8,128)(2,1)}, bf16[2,2,1536,64]{2,3,1,0:T(8,128)(2,1)}, u32[]{:S(2)}, u32[]{:S(2)}) collective-permute-start(bf16[2,2,1536,64]{2,3,1,0:T(8,128)(2,1)} %param.20), channel_id=1, source_target_pairs={{0,8},{8,0},{1,9},{9,1},{2,10},{10,2},{3,11},{11,3},{4,12},{12,4},... | collective-permute-start | bytes 2359304 | tf_op jit(solution)/shard_map/ppermute | solution.py:50
  35.0 20.4 %collective-permute-start.1 = (bf16[2,2,1536,64]{2,3,1,0:T(8,128)(2,1)}, bf16[2,2,1536,64]{2,3,1,0:T(8,128)(2,1)}, u32[]{:S(2)}, u32[]{:S(2)}) collective-permute-start(bf16[2,2,1536,64]{2,3,1,0:T(8,128)(2,1)} %param.20), channel_id=1, source_target_pairs={{0,4},{4,0},{1,5},{5,1},{2,6},{6,2},{3,7},{7,3},{8,12},{12,8},{9,1... | collective-permute-start | bytes 2359304 | tf_op jit(solution)/shard_map/ppermute | solution.py:51
  54.7 2.6 collective-permute-start.3
  85.2 1.3 copy-start.9
  85.2 20.7 %collective-permute-start = (bf16[192,6144]{1,0:T(8,128)(2,1)}, bf16[192,6144]{1,0:T(8,128)(2,1)}, u32[]{:S(2)}, u32[]{:S(2)}) collective-permute-start(bf16[192,6144]{1,0:T(8,128)(2,1)} %all-gather.8.cloned.1.call-done), channel_id=1, source_target_pairs={{0,4},{4,0},{1,5},{5,1},{2,6},{6,2},{3,7},{7,3},{8,12},{12,8},{9,1... | collective-permute-start | bytes 7077896 | tf_op jit(solution)/shard_map/ppermute | solution.py:83
  87.0 16.6 %copy-start.12 = (s32[384,2]{0,1:T(2,128)S(1)}, s32[384,2]{0,1:T(2,128)}, u32[]{:S(2)}) copy-start(s32[384,2]{0,1:T(2,128)} %param.13) | copy-start | bytes 9220
  103.5 1.3 collective-permute-start.4
  105.6 2.8 copy-start.10
  105.8 16.2 %copy-start.6 = (f32[3,128,2,1024]{3,1,0,2:T(8,128)}, f32[3,128,2,1024]{3,1,0,2:T(8,128)S(1)}, u32[]{:S(2)}) copy-start(f32[3,128,2,1024]{3,1,0,2:T(8,128)S(1)} %copy.25) | copy-start | bytes 9437188
  105.8 6.6 %copy-start.11 = (bf16[6144,8]{0,1:T(8,128)(2,1)S(1)}, bf16[6144,8]{0,1:T(8,128)(2,1)}, u32[]{:S(2)}) copy-start(bf16[6144,8]{0,1:T(8,128)(2,1)} %param.16) | copy-start | bytes 294916
  112.4 9.6 %copy-start.3 = (bf16[384,6144]{1,0:T(8,128)(2,1)}, bf16[384,6144]{1,0:T(8,128)(2,1)S(1)}, u32[]{:S(2)}) copy-start(bf16[384,6144]{1,0:T(8,128)(2,1)S(1)} %maximum_select_fusion) | copy-start | bytes 14155780
  131.0 125.6 %all-gather.10.cloned.1.call-start = ((), (), s32[]{:S(2)}) async-start(), calls=%async_computation.2 | async-start | bytes 3932160 | tf_op jit(solution)/shard_map/all_gather | solution.py:122
  131.3 11.1 %copy-start.4 = (bf16[384,6144]{1,0:T(8,128)(2,1)S(1)}, bf16[384,6144]{1,0:T(8,128)(2,1)}, u32[]{:S(2)}) copy-start(bf16[384,6144]{1,0:T(8,128)(2,1)} %copy-done.3) | copy-start | bytes 14155780
  131.3 11.1 %copy-start.7 = (f32[3,128,2,1024]{3,1,0,2:T(8,128)S(1)}, f32[3,128,2,1024]{3,1,0,2:T(8,128)}, u32[]{:S(2)}) copy-start(f32[3,128,2,1024]{3,1,0,2:T(8,128)} %copy-done.6) | copy-start | bytes 9437188
  265.9 1.4 copy-start.5
  267.5 2.9 collective-permute-start.5
  270.4 18.4 %copy-start.1 = (bf16[8,2,64,1024]{3,2,1,0:T(8,128)(2,1)S(1)}, bf16[8,2,64,1024]{3,2,1,0:T(8,128)(2,1)}, u32[]{:S(2)}) copy-start(bf16[8,2,64,1024]{3,2,1,0:T(8,128)(2,1)} %param.21) | copy-start | bytes 6291460
  272.5 15.4 %collective-permute-start.6 = (f32[96,1536]{1,0:T(8,128)S(1)}, f32[96,1536]{1,0:T(8,128)S(1)}, u32[]{:S(2)}, u32[]{:S(2)}) collective-permute-start(f32[96,1536]{1,0:T(8,128)S(1)} %select_bitcast_fusion.1), channel_id=1, source_target_pairs={{0,8},{8,0},{1,9},{9,1},{2,10},{10,2},{3,11},{11,3},{4,12},{12,4},... | collective-permute-start | bytes 1769480 | tf_op jit(solution)/shard_map/ppermute | solution.py:139
Sparse Core Ops, SparseCore 0:
  8.9 22.3 all-gather.5
  34.7 50.4 all-gather.7
  131.2 61.8 all-gather.11
  194.5 62.1 all-gather.9

commit v11 on v10

--- a/solution.py
+++ b/solution.py
@@ -120,9 +120,21 @@
             weight[:, expert_number, None] * jax.nn.silu(gate_pre) * up_value
         ).astype(jnp.bfloat16)
         gathered = lax.all_gather(hidden, "expert", axis=1, tiled=True)
-        part = jnp.dot(gathered, down_weight[expert_number], preferred_element_type=jnp.float32)
-        running = part if running is None else running + part
-    return reduce_rows(running, core, cores).astype(jnp.bfloat16)
+        if expert_number < window - 1:
+            part = jnp.dot(gathered, down_weight[expert_number], preferred_element_type=jnp.float32)
+            running = part if running is None else running + part
+            continue
+        width = down_weight.shape[2] // 2
+        outs = []
+        for c in range(2):
+            cols = slice(c * width, (c + 1) * width)
+            part = jnp.dot(
+                gathered, down_weight[expert_number, :, cols], preferred_element_type=jnp.float32
+            )
+            if running is not None:
+                part = running[:, cols] + part
+            outs.append(reduce_rows(part, core, cores))
+    return jnp.concatenate(outs, axis=1).astype(jnp.bfloat16)
 
 
 def reduce_rows(running, core, cores):

time: 296 us -> 295 us (level)
  waiting for transfers between devices: 180 us -> 174 us
  matrix products: 59.1 us -> 64 us
    dot_general x0 -> x2, matrix products: none -> 12.1 us  [per_device(): jnp.dot(gathered, down_weight[expert_number, :, cols], preferred_element_...]
    dot_general x2 -> x1, matrix products: 19.3 us -> 10 us  [per_device(): jnp.dot(gathered, down_weight[expert_number], preferred_element_type=jnp....]
    ppermute x1 -> x2, waiting for transfers between devices: 13.9 us -> 10.6 us  [reduce_rows(): return mine + lax.ppermute(away, 'wy', [(0, 1), (1, 0)])]
  transfers between devices with their start and end apart: 11 -> 13, of which waited for: 9 -> 10; matrix products, arithmetic and copies ran while one was open for 14% -> 17% of each run, Pallas kernels for 0% -> 0%
where the time goes in v11:
time: 295 us
  waiting for transfers between devices  174 us (59%)
  matrix products  64 us (22%)
  blocking collectives  16.2 us (5%)
  other arithmetic  13.7 us (5%)
  between operations  13.5 us (5%)
  local copies, waits for them, and re-layouts  8.97 us (3%)
  starting transfers between devices  4.35 us (1%)
    all_gather x2, waiting for transfers between devices, per_device(): gathered = lax.all_gather(hidden, 'expert', axis=1, tiled=True)  94.8 us
    all_gather x1, waiting for transfers between devices, per_device(): slots_q = lax.all_gather(prompts, WIDE, axis=0, tiled=True)  23.2 us
    all_gather x1, waiting for transfers between devices, per_device(): mine = lax.all_gather(mine_q, 'expert', axis=1, tiled=True)  22.1 us
    ppermute x1, waiting for transfers between devices, per_device(): from_chip = lax.ppermute(adapter_down_weight, 'wy', swap)  19.7 us
    dot_general x2, matrix products, per_device(): jnp.dot(input_rows, gate_weight[expert_number], preferred_element_type=jn...  19.6 us
    dot_general x2, matrix products, per_device(): jnp.dot(input_rows, up_weight[expert_number], preferred_element_type=jnp....  18.5 us
    all_gather x1, blocking collectives, per_device(): lax.all_gather(rank_q, 'expert', axis=1, tiled=False).astype(jnp.float32)  16.2 us
    dot_general x2, matrix products, per_device(): jnp.dot(gathered, down_weight[expert_number, :, cols], preferred_element_...  12.1 us
  transfers between devices with their start and end apart: 13, of which 10 were waited for; matrix products, arithmetic and copies ran while one was open for 17% of the time, Pallas kernels for 0%

profile of v11, /device:TPU:0, one launch (start us, length us, event | category | flops | bytes accessed | tf_op | source)
XLA Modules:
  0.0 294.6 jit_solution(18430318369628564892)
XLA Ops:
  6.5 0.7 all-gather.6.cloned.1.call-update
  7.3 0.7 compare_and_fusion.2
  8.1 23.2 %all-gather.6.cloned.1.call-done = bf16[4,128,1536]{2,1,0:T(8,128)(2,1)} async-done(((bf16[1,128,1536]{2,1,0:T(8,128)(2,1)}), bf16[4,128,1536]{2,1,0:T(8,128)(2,1)}) %all-gather.6.cloned.1.call-update) | async-done | bytes 1572880 | tf_op jit(solution)/shard_map/all_gather | solution.py:40
  31.3 2.0 gather_fusion
  33.4 1.2 dynamic-slice_select_fusion
  35.0 19.7 %collective-permute-done.2 = bf16[2,2,1536,64]{2,3,1,0:T(8,128)(2,1)} collective-permute-done((bf16[2,2,1536,64]{2,3,1,0:T(8,128)(2,1)}, bf16[2,2,1536,64]{2,3,1,0:T(8,128)(2,1)}, u32[]{:S(2)}, u32[]{:S(2)}) %collective-permute-start.2) | collective-permute-done | bytes 786464 | tf_op jit(solution)/shard_map/ppermute | solution.py:50
  55.4 1.9 collective-permute-done.3
  57.3 3.2 %pad_maximum_fusion = bf16[4,2,2,1536,64]{3,4,2,1,0:T(8,128)(2,1)} fusion(bf16[1,2,2,1536,64]{3,4,2,1,0:T(8,128)(2,1)} %bitcast.9, bf16[1,2,2,1536,64]{3,4,2,1,0:T(8,128)(2,1)} %bitcast.8, bf16[1,2,2,1536,64]{3,4,2,1,0:T(8,128)(2,1)} %bitcast.7, bf16[1,2,2,1536,64]{3,4,2,1,0:T(8,128)(2,1)} %bitcast.150), kind=kLoop, calls=%fused_computation.26 | loop fusion | flops 4718592 | bytes 6291456 | tf_op jit(solution)/shard_map/stack | solution.py:53
  60.6 2.5 gather_fusion.3
  63.1 22.1 %all-gather.8.cloned.1.call-done = bf16[192,6144]{1,0:T(8,128)(2,1)} async-done(((bf16[192,1536]{1,0:T(8,128)(2,1)}), bf16[192,6144]{1,0:T(8,128)(2,1)}) %all-gather.8.cloned.1.call-update) | async-done | bytes 2359312 | tf_op jit(solution)/shard_map/all_gather | solution.py:75
  85.4 1.8 fusion.39
  87.6 16.2 %all-gather = bf16[192,1024]{0,1:T(8,128)(2,1)S(1)} all-gather(bf16[192,256]{0,1:T(8,128)(2,1)S(1)} %fusion.50), channel_id=2, replica_groups=mesh['groups'=2,'wy'=2,'wc'=2,'expert'=4] {'expert'}, dimensions={1}, use_global_device_ids=true | all-gather | bytes 491520 | tf_op jit(solution)/shard_map/all_gather | solution.py:80
  106.3 2.5 copy-done.8
  108.9 3.8 %maximum_select_fusion = bf16[384,6144]{1,0:T(8,128)(2,1)S(1)} fusion(bf16[192,6144]{1,0:T(8,128)(2,1)} %collective-permute-done, bf16[192,6144]{1,0:T(8,128)(2,1)S(1)} %copy-done.8, pred[]{:T(512)S(6)} %eq.13), kind=kLoop, calls=%fused_computation.25 | loop fusion | flops 21233664 | bytes 9437185 | tf_op jit(solution)/shard_map/jit(_where)/select_n | solution.py:85
  112.7 1.3 fusion.59
  114.1 8.3 %fusion.8 = f32[384,1024]{1,0:T(8,128)S(1)} fusion(bf16[384,6144]{1,0:T(8,128)(2,1)S(1)} %maximum_select_fusion, bf16[2,6144,1024]{2,1,0:T(8,128)(2,1)} %param.17), kind=kOutput, calls=%fused_computation.12 | convolution fusion | flops 4831838208 | bytes 18874368 | tf_op jit(solution)/shard_map/dot_general | solution.py:112
  122.5 9.3 %fusion.28 = bf16[384,1024]{1,0:T(8,128)(2,1)} fusion(f32[384,2,1024]{2,0,1:T(8,128)S(1)} %bitcast.145, f32[384,1024]{1,0:T(8,128)S(1)} %fusion.8, bf16[384,6144]{1,0:T(8,128)(2,1)S(1)} %maximum_select_fusion, bf16[2,6144,1024]{2,1,0:T(8,128)(2,1)} %param.18, f32[384]{0:T(512)S(1)} %get-tuple-element.7), kind=kOutput, calls=%fused_computation.37 | convolution fusion | flops 4835377152 | bytes 21235200 | tf_op jit(solution)/shard_map/dot_general | solution.py:116
  132.0 11.3 %fusion.2 = f32[384,1024]{1,0:T(8,128)S(1)} fusion(bf16[384,6144]{1,0:T(8,128)(2,1)} %copy-done.3, bf16[2,6144,1024]{2,1,0:T(8,128)(2,1)} %param.17), kind=kOutput, calls=%fused_computation.6 | convolution fusion | flops 4831838208 | bytes 18874368 | tf_op jit(solution)/shard_map/dot_general | solution.py:112
  143.3 9.2 %fusion.24 = bf16[384,1024]{1,0:T(8,128)(2,1)} fusion(f32[384,2,1024]{2,0,1:T(8,128)S(1)} %bitcast.146, f32[384,1024]{1,0:T(8,128)S(1)} %fusion.2, bf16[384,6144]{1,0:T(8,128)(2,1)S(1)} %copy-done.4, bf16[2,6144,1024]{2,1,0:T(8,128)(2,1)} %param.18, f32[384]{0:T(512)S(1)} %get-tuple-element.8), kind=kOutput, calls=%fused_computation.32 | convolution fusion | flops 4835377152 | bytes 21235200 | tf_op jit(solution)/shard_map/dot_general | solution.py:116
  152.5 41.2 %all-gather.10.cloned.1.call-done = bf16[384,4096]{1,0:T(8,128)(2,1)} async-done(((bf16[384,1024]{1,0:T(8,128)(2,1)}), bf16[384,4096]{1,0:T(8,128)(2,1)}) %all-gather.10.cloned.1.call-update) | async-done | bytes 3145744 | tf_op jit(solution)/shard_map/all_gather | solution.py:122
  193.8 10.0 %fusion.4 = f32[384,1536]{1,0:T(8,128)} fusion(bf16[384,4096]{1,0:T(8,128)(2,1)} %all-gather.10.cloned.1.call-done, bf16[2,4096,1536]{2,1,0:T(8,128)(2,1)} %param.19), kind=kOutput, calls=%fused_computation.8 | convolution fusion | flops 4831838208 | bytes 18087936 | tf_op jit(solution)/shard_map/dot_general | solution.py:124
  203.8 53.6 %all-gather.12.cloned.1.call-done = bf16[384,4096]{1,0:T(8,128)(2,1)} async-done(((bf16[384,1024]{1,0:T(8,128)(2,1)}), bf16[384,4096]{1,0:T(8,128)(2,1)}) %all-gather.12.cloned.1.call-update) | async-done | bytes 3145744 | tf_op jit(solution)/shard_map/all_gather | solution.py:122
  257.4 6.7 %fusion.33 = f32[384,768]{1,0:T(8,128)S(1)} fusion(bf16[384,4096]{1,0:T(8,128)(2,1)} %all-gather.12.cloned.1.call-done, bf16[2,4096,1536]{2,1,0:T(8,128)(2,1)} %param.19, f32[384,1536]{1,0:T(8,128)} %fusion.4), kind=kOutput, calls=%fused_computation.38 | convolution fusion | flops 2416214016 | bytes 11796480 | tf_op jit(solution)/shard_map/dot_general | solution.py:131
  264.1 0.9 select_bitcast_fusion.1
  265.0 5.4 %fusion.36 = f32[384,768]{1,0:T(8,128)S(1)} fusion(bf16[384,4096]{1,0:T(8,128)(2,1)S(1)} %copy-done.12, bf16[2,4096,1536]{2,1,0:T(8,128)(2,1)} %param.19, f32[384,1536]{1,0:T(8,128)S(1)} %copy-done.13), kind=kOutput, calls=%fused_computation.39 | convolution fusion | flops 2416214016 | bytes 11796480 | tf_op jit(solution)/shard_map/dot_general | solution.py:131
  270.4 0.9 select_bitcast_fusion
  272.0 1.5 collective-permute-start.6
  273.8 1.2 bitcast_add_fusion
  275.0 1.6 collective-permute-start.8
  276.6 5.3 %collective-permute-done.6 = f32[96,768]{1,0:T(8,128)S(1)} collective-permute-done((f32[96,768]{1,0:T(8,128)S(1)}, f32[96,768]{1,0:T(8,128)S(1)}, u32[]{:S(2)}, u32[]{:S(2)}) %collective-permute-start.6) | collective-permute-done | bytes 294944 | tf_op jit(solution)/shard_map/ppermute | solution.py:151
  281.9 5.3 %collective-permute-done.8 = f32[96,768]{1,0:T(8,128)S(1)} collective-permute-done((f32[96,768]{1,0:T(8,128)S(1)}, f32[96,768]{1,0:T(8,128)S(1)}, u32[]{:S(2)}, u32[]{:S(2)}) %collective-permute-start.8) | collective-permute-done | bytes 294944 | tf_op jit(solution)/shard_map/ppermute | solution.py:151
  287.3 0.7 pad_maximum_fusion.1
  (75 shorter events, 5.8 us)
Async XLA Ops:
  6.5 97.5 %copy-start = (bf16[8,2,64,1024]{3,2,1,0:T(8,128)(2,1)S(1)}, bf16[8,2,64,1024]{3,2,1,0:T(8,128)(2,1)}, u32[]{:S(2)}) copy-start(bf16[8,2,64,1024]{3,2,1,0:T(8,128)(2,1)} %param.21) | copy-start | bytes 6291460
  6.5 48.2 %copy-start.11 = (s32[3]{0:T(128)S(1)}, s32[3]{0:T(128)}, u32[]{:S(2)}) copy-start(s32[3]{0:T(128)} %param.14) | copy-start | bytes 40
  6.5 48.2 %copy-start.2 = (s32[8]{0:T(128)S(1)}, s32[8]{0:T(128)}, u32[]{:S(2)}) copy-start(s32[8]{0:T(128)} %param.15) | copy-start | bytes 100
  6.5 24.8 %all-gather.6.cloned.1.call-start = ((), (), s32[]{:S(2)}) async-start(), calls=%async_computation | async-start | bytes 1966080 | tf_op jit(solution)/shard_map/all_gather | solution.py:40
  7.3 77.9 %all-gather.8.cloned.1.call-start = ((), (), s32[]{:S(2)}) async-start(), calls=%async_computation.1 | async-start | bytes 2949120 | tf_op jit(solution)/shard_map/all_gather | solution.py:75
  33.4 27.2 %copy-start.7 = (bf16[3,128,1536]{2,1,0:T(8,128)(2,1)}, bf16[3,128,1536]{2,1,0:T(8,128)(2,1)S(1)}, u32[]{:S(2)}) copy-start(bf16[3,128,1536]{2,1,0:T(8,128)(2,1)S(1)} %gather_fusion) | copy-start | bytes 3538948
  34.6 159.2 %all-gather.10.cloned.1.call-start = ((), (), s32[]{:S(2)}) async-start(), calls=%async_computation.2 | async-start | bytes 3932160 | tf_op jit(solution)/shard_map/all_gather | solution.py:122
  34.7 20.1 %collective-permute-start.2 = (bf16[2,2,1536,64]{2,3,1,0:T(8,128)(2,1)}, bf16[2,2,1536,64]{2,3,1,0:T(8,128)(2,1)}, u32[]{:S(2)}, u32[]{:S(2)}) collective-permute-start(bf16[2,2,1536,64]{2,3,1,0:T(8,128)(2,1)} %param.20), channel_id=1, source_target_pairs={{0,8},{8,0},{1,9},{9,1},{2,10},{10,2},{3,11},{11,3},{4,12},{12,4},... | collective-permute-start | bytes 2359304 | tf_op jit(solution)/shard_map/ppermute | solution.py:50
  35.0 20.4 %collective-permute-start.1 = (bf16[2,2,1536,64]{2,3,1,0:T(8,128)(2,1)}, bf16[2,2,1536,64]{2,3,1,0:T(8,128)(2,1)}, u32[]{:S(2)}, u32[]{:S(2)}) collective-permute-start(bf16[2,2,1536,64]{2,3,1,0:T(8,128)(2,1)} %param.20), channel_id=1, source_target_pairs={{0,4},{4,0},{1,5},{5,1},{2,6},{6,2},{3,7},{7,3},{8,12},{12,8},{9,1... | collective-permute-start | bytes 2359304 | tf_op jit(solution)/shard_map/ppermute | solution.py:51
  54.7 2.6 collective-permute-start.3
  85.2 21.1 %collective-permute-start = (bf16[192,6144]{1,0:T(8,128)(2,1)}, bf16[192,6144]{1,0:T(8,128)(2,1)}, u32[]{:S(2)}, u32[]{:S(2)}) collective-permute-start(bf16[192,6144]{1,0:T(8,128)(2,1)} %all-gather.8.cloned.1.call-done), channel_id=1, source_target_pairs={{0,4},{4,0},{1,5},{5,1},{2,6},{6,2},{3,7},{7,3},{8,12},{12,8},{9,1... | collective-permute-start | bytes 7077896 | tf_op jit(solution)/shard_map/ppermute | solution.py:83
  87.2 16.8 %copy-start.10 = (s32[384,2]{0,1:T(2,128)S(1)}, s32[384,2]{0,1:T(2,128)}, u32[]{:S(2)}) copy-start(s32[384,2]{0,1:T(2,128)} %param.13) | copy-start | bytes 9220
  104.0 1.3 collective-permute-start.4
  106.1 2.8 copy-start.8
  106.3 16.2 %copy-start.5 = (f32[3,128,2,1024]{3,1,0,2:T(8,128)}, f32[3,128,2,1024]{3,1,0,2:T(8,128)S(1)}, u32[]{:S(2)}) copy-start(f32[3,128,2,1024]{3,1,0,2:T(8,128)S(1)} %copy.29) | copy-start | bytes 9437188
  106.3 6.4 %copy-start.9 = (bf16[6144,8]{0,1:T(8,128)(2,1)S(1)}, bf16[6144,8]{0,1:T(8,128)(2,1)}, u32[]{:S(2)}) copy-start(bf16[6144,8]{0,1:T(8,128)(2,1)} %param.16) | copy-start | bytes 294916
  112.7 9.8 %copy-start.3 = (bf16[384,6144]{1,0:T(8,128)(2,1)}, bf16[384,6144]{1,0:T(8,128)(2,1)S(1)}, u32[]{:S(2)}) copy-start(bf16[384,6144]{1,0:T(8,128)(2,1)S(1)} %maximum_select_fusion) | copy-start | bytes 14155780
  131.8 125.6 %all-gather.12.cloned.1.call-start = ((), (), s32[]{:S(2)}) async-start(), calls=%async_computation.3 | async-start | bytes 3932160 | tf_op jit(solution)/shard_map/all_gather | solution.py:122
  132.0 11.3 %copy-start.4 = (bf16[384,6144]{1,0:T(8,128)(2,1)S(1)}, bf16[384,6144]{1,0:T(8,128)(2,1)}, u32[]{:S(2)}) copy-start(bf16[384,6144]{1,0:T(8,128)(2,1)} %copy-done.3) | copy-start | bytes 14155780
  132.0 11.3 %copy-start.6 = (f32[3,128,2,1024]{3,1,0,2:T(8,128)S(1)}, f32[3,128,2,1024]{3,1,0,2:T(8,128)}, u32[]{:S(2)}) copy-start(f32[3,128,2,1024]{3,1,0,2:T(8,128)} %copy-done.5) | copy-start | bytes 9437188
  257.4 7.6 %copy-start.12 = (bf16[384,4096]{1,0:T(8,128)(2,1)S(1)}, bf16[384,4096]{1,0:T(8,128)(2,1)}, u32[]{:S(2)}) copy-start(bf16[384,4096]{1,0:T(8,128)(2,1)} %all-gather.12.cloned.1.call-done) | copy-start | bytes 9437188
  257.4 7.6 %copy-start.13 = (f32[384,1536]{1,0:T(8,128)S(1)}, f32[384,1536]{1,0:T(8,128)}, u32[]{:S(2)}) copy-start(f32[384,1536]{1,0:T(8,128)} %fusion.4) | copy-start | bytes 7077892
  265.0 6.8 %collective-permute-start.5 = (f32[2,96,768]{2,1,0:T(8,128)}, f32[2,96,768]{2,1,0:T(8,128)S(1)}, u32[]{:S(2)}, u32[]{:S(2)}) collective-permute-start(f32[2,96,768]{2,1,0:T(8,128)} %select_bitcast_fusion.1), channel_id=1, source_target_pairs={{0,4},{4,0},{1,5},{5,1},{2,6},{6,2},{3,7},{7,3},{8,12},{12,8},{9,1... | collective-permute-start | bytes 1769480 | tf_op jit(solution)/shard_map/ppermute | solution.py:146
  271.3 2.5 collective-permute-start.7
  271.9 16.2 %copy-start.1 = (bf16[8,2,64,1024]{3,2,1,0:T(8,128)(2,1)S(1)}, bf16[8,2,64,1024]{3,2,1,0:T(8,128)(2,1)}, u32[]{:S(2)}) copy-start(bf16[8,2,64,1024]{3,2,1,0:T(8,128)(2,1)} %param.21) | copy-start | bytes 6291460
  272.0 9.9 %collective-permute-start.6 = (f32[96,768]{1,0:T(8,128)S(1)}, f32[96,768]{1,0:T(8,128)S(1)}, u32[]{:S(2)}, u32[]{:S(2)}) collective-permute-start(f32[96,768]{1,0:T(8,128)S(1)} %select_bitcast_fusion.3), channel_id=1, source_target_pairs={{0,8},{8,0},{1,9},{9,1},{2,10},{10,2},{3,11},{11,3},{4,12},{12,4},... | collective-permute-start | bytes 884744 | tf_op jit(solution)/shard_map/ppermute | solution.py:151
  275.0 12.2 %collective-permute-start.8 = (f32[96,768]{1,0:T(8,128)S(1)}, f32[96,768]{1,0:T(8,128)S(1)}, u32[]{:S(2)}, u32[]{:S(2)}) collective-permute-start(f32[96,768]{1,0:T(8,128)S(1)} %select_bitcast_fusion.2), channel_id=1, source_target_pairs={{0,8},{8,0},{1,9},{9,1},{2,10},{10,2},{3,11},{11,3},{4,12},{12,4},... | collective-permute-start | bytes 884744 | tf_op jit(solution)/shard_map/ppermute | solution.py:151
Sparse Core Ops, SparseCore 0:
  8.9 22.3 all-gather.5
  34.7 50.4 all-gather.7
  131.9 61.8 all-gather.9
  195.2 62.1 all-gather.11

commit v12 on v10

--- a/solution.py
+++ b/solution.py
@@ -71,14 +71,19 @@
     half = tokens // cores
     expert_size = lax.axis_size("expert")
     swap = [(i, (i + 1) % cores) for i in range(cores)]
-    mine_q = lax.dynamic_slice_in_dim(rows_q, core * half, half, 0)
-    mine = lax.all_gather(mine_q, "expert", axis=1, tiled=True)
     rank_q = lax.dynamic_slice_in_dim(
         jnp.concatenate([rank_hi, rank_lo], axis=1), core * half, half, 0
     )
-    rank_q, _ = lax.optimization_barrier((rank_q, mine))
-    pieces = lax.all_gather(rank_q, "expert", axis=1, tiled=False).astype(jnp.float32)
-    mine_rank = jnp.sum(pieces[:, :, : window * rank] + pieces[:, :, window * rank :], axis=1)
+    rank_rows = rank_q.reshape(-1, quarter)
+    mine_q = jnp.concatenate(
+        [lax.dynamic_slice_in_dim(rows_q, core * half, half, 0), rank_rows], axis=0
+    )
+    arrived = lax.all_gather(mine_q, "expert", axis=1, tiled=True)
+    mine = arrived[:half]
+    pieces = jnp.transpose(
+        arrived[half:].reshape(rank_rows.shape[0], expert_size, quarter), (1, 0, 2)
+    ).reshape(expert_size, half, rank_q.shape[1]).astype(jnp.float32)
+    mine_rank = jnp.sum(pieces[:, :, : window * rank] + pieces[:, :, window * rank :], axis=0)
     mine_rank = mine_rank.astype(jnp.bfloat16)
     other = lax.ppermute(mine, "wc", swap)
     other_rank = lax.ppermute(mine_rank, "wc", swap)

time: 296 us -> 312 us (1.054)
  waiting for transfers between devices: 180 us -> 197 us
  blocking collectives: 15.9 us -> 0 us
  other arithmetic: 13 us -> 19.3 us
  local copies, waits for them, and re-layouts: 11.5 us -> 16 us
  starting transfers between devices: 2.38 us -> 5.53 us
    all_gather x1, waiting for transfers between devices: 22.1 us -> 59.4 us  [per_device(): arrived = lax.all_gather(mine_q, 'expert', axis=1, tiled=True)]
    all_gather x1, waiting for transfers between devices: 23.2 us -> 0.01 us  [per_device(): slots_q = lax.all_gather(prompts, WIDE, axis=0, tiled=True)]
    all_gather x1 -> x0, blocking collectives: 15.9 us -> none  [per_device(): lax.all_gather(rank_q, 'expert', axis=1, tiled=False).astype(jnp.float32)]
    ppermute x1, waiting for transfers between devices: 19.7 us -> 24.6 us  [per_device(): from_chip = lax.ppermute(adapter_down_weight, 'wy', swap)]
    convert_element_type x0 -> x3, local copies, waits for them, and re-layouts: none -> 3.91 us  [per_device(): pieces = jnp.transpose(arrived[half:].reshape(rank_rows.shape[0], expert_...]
    unnamed x28 -> x18, local copies, waits for them, and re-layouts: 5.08 us -> 1.45 us
    slice x0 -> x1, local copies, waits for them, and re-layouts: none -> 3.32 us  [per_device(): mine = arrived[:half]]
  transfers between devices with their start and end apart: 11 -> 11, of which waited for: 9 -> 7; matrix products, arithmetic and copies ran while one was open for 14% -> 15% of each run, Pallas kernels for 0% -> 0%
where the time goes in v12:
time: 312 us; the launch traced here: 311 us
  waiting for transfers between devices  197 us (63%)
  matrix products  60.3 us (19%)
  other arithmetic  19.3 us (6%)
  local copies, waits for them, and re-layouts  16 us (5%)
  between operations  13.5 us (4%)
  starting transfers between devices  5.53 us (2%)
    all_gather x2, waiting for transfers between devices, per_device(): gathered = lax.all_gather(hidden, 'expert', axis=1, tiled=True)  95.6 us
    all_gather x1, waiting for transfers between devices, per_device(): arrived = lax.all_gather(mine_q, 'expert', axis=1, tiled=True)  59.4 us
    ppermute x1, waiting for transfers between devices, per_device(): from_chip = lax.ppermute(adapter_down_weight, 'wy', swap)  24.6 us
    dot_general x2, matrix products, per_device(): jnp.dot(gathered, down_weight[expert_number], preferred_element_type=jnp....  19.3 us
    dot_general x2, matrix products, per_device(): jnp.dot(input_rows, gate_weight[expert_number], preferred_element_type=jn...  19.2 us
    dot_general x2, matrix products, per_device(): jnp.dot(input_rows, up_weight[expert_number], preferred_element_type=jnp....  18.1 us
    ppermute x1, waiting for transfers between devices, reduce_rows(): return mine + lax.ppermute(away, 'wy', [(0, 1), (1, 0)])  13.9 us
    select_n x1, other arithmetic, per_device(): jnp.where(core == 0, jnp.concatenate([mine, other], axis=0), jnp.concaten...  6.28 us
  transfers between devices with their start and end apart: 11, of which 7 were waited for; matrix products, arithmetic and copies ran while one was open for 15% of the time, Pallas kernels for 0%

profile of v12, /device:TPU:0, one launch (start us, length us, event | category | flops | bytes accessed | tf_op | source)
XLA Modules:
  0.0 311.2 jit_solution(9651579633128031640)
XLA Ops:
  6.5 3.0 collective-permute-start.1
  10.3 24.6 %collective-permute-done.1 = bf16[2,2,1536,64]{2,3,1,0:T(8,128)(2,1)S(1)} collective-permute-done((bf16[2,2,1536,64]{2,3,1,0:T(8,128)(2,1)}, bf16[2,2,1536,64]{2,3,1,0:T(8,128)(2,1)S(1)}, u32[]{:S(2)}, u32[]{:S(2)}) %collective-permute-start.1) | collective-permute-done | bytes 786464 | tf_op jit(solution)/shard_map/ppermute | solution.py:50
  35.8 1.3 gather_fusion.1
  37.8 3.1 pad_maximum_fusion
  40.9 2.5 gather_fusion.2
  43.4 1.2 broadcast_select_fusion
  44.6 2.0 gather_fusion
  46.6 1.8 fusion.33
  49.2 0.9 pad_maximum_fusion.1
  50.2 59.4 %all-gather.7.cloned.1.call-done = bf16[224,6144]{1,0:T(8,128)(2,1)} async-done(((bf16[224,1536]{1,0:T(8,128)(2,1)}), bf16[224,6144]{1,0:T(8,128)(2,1)}) %all-gather.7.cloned.1.call-update) | async-done | bytes 2752528 | tf_op jit(solution)/shard_map/all_gather | solution.py:81
  109.6 3.3 %slice.106 = bf16[192,6144]{1,0:T(8,128)(2,1)} slice(bf16[224,6144]{1,0:T(8,128)(2,1)} %all-gather.7.cloned.1.call-done), slice={[0:192], [0:6144]} | slice | bytes 4718592 | tf_op jit(solution)/shard_map/slice | solution.py:82
  112.9 1.0 slice_convert_fusion
  114.0 1.4 reshape.98
  115.4 1.4 copy.32
  116.8 1.1 reshape.97
  117.9 1.2 fusion.40
  121.5 6.3 %maximum_select_fusion = bf16[384,6144]{1,0:T(8,128)(2,1)S(1)} fusion(bf16[192,6144]{1,0:T(8,128)(2,1)} %collective-permute-done.3, bf16[192,6144]{1,0:T(8,128)(2,1)} %slice.106, pred[]{:T(512)S(6)} %eq.13), kind=kLoop, calls=%fused_computation.22 | loop fusion | flops 21233664 | bytes 9437185 | tf_op jit(solution)/shard_map/jit(_where)/select_n | solution.py:90
  127.8 1.3 fusion.52
  129.3 8.1 %fusion.4 = f32[384,1024]{1,0:T(8,128)S(1)} fusion(bf16[384,6144]{1,0:T(8,128)(2,1)S(1)} %maximum_select_fusion, bf16[2,6144,1024]{2,1,0:T(8,128)(2,1)} %param.17), kind=kOutput, calls=%fused_computation.8 | convolution fusion | flops 4831838208 | bytes 18874368 | tf_op jit(solution)/shard_map/dot_general | solution.py:117
  137.4 9.0 %fusion.24 = bf16[384,1024]{1,0:T(8,128)(2,1)} fusion(f32[384,2,1024]{2,0,1:T(8,128)S(1)} %bitcast.110, f32[384,1024]{1,0:T(8,128)S(1)} %fusion.4, bf16[384,6144]{1,0:T(8,128)(2,1)S(1)} %maximum_select_fusion, bf16[2,6144,1024]{2,1,0:T(8,128)(2,1)} %param.18, f32[384]{0:T(512)S(1)} %get-tuple-element.6), kind=kOutput, calls=%fused_computation.30 | convolution fusion | flops 4835377152 | bytes 21235200 | tf_op jit(solution)/shard_map/dot_general | solution.py:121
  146.7 11.1 %fusion.10 = f32[384,1024]{1,0:T(8,128)S(1)} fusion(bf16[384,6144]{1,0:T(8,128)(2,1)} %copy-done.2, bf16[2,6144,1024]{2,1,0:T(8,128)(2,1)} %param.17), kind=kOutput, calls=%fused_computation.14 | convolution fusion | flops 4831838208 | bytes 18874368 | tf_op jit(solution)/shard_map/dot_general | solution.py:117
  157.8 9.1 %fusion.28 = bf16[384,1024]{1,0:T(8,128)(2,1)} fusion(f32[384,2,1024]{2,0,1:T(8,128)S(1)} %bitcast.111, f32[384,1024]{1,0:T(8,128)S(1)} %fusion.10, bf16[384,6144]{1,0:T(8,128)(2,1)S(1)} %copy-done.3, bf16[2,6144,1024]{2,1,0:T(8,128)(2,1)} %param.18, f32[384]{0:T(512)S(1)} %get-tuple-element.5), kind=kOutput, calls=%fused_computation.35 | convolution fusion | flops 4835377152 | bytes 21235200 | tf_op jit(solution)/shard_map/dot_general | solution.py:121
  166.9 42.0 %all-gather.11.cloned.1.call-done = bf16[384,4096]{1,0:T(8,128)(2,1)} async-done(((bf16[384,1024]{1,0:T(8,128)(2,1)}), bf16[384,4096]{1,0:T(8,128)(2,1)}) %all-gather.11.cloned.1.call-update) | async-done | bytes 3145744 | tf_op jit(solution)/shard_map/all_gather | solution.py:127
  208.9 10.0 %fusion = f32[384,1536]{1,0:T(8,128)} fusion(bf16[384,4096]{1,0:T(8,128)(2,1)} %all-gather.11.cloned.1.call-done, bf16[2,4096,1536]{2,1,0:T(8,128)(2,1)} %param.19), kind=kOutput, calls=%fused_computation.4 | convolution fusion | flops 4831838208 | bytes 18087936 | tf_op jit(solution)/shard_map/dot_general | solution.py:128
  218.9 53.6 %all-gather.9.cloned.1.call-done = bf16[384,4096]{1,0:T(8,128)(2,1)} async-done(((bf16[384,1024]{1,0:T(8,128)(2,1)}), bf16[384,4096]{1,0:T(8,128)(2,1)}) %all-gather.9.cloned.1.call-update) | async-done | bytes 3145744 | tf_op jit(solution)/shard_map/all_gather | solution.py:127
  272.5 9.3 %fusion.18 = f32[384,1536]{1,0:T(8,128)S(1)} fusion(f32[384,1536]{1,0:T(8,128)} %fusion, bf16[384,4096]{1,0:T(8,128)(2,1)} %all-gather.9.cloned.1.call-done, bf16[2,4096,1536]{2,1,0:T(8,128)(2,1)} %param.19), kind=kOutput, calls=%fused_computation.24 | convolution fusion | flops 4832428032 | bytes 20447232 | tf_op jit(solution)/shard_map/dot_general | solution.py:128
  281.8 1.4 copy-done.4
  283.4 2.8 collective-permute-done.5
  286.3 2.0 bitcast_add_fusion
  288.4 1.5 collective-permute-start.6
  289.9 13.9 %collective-permute-done.6 = f32[96,1536]{1,0:T(8,128)S(1)} collective-permute-done((f32[96,1536]{1,0:T(8,128)S(1)}, f32[96,1536]{1,0:T(8,128)S(1)}, u32[]{:S(2)}, u32[]{:S(2)}) %collective-permute-start.6) | collective-permute-done | bytes 589856 | tf_op jit(solution)/shard_map/ppermute | solution.py:144
  303.8 0.8 fusion.38
  (61 shorter events, 6.2 us)
Async XLA Ops:
  6.5 113.1 %copy-start = (bf16[8,2,64,1024]{3,2,1,0:T(8,128)(2,1)S(1)}, bf16[8,2,64,1024]{3,2,1,0:T(8,128)(2,1)}, u32[]{:S(2)}) copy-start(bf16[8,2,64,1024]{3,2,1,0:T(8,128)(2,1)} %param.21) | copy-start | bytes 6291460
  6.5 38.1 %all-gather.5.cloned.1.call-start = ((), (), s32[]{:S(2)}) async-start(), calls=%async_computation | async-start | bytes 1966080 | tf_op jit(solution)/shard_map/all_gather | solution.py:40
  6.5 28.4 %collective-permute-start.1 = (bf16[2,2,1536,64]{2,3,1,0:T(8,128)(2,1)}, bf16[2,2,1536,64]{2,3,1,0:T(8,128)(2,1)S(1)}, u32[]{:S(2)}, u32[]{:S(2)}) collective-permute-start(bf16[2,2,1536,64]{2,3,1,0:T(8,128)(2,1)} %param.20), channel_id=1, source_target_pairs={{0,8},{8,0},{1,9},{9,1},{2,10},{10,2},{3,11},{11,3},{4,12},{12,4},... | collective-permute-start | bytes 2359304 | tf_op jit(solution)/shard_map/ppermute | solution.py:50
  9.5 100.0 %all-gather.7.cloned.1.call-start = ((), (), s32[]{:S(2)}) async-start(), calls=%async_computation.1 | async-start | bytes 3440640 | tf_op jit(solution)/shard_map/all_gather | solution.py:81
  9.6 28.2 %collective-permute-start = (bf16[2,2,1536,64]{2,3,1,0:T(8,128)(2,1)}, bf16[2,2,1536,64]{2,3,1,0:T(8,128)(2,1)}, u32[]{:S(2)}, u32[]{:S(2)}) collective-permute-start(bf16[2,2,1536,64]{2,3,1,0:T(8,128)(2,1)} %param.20), channel_id=1, source_target_pairs={{0,4},{4,0},{1,5},{5,1},{2,6},{6,2},{3,7},{7,3},{8,12},{12,8},{9,1... | collective-permute-start | bytes 2359304 | tf_op jit(solution)/shard_map/ppermute | solution.py:51
  34.9 2.8 collective-permute-start.2
  50.2 158.7 %all-gather.11.cloned.1.call-start = ((), (), s32[]{:S(2)}) async-start(), calls=%async_computation.3 | async-start | bytes 3932160 | tf_op jit(solution)/shard_map/all_gather | solution.py:127
  112.9 8.6 %collective-permute-start.3 = (bf16[192,6144]{1,0:T(8,128)(2,1)}, bf16[192,6144]{1,0:T(8,128)(2,1)}, u32[]{:S(2)}, u32[]{:S(2)}) collective-permute-start(bf16[192,6144]{1,0:T(8,128)(2,1)} %slice.106), channel_id=1, source_target_pairs={{0,4},{4,0},{1,5},{5,1},{2,6},{6,2},{3,7},{7,3},{8,12},{12,8},{9,1... | collective-permute-start | bytes 7077896 | tf_op jit(solution)/shard_map/ppermute | solution.py:88
  115.4 4.2 %copy-start.8 = (s32[384,2]{0,1:T(2,128)S(1)}, s32[384,2]{0,1:T(2,128)}, u32[]{:S(2)}) copy-start(s32[384,2]{0,1:T(2,128)} %param.13) | copy-start | bytes 9220
  119.0 1.5 collective-permute-start.4
  121.5 15.9 %copy-start.5 = (f32[3,128,2,1024]{3,1,0,2:T(8,128)}, f32[3,128,2,1024]{3,1,0,2:T(8,128)S(1)}, u32[]{:S(2)}) copy-start(f32[3,128,2,1024]{3,1,0,2:T(8,128)S(1)} %copy.35) | copy-start | bytes 9437188
  121.5 6.3 %copy-start.7 = (bf16[6144,8]{0,1:T(8,128)(2,1)S(1)}, bf16[6144,8]{0,1:T(8,128)(2,1)}, u32[]{:S(2)}) copy-start(bf16[6144,8]{0,1:T(8,128)(2,1)} %param.16) | copy-start | bytes 294916
  127.8 9.6 %copy-start.2 = (bf16[384,6144]{1,0:T(8,128)(2,1)}, bf16[384,6144]{1,0:T(8,128)(2,1)S(1)}, u32[]{:S(2)}) copy-start(bf16[384,6144]{1,0:T(8,128)(2,1)S(1)} %maximum_select_fusion) | copy-start | bytes 14155780
  146.4 126.0 %all-gather.9.cloned.1.call-start = ((), (), s32[]{:S(2)}) async-start(), calls=%async_computation.2 | async-start | bytes 3932160 | tf_op jit(solution)/shard_map/all_gather | solution.py:127
  146.7 11.1 %copy-start.3 = (bf16[384,6144]{1,0:T(8,128)(2,1)S(1)}, bf16[384,6144]{1,0:T(8,128)(2,1)}, u32[]{:S(2)}) copy-start(bf16[384,6144]{1,0:T(8,128)(2,1)} %copy-done.2) | copy-start | bytes 14155780
  146.7 11.1 %copy-start.6 = (f32[3,128,2,1024]{3,1,0,2:T(8,128)S(1)}, f32[3,128,2,1024]{3,1,0,2:T(8,128)}, u32[]{:S(2)}) copy-start(f32[3,128,2,1024]{3,1,0,2:T(8,128)} %copy-done.5) | copy-start | bytes 9437188
  281.8 1.4 copy-start.4
  283.3 2.9 collective-permute-start.5
  286.3 18.4 %copy-start.1 = (bf16[8,2,64,1024]{3,2,1,0:T(8,128)(2,1)S(1)}, bf16[8,2,64,1024]{3,2,1,0:T(8,128)(2,1)}, u32[]{:S(2)}) copy-start(bf16[8,2,64,1024]{3,2,1,0:T(8,128)(2,1)} %param.21) | copy-start | bytes 6291460
  288.4 15.4 %collective-permute-start.6 = (f32[96,1536]{1,0:T(8,128)S(1)}, f32[96,1536]{1,0:T(8,128)S(1)}, u32[]{:S(2)}, u32[]{:S(2)}) collective-permute-start(f32[96,1536]{1,0:T(8,128)S(1)} %select_bitcast_fusion.1), channel_id=1, source_target_pairs={{0,8},{8,0},{1,9},{9,1},{2,10},{10,2},{3,11},{11,3},{4,12},{12,4},... | collective-permute-start | bytes 1769480 | tf_op jit(solution)/shard_map/ppermute | solution.py:144
Sparse Core Ops, SparseCore 0:
  9.7 27.7 all-gather.4
  50.3 59.2 all-gather.6
  146.6 62.2 all-gather.10
  210.3 62.1 all-gather.8

commit v13 on v10

--- a/solution.py
+++ b/solution.py
@@ -37,9 +37,22 @@
     tile_rows = tokens // tile_count
     resident_slots = adapter_down_weight.shape[0]
     rank = adapter_down_weight.shape[3]
-    slots_q = lax.all_gather(prompts, WIDE, axis=0, tiled=True)
     slot_of_span = span_slot_owner[:nchunk]
-    rows_q = jnp.take(slots_q, slot_of_span, axis=0).reshape(tokens, quarter)
+    held_slots = prompts.shape[0]
+    if lax.axis_size("wy") == 2 and cores == 2:
+        pair = [(0, 1), (1, 0)]
+        slot_chip = lax.ppermute(prompts, "wy", pair)
+        slot_core = lax.ppermute(prompts, "wc", pair)
+        slot_both = lax.ppermute(slot_chip, "wc", pair)
+        slots_q = jnp.concatenate([prompts, slot_core, slot_chip, slot_both], axis=0)
+        slot_pick = (
+            jnp.bitwise_xor(slot_of_span // held_slots, wide_index) * held_slots
+            + slot_of_span % held_slots
+        )
+    else:
+        slots_q = lax.all_gather(prompts, WIDE, axis=0, tiled=True)
+        slot_pick = slot_of_span
+    rows_q = jnp.take(slots_q, slot_pick, axis=0).reshape(tokens, quarter)
 
     chips = lax.axis_size("wy")
     tile_slot_index = jnp.take(tenant_adapter_slot, tile_tenant_index)

time: 296 us -> 289 us (0.976)
  waiting for transfers between devices: 180 us -> 167 us
  starting transfers between devices: 2.38 us -> 6.73 us
    all_gather x1 -> x0, waiting for transfers between devices: 23.2 us -> none  [per_device(): slots_q = lax.all_gather(prompts, WIDE, axis=0, tiled=True)]
    ppermute x0 -> x3, waiting for transfers between devices: none -> 10.2 us  [the longest x1 9.32 us: per_device(): slot_chip = lax.ppermute(prompts, 'wy', pair)]
    ppermute x0 -> x3, starting transfers between devices: none -> 2.97 us  [the longest x1 2.97 us: per_device(): slot_chip = lax.ppermute(prompts, 'wy', pair)]
  transfers between devices with their start and end apart: 11 -> 13, of which waited for: 9 -> 10; matrix products, arithmetic and copies ran while one was open for 14% -> 14% of each run, Pallas kernels for 0% -> 0%
where the time goes in v13:
time: 289 us
  waiting for transfers between devices  167 us (58%)
  matrix products  59.1 us (20%)
  blocking collectives  15.9 us (6%)
  other arithmetic  15.3 us (5%)
  between operations  13.5 us (5%)
  local copies, waits for them, and re-layouts  11.5 us (4%)
  starting transfers between devices  6.73 us (2%)
    all_gather x2, waiting for transfers between devices, per_device(): gathered = lax.all_gather(hidden, 'expert', axis=1, tiled=True)  95.4 us
    all_gather x1, waiting for transfers between devices, per_device(): mine = lax.all_gather(mine_q, 'expert', axis=1, tiled=True)  23.7 us
    dot_general x2, matrix products, per_device(): jnp.dot(gathered, down_weight[expert_number], preferred_element_type=jnp....  19.3 us
    dot_general x2, matrix products, per_device(): jnp.dot(input_rows, gate_weight[expert_number], preferred_element_type=jn...  19.2 us
    ppermute x1, waiting for transfers between devices, per_device(): from_chip = lax.ppermute(adapter_down_weight, 'wy', swap)  18.2 us
    dot_general x2, matrix products, per_device(): jnp.dot(input_rows, up_weight[expert_number], preferred_element_type=jnp....  18.1 us
    all_gather x1, blocking collectives, per_device(): lax.all_gather(rank_q, 'expert', axis=1, tiled=False).astype(jnp.float32)  15.9 us
    ppermute x1, waiting for transfers between devices, reduce_rows(): return mine + lax.ppermute(away, 'wy', [(0, 1), (1, 0)])  13.9 us
  transfers between devices with their start and end apart: 13, of which 10 were waited for; matrix products, arithmetic and copies ran while one was open for 14% of the time, Pallas kernels for 0%

profile of v13, /device:TPU:0, one launch (start us, length us, event | category | flops | bytes accessed | tf_op | source)
XLA Modules:
  0.0 288.8 jit_solution(2763385082048566804)
XLA Ops:
  6.5 3.0 %collective-permute-start.1 = (bf16[1,128,1536]{2,1,0:T(8,128)(2,1)}, bf16[1,128,1536]{2,1,0:T(8,128)(2,1)S(1)}, u32[]{:S(2)}, u32[]{:S(2)}) collective-permute-start(bf16[1,128,1536]{2,1,0:T(8,128)(2,1)} %param.11), channel_id=1, source_target_pairs={{0,8},{8,0},{1,9},{9,1},{2,10},{10,2},{3,11},{11,3},{4,12},{12,4},... | collective-permute-start | bytes 1179656 | tf_op jit(solution)/shard_map/ppermute | solution.py:44
  9.5 9.3 %collective-permute-done.1 = bf16[1,128,1536]{2,1,0:T(8,128)(2,1)S(1)} collective-permute-done((bf16[1,128,1536]{2,1,0:T(8,128)(2,1)}, bf16[1,128,1536]{2,1,0:T(8,128)(2,1)S(1)}, u32[]{:S(2)}, u32[]{:S(2)}) %collective-permute-start.1) | collective-permute-done | bytes 393248 | tf_op jit(solution)/shard_map/ppermute | solution.py:44
  18.8 0.7 compare_and_fusion.2
  19.7 0.9 collective-permute-done.2
  20.6 2.4 pad_maximum_fusion.1
  22.9 2.1 gather_fusion
  25.0 1.2 dynamic-slice_select_fusion
  26.3 1.8 collective-permute-start.5
  28.1 18.2 %collective-permute-done.5 = bf16[2,2,1536,64]{2,3,1,0:T(8,128)(2,1)} collective-permute-done((bf16[2,2,1536,64]{2,3,1,0:T(8,128)(2,1)}, bf16[2,2,1536,64]{2,3,1,0:T(8,128)(2,1)}, u32[]{:S(2)}, u32[]{:S(2)}) %collective-permute-start.5) | collective-permute-done | bytes 786464 | tf_op jit(solution)/shard_map/ppermute | solution.py:63
  47.0 1.9 collective-permute-done.6
  48.9 3.2 %pad_maximum_fusion = bf16[4,2,2,1536,64]{3,4,2,1,0:T(8,128)(2,1)} fusion(bf16[1,2,2,1536,64]{3,4,2,1,0:T(8,128)(2,1)} %bitcast.9, bf16[1,2,2,1536,64]{3,4,2,1,0:T(8,128)(2,1)} %bitcast.8, bf16[1,2,2,1536,64]{3,4,2,1,0:T(8,128)(2,1)} %bitcast.7, bf16[1,2,2,1536,64]{3,4,2,1,0:T(8,128)(2,1)} %bitcast.119), kind=kLoop, calls=%fused_computation.23 | loop fusion | flops 4718592 | bytes 6291456 | tf_op jit(solution)/shard_map/stack | solution.py:66
  52.1 2.5 gather_fusion.3
  54.6 23.7 %all-gather.5.cloned.1.call-done = bf16[192,6144]{1,0:T(8,128)(2,1)} async-done(((bf16[192,1536]{1,0:T(8,128)(2,1)}), bf16[192,6144]{1,0:T(8,128)(2,1)}) %all-gather.5.cloned.1.call-update) | async-done | bytes 2359312 | tf_op jit(solution)/shard_map/all_gather | solution.py:88
  78.5 1.1 copy-done.9
  80.5 15.9 %all-gather = bf16[192,1024]{0,1:T(8,128)(2,1)S(1)} all-gather(bf16[192,256]{0,1:T(8,128)(2,1)S(1)} %fusion.43), channel_id=2, replica_groups=mesh['groups'=2,'wy'=2,'wc'=2,'expert'=4] {'expert'}, dimensions={1}, use_global_device_ids=true | all-gather | bytes 491520 | tf_op jit(solution)/shard_map/all_gather | solution.py:93
  99.0 2.5 copy-done.10
  101.5 4.0 %maximum_select_fusion = bf16[384,6144]{1,0:T(8,128)(2,1)S(1)} fusion(bf16[192,6144]{1,0:T(8,128)(2,1)} %collective-permute-done.3, bf16[192,6144]{1,0:T(8,128)(2,1)S(1)} %copy-done.10, pred[]{:T(512)S(6)} %eq.14), kind=kLoop, calls=%fused_computation.22 | loop fusion | flops 21233664 | bytes 9437185 | tf_op jit(solution)/shard_map/jit(_where)/select_n | solution.py:98
  105.5 1.3 fusion.52
  107.0 8.1 %fusion.4 = f32[384,1024]{1,0:T(8,128)S(1)} fusion(bf16[384,6144]{1,0:T(8,128)(2,1)S(1)} %maximum_select_fusion, bf16[2,6144,1024]{2,1,0:T(8,128)(2,1)} %param.17), kind=kOutput, calls=%fused_computation.8 | convolution fusion | flops 4831838208 | bytes 18874368 | tf_op jit(solution)/shard_map/dot_general | solution.py:125
  115.1 9.0 %fusion.24 = bf16[384,1024]{1,0:T(8,128)(2,1)} fusion(f32[384,2,1024]{2,0,1:T(8,128)S(1)} %bitcast.114, f32[384,1024]{1,0:T(8,128)S(1)} %fusion.4, bf16[384,6144]{1,0:T(8,128)(2,1)S(1)} %maximum_select_fusion, bf16[2,6144,1024]{2,1,0:T(8,128)(2,1)} %param.18, f32[384]{0:T(512)S(1)} %get-tuple-element.8), kind=kOutput, calls=%fused_computation.30 | convolution fusion | flops 4835377152 | bytes 21235200 | tf_op jit(solution)/shard_map/dot_general | solution.py:129
  124.4 11.1 %fusion.10 = f32[384,1024]{1,0:T(8,128)S(1)} fusion(bf16[384,6144]{1,0:T(8,128)(2,1)} %copy-done.3, bf16[2,6144,1024]{2,1,0:T(8,128)(2,1)} %param.17), kind=kOutput, calls=%fused_computation.14 | convolution fusion | flops 4831838208 | bytes 18874368 | tf_op jit(solution)/shard_map/dot_general | solution.py:125
  135.5 9.1 %fusion.28 = bf16[384,1024]{1,0:T(8,128)(2,1)} fusion(f32[384,2,1024]{2,0,1:T(8,128)S(1)} %bitcast.115, f32[384,1024]{1,0:T(8,128)S(1)} %fusion.10, bf16[384,6144]{1,0:T(8,128)(2,1)S(1)} %copy-done.4, bf16[2,6144,1024]{2,1,0:T(8,128)(2,1)} %param.18, f32[384]{0:T(512)S(1)} %get-tuple-element.7), kind=kOutput, calls=%fused_computation.35 | convolution fusion | flops 4835377152 | bytes 21235200 | tf_op jit(solution)/shard_map/dot_general | solution.py:129
  144.6 41.7 %all-gather.9.cloned.1.call-done = bf16[384,4096]{1,0:T(8,128)(2,1)} async-done(((bf16[384,1024]{1,0:T(8,128)(2,1)}), bf16[384,4096]{1,0:T(8,128)(2,1)}) %all-gather.9.cloned.1.call-update) | async-done | bytes 3145744 | tf_op jit(solution)/shard_map/all_gather | solution.py:135
  186.3 10.0 %fusion = f32[384,1536]{1,0:T(8,128)} fusion(bf16[384,4096]{1,0:T(8,128)(2,1)} %all-gather.9.cloned.1.call-done, bf16[2,4096,1536]{2,1,0:T(8,128)(2,1)} %param.19), kind=kOutput, calls=%fused_computation.4 | convolution fusion | flops 4831838208 | bytes 18087936 | tf_op jit(solution)/shard_map/dot_general | solution.py:136
  196.4 53.7 %all-gather.7.cloned.1.call-done = bf16[384,4096]{1,0:T(8,128)(2,1)} async-done(((bf16[384,1024]{1,0:T(8,128)(2,1)}), bf16[384,4096]{1,0:T(8,128)(2,1)}) %all-gather.7.cloned.1.call-update) | async-done | bytes 3145744 | tf_op jit(solution)/shard_map/all_gather | solution.py:135
  250.1 9.3 %fusion.18 = f32[384,1536]{1,0:T(8,128)S(1)} fusion(f32[384,1536]{1,0:T(8,128)} %fusion, bf16[384,4096]{1,0:T(8,128)(2,1)} %all-gather.7.cloned.1.call-done, bf16[2,4096,1536]{2,1,0:T(8,128)(2,1)} %param.19), kind=kOutput, calls=%fused_computation.24 | convolution fusion | flops 4832428032 | bytes 20447232 | tf_op jit(solution)/shard_map/dot_general | solution.py:136
  259.4 1.4 copy-done.5
  261.0 2.8 collective-permute-done.8
  263.8 2.0 bitcast_add_fusion
  265.9 1.5 collective-permute-start.9
  267.5 13.9 %collective-permute-done.9 = f32[96,1536]{1,0:T(8,128)S(1)} collective-permute-done((f32[96,1536]{1,0:T(8,128)S(1)}, f32[96,1536]{1,0:T(8,128)S(1)}, u32[]{:S(2)}, u32[]{:S(2)}) %collective-permute-start.9) | collective-permute-done | bytes 589856 | tf_op jit(solution)/shard_map/ppermute | solution.py:152
  281.4 0.8 fusion.38
  (69 shorter events, 5.1 us)
Async XLA Ops:
  6.5 90.2 %copy-start = (bf16[8,2,64,1024]{3,2,1,0:T(8,128)(2,1)S(1)}, bf16[8,2,64,1024]{3,2,1,0:T(8,128)(2,1)}, u32[]{:S(2)}) copy-start(bf16[8,2,64,1024]{3,2,1,0:T(8,128)(2,1)} %param.21) | copy-start | bytes 6291460
  6.5 71.8 %all-gather.5.cloned.1.call-start = ((), (), s32[]{:S(2)}) async-start(), calls=%async_computation | async-start | bytes 2949120 | tf_op jit(solution)/shard_map/all_gather | solution.py:88
  6.5 12.3 %collective-permute-start.1 = (bf16[1,128,1536]{2,1,0:T(8,128)(2,1)}, bf16[1,128,1536]{2,1,0:T(8,128)(2,1)S(1)}, u32[]{:S(2)}, u32[]{:S(2)}) collective-permute-start(bf16[1,128,1536]{2,1,0:T(8,128)(2,1)} %param.11), channel_id=1, source_target_pairs={{0,8},{8,0},{1,9},{9,1},{2,10},{10,2},{3,11},{11,3},{4,12},{12,4},... | collective-permute-start | bytes 1179656 | tf_op jit(solution)/shard_map/ppermute | solution.py:44
  9.5 10.2 %collective-permute-start = (bf16[1,128,1536]{2,1,0:T(8,128)(2,1)}, bf16[1,128,1536]{2,1,0:T(8,128)(2,1)S(1)}, u32[]{:S(2)}, u32[]{:S(2)}) collective-permute-start(bf16[1,128,1536]{2,1,0:T(8,128)(2,1)} %param.11), channel_id=1, source_target_pairs={{0,4},{4,0},{1,5},{5,1},{2,6},{6,2},{3,7},{7,3},{8,12},{12,8},{9,1... | collective-permute-start | bytes 1179656 | tf_op jit(solution)/shard_map/ppermute | solution.py:45
  18.8 1.7 collective-permute-start.2
  22.9 23.3 %copy-start.13 = (s32[3]{0:T(128)S(1)}, s32[3]{0:T(128)}, u32[]{:S(2)}) copy-start(s32[3]{0:T(128)} %param.14) | copy-start | bytes 40
  22.9 23.3 %copy-start.2 = (s32[8]{0:T(128)S(1)}, s32[8]{0:T(128)}, u32[]{:S(2)}) copy-start(s32[8]{0:T(128)} %param.15) | copy-start | bytes 100
  25.0 27.1 %copy-start.8 = (bf16[3,128,1536]{2,1,0:T(8,128)(2,1)}, bf16[3,128,1536]{2,1,0:T(8,128)(2,1)S(1)}, u32[]{:S(2)}) copy-start(bf16[3,128,1536]{2,1,0:T(8,128)(2,1)S(1)} %gather_fusion) | copy-start | bytes 3538948
  26.2 160.1 %all-gather.9.cloned.1.call-start = ((), (), s32[]{:S(2)}) async-start(), calls=%async_computation.2 | async-start | bytes 3932160 | tf_op jit(solution)/shard_map/all_gather | solution.py:135
  26.3 20.0 %collective-permute-start.5 = (bf16[2,2,1536,64]{2,3,1,0:T(8,128)(2,1)}, bf16[2,2,1536,64]{2,3,1,0:T(8,128)(2,1)}, u32[]{:S(2)}, u32[]{:S(2)}) collective-permute-start(bf16[2,2,1536,64]{2,3,1,0:T(8,128)(2,1)} %param.20), channel_id=1, source_target_pairs={{0,8},{8,0},{1,9},{9,1},{2,10},{10,2},{3,11},{11,3},{4,12},{12,4},... | collective-permute-start | bytes 2359304 | tf_op jit(solution)/shard_map/ppermute | solution.py:63
  28.1 18.9 %collective-permute-start.4 = (bf16[2,2,1536,64]{2,3,1,0:T(8,128)(2,1)}, bf16[2,2,1536,64]{2,3,1,0:T(8,128)(2,1)}, u32[]{:S(2)}, u32[]{:S(2)}) collective-permute-start(bf16[2,2,1536,64]{2,3,1,0:T(8,128)(2,1)} %param.20), channel_id=1, source_target_pairs={{0,4},{4,0},{1,5},{5,1},{2,6},{6,2},{3,7},{7,3},{8,12},{12,8},{9,1... | collective-permute-start | bytes 2359304 | tf_op jit(solution)/shard_map/ppermute | solution.py:64
  46.2 2.6 collective-permute-start.6
  78.3 1.3 copy-start.9
  78.3 20.7 %collective-permute-start.3 = (bf16[192,6144]{1,0:T(8,128)(2,1)}, bf16[192,6144]{1,0:T(8,128)(2,1)}, u32[]{:S(2)}, u32[]{:S(2)}) collective-permute-start(bf16[192,6144]{1,0:T(8,128)(2,1)} %all-gather.5.cloned.1.call-done), channel_id=1, source_target_pairs={{0,4},{4,0},{1,5},{5,1},{2,6},{6,2},{3,7},{7,3},{8,12},{12,8},{9,1... | collective-permute-start | bytes 7077896 | tf_op jit(solution)/shard_map/ppermute | solution.py:96
  80.1 16.6 %copy-start.12 = (s32[384,2]{0,1:T(2,128)S(1)}, s32[384,2]{0,1:T(2,128)}, u32[]{:S(2)}) copy-start(s32[384,2]{0,1:T(2,128)} %param.13) | copy-start | bytes 9220
  96.6 1.3 collective-permute-start.7
  98.7 2.8 copy-start.10
  98.9 16.2 %copy-start.6 = (f32[3,128,2,1024]{3,1,0,2:T(8,128)}, f32[3,128,2,1024]{3,1,0,2:T(8,128)S(1)}, u32[]{:S(2)}) copy-start(f32[3,128,2,1024]{3,1,0,2:T(8,128)S(1)} %copy.20) | copy-start | bytes 9437188
  98.9 6.6 %copy-start.11 = (bf16[6144,8]{0,1:T(8,128)(2,1)S(1)}, bf16[6144,8]{0,1:T(8,128)(2,1)}, u32[]{:S(2)}) copy-start(bf16[6144,8]{0,1:T(8,128)(2,1)} %param.16) | copy-start | bytes 294916
  105.5 9.6 %copy-start.3 = (bf16[384,6144]{1,0:T(8,128)(2,1)}, bf16[384,6144]{1,0:T(8,128)(2,1)S(1)}, u32[]{:S(2)}) copy-start(bf16[384,6144]{1,0:T(8,128)(2,1)S(1)} %maximum_select_fusion) | copy-start | bytes 14155780
  124.1 125.9 %all-gather.7.cloned.1.call-start = ((), (), s32[]{:S(2)}) async-start(), calls=%async_computation.1 | async-start | bytes 3932160 | tf_op jit(solution)/shard_map/all_gather | solution.py:135
  124.4 11.1 %copy-start.4 = (bf16[384,6144]{1,0:T(8,128)(2,1)S(1)}, bf16[384,6144]{1,0:T(8,128)(2,1)}, u32[]{:S(2)}) copy-start(bf16[384,6144]{1,0:T(8,128)(2,1)} %copy-done.3) | copy-start | bytes 14155780
  124.4 11.1 %copy-start.7 = (f32[3,128,2,1024]{3,1,0,2:T(8,128)S(1)}, f32[3,128,2,1024]{3,1,0,2:T(8,128)}, u32[]{:S(2)}) copy-start(f32[3,128,2,1024]{3,1,0,2:T(8,128)} %copy-done.6) | copy-start | bytes 9437188
  259.4 1.4 copy-start.5
  260.9 2.9 %collective-permute-start.8 = (f32[2,96,1536]{2,1,0:T(8,128)S(1)}, f32[2,96,1536]{2,1,0:T(8,128)S(1)}, u32[]{:S(2)}, u32[]{:S(2)}) collective-permute-start(f32[2,96,1536]{2,1,0:T(8,128)S(1)} %select_bitcast_fusion), channel_id=1, source_target_pairs={{0,4},{4,0},{1,5},{5,1},{2,6},{6,2},{3,7},{7,3},{8,12},{12,8},{9,1... | collective-permute-start | bytes 3538952 | tf_op jit(solution)/shard_map/ppermute | solution.py:147
  263.8 18.4 %copy-start.1 = (bf16[8,2,64,1024]{3,2,1,0:T(8,128)(2,1)S(1)}, bf16[8,2,64,1024]{3,2,1,0:T(8,128)(2,1)}, u32[]{:S(2)}) copy-start(bf16[8,2,64,1024]{3,2,1,0:T(8,128)(2,1)} %param.21) | copy-start | bytes 6291460
  265.9 15.4 %collective-permute-start.9 = (f32[96,1536]{1,0:T(8,128)S(1)}, f32[96,1536]{1,0:T(8,128)S(1)}, u32[]{:S(2)}, u32[]{:S(2)}) collective-permute-start(f32[96,1536]{1,0:T(8,128)S(1)} %select_bitcast_fusion.1), channel_id=1, source_target_pairs={{0,8},{8,0},{1,9},{9,1},{2,10},{10,2},{3,11},{11,3},{4,12},{12,4},... | collective-permute-start | bytes 1769480 | tf_op jit(solution)/shard_map/ppermute | solution.py:152
Sparse Core Ops, SparseCore 0:
  26.3 51.9 all-gather.4
  124.3 62.0 all-gather.8
  187.9 62.1 all-gather.6

commit v14 on v13

--- a/solution.py
+++ b/solution.py
@@ -149,7 +149,8 @@
         chip = lax.axis_index("wy")
         mine = jnp.where(chip == 0, chip_sum[0], chip_sum[1])
         away = jnp.where(chip == 0, chip_sum[1], chip_sum[0])
-        return mine + lax.ppermute(away, "wy", [(0, 1), (1, 0)])
+        arrived = lax.ppermute(away.astype(jnp.bfloat16), "wy", [(0, 1), (1, 0)])
+        return mine + arrived.astype(jnp.float32)
     return lax.psum_scatter(chip_sum, "wy", scatter_dimension=0, tiled=True).reshape(block, -1)
 
 

time: 289 us -> 283 us (0.979)
  waiting for transfers between devices: 167 us -> 160 us
    ppermute x1, waiting for transfers between devices: 13.9 us -> 7.58 us  [reduce_rows(): arrived = lax.ppermute(away.astype(jnp.bfloat16), 'wy', [(0, 1), (1, 0)])]
where the time goes in v14:
time: 283 us; the launch traced here: 282 us
  waiting for transfers between devices  160 us (57%)
  matrix products  59.1 us (21%)
  blocking collectives  15.9 us (6%)
  other arithmetic  15.3 us (5%)
  between operations  13.5 us (5%)
  local copies, waits for them, and re-layouts  11.5 us (4%)
  starting transfers between devices  6.73 us (2%)
    all_gather x2, waiting for transfers between devices, per_device(): gathered = lax.all_gather(hidden, 'expert', axis=1, tiled=True)  95.4 us
    all_gather x1, waiting for transfers between devices, per_device(): mine = lax.all_gather(mine_q, 'expert', axis=1, tiled=True)  23.7 us
    dot_general x2, matrix products, per_device(): jnp.dot(gathered, down_weight[expert_number], preferred_element_type=jnp....  19.3 us
    dot_general x2, matrix products, per_device(): jnp.dot(input_rows, gate_weight[expert_number], preferred_element_type=jn...  19.2 us
    ppermute x1, waiting for transfers between devices, per_device(): from_chip = lax.ppermute(adapter_down_weight, 'wy', swap)  18.2 us
    dot_general x2, matrix products, per_device(): jnp.dot(input_rows, up_weight[expert_number], preferred_element_type=jnp....  18.1 us
    all_gather x1, blocking collectives, per_device(): lax.all_gather(rank_q, 'expert', axis=1, tiled=False).astype(jnp.float32)  15.9 us
    ppermute x1, waiting for transfers between devices, per_device(): slot_chip = lax.ppermute(prompts, 'wy', pair)  9.32 us
  transfers between devices with their start and end apart: 13, of which 10 were waited for; matrix products, arithmetic and copies ran while one was open for 14% of the time, Pallas kernels for 0%

profile of v14, /device:TPU:0, one launch (start us, length us, event | category | flops | bytes accessed | tf_op | source)
XLA Modules:
  0.0 282.4 jit_solution(12810220067142073298)
XLA Ops:
  6.5 3.0 %collective-permute-start.1 = (bf16[1,128,1536]{2,1,0:T(8,128)(2,1)}, bf16[1,128,1536]{2,1,0:T(8,128)(2,1)S(1)}, u32[]{:S(2)}, u32[]{:S(2)}) collective-permute-start(bf16[1,128,1536]{2,1,0:T(8,128)(2,1)} %param.11), channel_id=1, source_target_pairs={{0,8},{8,0},{1,9},{9,1},{2,10},{10,2},{3,11},{11,3},{4,12},{12,4},... | collective-permute-start | bytes 1179656 | tf_op jit(solution)/shard_map/ppermute | solution.py:44
  9.5 9.3 %collective-permute-done.1 = bf16[1,128,1536]{2,1,0:T(8,128)(2,1)S(1)} collective-permute-done((bf16[1,128,1536]{2,1,0:T(8,128)(2,1)}, bf16[1,128,1536]{2,1,0:T(8,128)(2,1)S(1)}, u32[]{:S(2)}, u32[]{:S(2)}) %collective-permute-start.1) | collective-permute-done | bytes 393248 | tf_op jit(solution)/shard_map/ppermute | solution.py:44
  18.8 0.7 compare_and_fusion.2
  19.7 0.9 collective-permute-done.2
  20.6 2.4 pad_maximum_fusion.1
  22.9 2.1 gather_fusion
  25.0 1.2 dynamic-slice_select_fusion
  26.3 1.8 collective-permute-start.5
  28.1 18.2 %collective-permute-done.5 = bf16[2,2,1536,64]{2,3,1,0:T(8,128)(2,1)} collective-permute-done((bf16[2,2,1536,64]{2,3,1,0:T(8,128)(2,1)}, bf16[2,2,1536,64]{2,3,1,0:T(8,128)(2,1)}, u32[]{:S(2)}, u32[]{:S(2)}) %collective-permute-start.5) | collective-permute-done | bytes 786464 | tf_op jit(solution)/shard_map/ppermute | solution.py:63
  47.0 1.9 collective-permute-done.6
  48.9 3.2 %pad_maximum_fusion = bf16[4,2,2,1536,64]{3,4,2,1,0:T(8,128)(2,1)} fusion(bf16[1,2,2,1536,64]{3,4,2,1,0:T(8,128)(2,1)} %bitcast.9, bf16[1,2,2,1536,64]{3,4,2,1,0:T(8,128)(2,1)} %bitcast.8, bf16[1,2,2,1536,64]{3,4,2,1,0:T(8,128)(2,1)} %bitcast.7, bf16[1,2,2,1536,64]{3,4,2,1,0:T(8,128)(2,1)} %bitcast.119), kind=kLoop, calls=%fused_computation.23 | loop fusion | flops 4718592 | bytes 6291456 | tf_op jit(solution)/shard_map/stack | solution.py:66
  52.1 2.5 gather_fusion.3
  54.6 23.7 %all-gather.5.cloned.1.call-done = bf16[192,6144]{1,0:T(8,128)(2,1)} async-done(((bf16[192,1536]{1,0:T(8,128)(2,1)}), bf16[192,6144]{1,0:T(8,128)(2,1)}) %all-gather.5.cloned.1.call-update) | async-done | bytes 2359312 | tf_op jit(solution)/shard_map/all_gather | solution.py:88
  78.5 1.1 copy-done.9
  80.5 15.9 %all-gather = bf16[192,1024]{0,1:T(8,128)(2,1)S(1)} all-gather(bf16[192,256]{0,1:T(8,128)(2,1)S(1)} %fusion.44), channel_id=2, replica_groups=mesh['groups'=2,'wy'=2,'wc'=2,'expert'=4] {'expert'}, dimensions={1}, use_global_device_ids=true | all-gather | bytes 491520 | tf_op jit(solution)/shard_map/all_gather | solution.py:93
  99.0 2.5 copy-done.10
  101.5 4.0 %maximum_select_fusion = bf16[384,6144]{1,0:T(8,128)(2,1)S(1)} fusion(bf16[192,6144]{1,0:T(8,128)(2,1)} %collective-permute-done.3, bf16[192,6144]{1,0:T(8,128)(2,1)S(1)} %copy-done.10, pred[]{:T(512)S(6)} %eq.14), kind=kLoop, calls=%fused_computation.22 | loop fusion | flops 21233664 | bytes 9437185 | tf_op jit(solution)/shard_map/jit(_where)/select_n | solution.py:98
  105.5 1.3 fusion.53
  107.0 8.1 %fusion.4 = f32[384,1024]{1,0:T(8,128)S(1)} fusion(bf16[384,6144]{1,0:T(8,128)(2,1)S(1)} %maximum_select_fusion, bf16[2,6144,1024]{2,1,0:T(8,128)(2,1)} %param.17), kind=kOutput, calls=%fused_computation.8 | convolution fusion | flops 4831838208 | bytes 18874368 | tf_op jit(solution)/shard_map/dot_general | solution.py:125
  115.1 9.0 %fusion.24 = bf16[384,1024]{1,0:T(8,128)(2,1)} fusion(f32[384,2,1024]{2,0,1:T(8,128)S(1)} %bitcast.114, f32[384,1024]{1,0:T(8,128)S(1)} %fusion.4, bf16[384,6144]{1,0:T(8,128)(2,1)S(1)} %maximum_select_fusion, bf16[2,6144,1024]{2,1,0:T(8,128)(2,1)} %param.18, f32[384]{0:T(512)S(1)} %get-tuple-element.8), kind=kOutput, calls=%fused_computation.30 | convolution fusion | flops 4835377152 | bytes 21235200 | tf_op jit(solution)/shard_map/dot_general | solution.py:129
  124.4 11.1 %fusion.10 = f32[384,1024]{1,0:T(8,128)S(1)} fusion(bf16[384,6144]{1,0:T(8,128)(2,1)} %copy-done.3, bf16[2,6144,1024]{2,1,0:T(8,128)(2,1)} %param.17), kind=kOutput, calls=%fused_computation.14 | convolution fusion | flops 4831838208 | bytes 18874368 | tf_op jit(solution)/shard_map/dot_general | solution.py:125
  135.5 9.1 %fusion.28 = bf16[384,1024]{1,0:T(8,128)(2,1)} fusion(f32[384,2,1024]{2,0,1:T(8,128)S(1)} %bitcast.115, f32[384,1024]{1,0:T(8,128)S(1)} %fusion.10, bf16[384,6144]{1,0:T(8,128)(2,1)S(1)} %copy-done.4, bf16[2,6144,1024]{2,1,0:T(8,128)(2,1)} %param.18, f32[384]{0:T(512)S(1)} %get-tuple-element.7), kind=kOutput, calls=%fused_computation.35 | convolution fusion | flops 4835377152 | bytes 21235200 | tf_op jit(solution)/shard_map/dot_general | solution.py:129
  144.6 41.7 %all-gather.9.cloned.1.call-done = bf16[384,4096]{1,0:T(8,128)(2,1)} async-done(((bf16[384,1024]{1,0:T(8,128)(2,1)}), bf16[384,4096]{1,0:T(8,128)(2,1)}) %all-gather.9.cloned.1.call-update) | async-done | bytes 3145744 | tf_op jit(solution)/shard_map/all_gather | solution.py:135
  186.3 10.0 %fusion = f32[384,1536]{1,0:T(8,128)} fusion(bf16[384,4096]{1,0:T(8,128)(2,1)} %all-gather.9.cloned.1.call-done, bf16[2,4096,1536]{2,1,0:T(8,128)(2,1)} %param.19), kind=kOutput, calls=%fused_computation.4 | convolution fusion | flops 4831838208 | bytes 18087936 | tf_op jit(solution)/shard_map/dot_general | solution.py:136
  196.4 53.7 %all-gather.7.cloned.1.call-done = bf16[384,4096]{1,0:T(8,128)(2,1)} async-done(((bf16[384,1024]{1,0:T(8,128)(2,1)}), bf16[384,4096]{1,0:T(8,128)(2,1)}) %all-gather.7.cloned.1.call-update) | async-done | bytes 3145744 | tf_op jit(solution)/shard_map/all_gather | solution.py:135
  250.1 9.3 %fusion.18 = f32[384,1536]{1,0:T(8,128)S(1)} fusion(f32[384,1536]{1,0:T(8,128)} %fusion, bf16[384,4096]{1,0:T(8,128)(2,1)} %all-gather.7.cloned.1.call-done, bf16[2,4096,1536]{2,1,0:T(8,128)(2,1)} %param.19), kind=kOutput, calls=%fused_computation.24 | convolution fusion | flops 4832428032 | bytes 20447232 | tf_op jit(solution)/shard_map/dot_general | solution.py:136
  259.4 1.4 copy-done.5
  261.0 2.8 %collective-permute-done.8 = f32[2,96,1536]{2,1,0:T(8,128)S(1)} collective-permute-done((f32[2,96,1536]{2,1,0:T(8,128)S(1)}, f32[2,96,1536]{2,1,0:T(8,128)S(1)}, u32[]{:S(2)}, u32[]{:S(2)}) %collective-permute-start.8) | collective-permute-done | bytes 1179680 | tf_op jit(solution)/shard_map/ppermute | solution.py:147
  263.8 2.0 bitcast_add_fusion
  265.9 1.5 collective-permute-start.9
  267.5 7.6 %collective-permute-done.9 = bf16[96,1536]{1,0:T(8,128)(2,1)S(1)} collective-permute-done((bf16[96,1536]{1,0:T(8,128)(2,1)S(1)}, bf16[96,1536]{1,0:T(8,128)(2,1)S(1)}, u32[]{:S(2)}, u32[]{:S(2)}) %collective-permute-start.9) | collective-permute-done | bytes 294944 | tf_op jit(solution)/shard_map/ppermute | solution.py:152
  275.1 0.8 fusion.38
  (69 shorter events, 5.1 us)
Async XLA Ops:
  6.5 90.2 %copy-start = (bf16[8,2,64,1024]{3,2,1,0:T(8,128)(2,1)S(1)}, bf16[8,2,64,1024]{3,2,1,0:T(8,128)(2,1)}, u32[]{:S(2)}) copy-start(bf16[8,2,64,1024]{3,2,1,0:T(8,128)(2,1)} %param.21) | copy-start | bytes 6291460
  6.5 71.8 %all-gather.5.cloned.1.call-start = ((), (), s32[]{:S(2)}) async-start(), calls=%async_computation | async-start | bytes 2949120 | tf_op jit(solution)/shard_map/all_gather | solution.py:88
  6.5 12.3 %collective-permute-start.1 = (bf16[1,128,1536]{2,1,0:T(8,128)(2,1)}, bf16[1,128,1536]{2,1,0:T(8,128)(2,1)S(1)}, u32[]{:S(2)}, u32[]{:S(2)}) collective-permute-start(bf16[1,128,1536]{2,1,0:T(8,128)(2,1)} %param.11), channel_id=1, source_target_pairs={{0,8},{8,0},{1,9},{9,1},{2,10},{10,2},{3,11},{11,3},{4,12},{12,4},... | collective-permute-start | bytes 1179656 | tf_op jit(solution)/shard_map/ppermute | solution.py:44
  9.5 10.2 %collective-permute-start = (bf16[1,128,1536]{2,1,0:T(8,128)(2,1)}, bf16[1,128,1536]{2,1,0:T(8,128)(2,1)S(1)}, u32[]{:S(2)}, u32[]{:S(2)}) collective-permute-start(bf16[1,128,1536]{2,1,0:T(8,128)(2,1)} %param.11), channel_id=1, source_target_pairs={{0,4},{4,0},{1,5},{5,1},{2,6},{6,2},{3,7},{7,3},{8,12},{12,8},{9,1... | collective-permute-start | bytes 1179656 | tf_op jit(solution)/shard_map/ppermute | solution.py:45
  18.8 1.7 collective-permute-start.2
  22.9 23.3 %copy-start.13 = (s32[3]{0:T(128)S(1)}, s32[3]{0:T(128)}, u32[]{:S(2)}) copy-start(s32[3]{0:T(128)} %param.14) | copy-start | bytes 40
  22.9 23.3 %copy-start.2 = (s32[8]{0:T(128)S(1)}, s32[8]{0:T(128)}, u32[]{:S(2)}) copy-start(s32[8]{0:T(128)} %param.15) | copy-start | bytes 100
  25.0 27.1 %copy-start.8 = (bf16[3,128,1536]{2,1,0:T(8,128)(2,1)}, bf16[3,128,1536]{2,1,0:T(8,128)(2,1)S(1)}, u32[]{:S(2)}) copy-start(bf16[3,128,1536]{2,1,0:T(8,128)(2,1)S(1)} %gather_fusion) | copy-start | bytes 3538948
  26.2 160.1 %all-gather.9.cloned.1.call-start = ((), (), s32[]{:S(2)}) async-start(), calls=%async_computation.2 | async-start | bytes 3932160 | tf_op jit(solution)/shard_map/all_gather | solution.py:135
  26.3 20.0 %collective-permute-start.5 = (bf16[2,2,1536,64]{2,3,1,0:T(8,128)(2,1)}, bf16[2,2,1536,64]{2,3,1,0:T(8,128)(2,1)}, u32[]{:S(2)}, u32[]{:S(2)}) collective-permute-start(bf16[2,2,1536,64]{2,3,1,0:T(8,128)(2,1)} %param.20), channel_id=1, source_target_pairs={{0,8},{8,0},{1,9},{9,1},{2,10},{10,2},{3,11},{11,3},{4,12},{12,4},... | collective-permute-start | bytes 2359304 | tf_op jit(solution)/shard_map/ppermute | solution.py:63
  28.1 18.9 %collective-permute-start.4 = (bf16[2,2,1536,64]{2,3,1,0:T(8,128)(2,1)}, bf16[2,2,1536,64]{2,3,1,0:T(8,128)(2,1)}, u32[]{:S(2)}, u32[]{:S(2)}) collective-permute-start(bf16[2,2,1536,64]{2,3,1,0:T(8,128)(2,1)} %param.20), channel_id=1, source_target_pairs={{0,4},{4,0},{1,5},{5,1},{2,6},{6,2},{3,7},{7,3},{8,12},{12,8},{9,1... | collective-permute-start | bytes 2359304 | tf_op jit(solution)/shard_map/ppermute | solution.py:64
  46.2 2.6 collective-permute-start.6
  78.3 1.3 copy-start.9
  78.3 20.7 %collective-permute-start.3 = (bf16[192,6144]{1,0:T(8,128)(2,1)}, bf16[192,6144]{1,0:T(8,128)(2,1)}, u32[]{:S(2)}, u32[]{:S(2)}) collective-permute-start(bf16[192,6144]{1,0:T(8,128)(2,1)} %all-gather.5.cloned.1.call-done), channel_id=1, source_target_pairs={{0,4},{4,0},{1,5},{5,1},{2,6},{6,2},{3,7},{7,3},{8,12},{12,8},{9,1... | collective-permute-start | bytes 7077896 | tf_op jit(solution)/shard_map/ppermute | solution.py:96
  80.1 16.6 %copy-start.12 = (s32[384,2]{0,1:T(2,128)S(1)}, s32[384,2]{0,1:T(2,128)}, u32[]{:S(2)}) copy-start(s32[384,2]{0,1:T(2,128)} %param.13) | copy-start | bytes 9220
  96.6 1.3 collective-permute-start.7
  98.7 2.8 copy-start.10
  98.9 16.2 %copy-start.6 = (f32[3,128,2,1024]{3,1,0,2:T(8,128)}, f32[3,128,2,1024]{3,1,0,2:T(8,128)S(1)}, u32[]{:S(2)}) copy-start(f32[3,128,2,1024]{3,1,0,2:T(8,128)S(1)} %copy.20) | copy-start | bytes 9437188
  98.9 6.6 %copy-start.11 = (bf16[6144,8]{0,1:T(8,128)(2,1)S(1)}, bf16[6144,8]{0,1:T(8,128)(2,1)}, u32[]{:S(2)}) copy-start(bf16[6144,8]{0,1:T(8,128)(2,1)} %param.16) | copy-start | bytes 294916
  105.5 9.6 %copy-start.3 = (bf16[384,6144]{1,0:T(8,128)(2,1)}, bf16[384,6144]{1,0:T(8,128)(2,1)S(1)}, u32[]{:S(2)}) copy-start(bf16[384,6144]{1,0:T(8,128)(2,1)S(1)} %maximum_select_fusion) | copy-start | bytes 14155780
  124.1 125.9 %all-gather.7.cloned.1.call-start = ((), (), s32[]{:S(2)}) async-start(), calls=%async_computation.1 | async-start | bytes 3932160 | tf_op jit(solution)/shard_map/all_gather | solution.py:135
  124.4 11.1 %copy-start.4 = (bf16[384,6144]{1,0:T(8,128)(2,1)S(1)}, bf16[384,6144]{1,0:T(8,128)(2,1)}, u32[]{:S(2)}) copy-start(bf16[384,6144]{1,0:T(8,128)(2,1)} %copy-done.3) | copy-start | bytes 14155780
  124.4 11.1 %copy-start.7 = (f32[3,128,2,1024]{3,1,0,2:T(8,128)S(1)}, f32[3,128,2,1024]{3,1,0,2:T(8,128)}, u32[]{:S(2)}) copy-start(f32[3,128,2,1024]{3,1,0,2:T(8,128)} %copy-done.6) | copy-start | bytes 9437188
  259.4 1.4 copy-start.5
  260.9 2.9 %collective-permute-start.8 = (f32[2,96,1536]{2,1,0:T(8,128)S(1)}, f32[2,96,1536]{2,1,0:T(8,128)S(1)}, u32[]{:S(2)}, u32[]{:S(2)}) collective-permute-start(f32[2,96,1536]{2,1,0:T(8,128)S(1)} %select_bitcast_fusion), channel_id=1, source_target_pairs={{0,4},{4,0},{1,5},{5,1},{2,6},{6,2},{3,7},{7,3},{8,12},{12,8},{9,1... | collective-permute-start | bytes 3538952 | tf_op jit(solution)/shard_map/ppermute | solution.py:147
  263.8 12.0 %copy-start.1 = (bf16[8,2,64,1024]{3,2,1,0:T(8,128)(2,1)S(1)}, bf16[8,2,64,1024]{3,2,1,0:T(8,128)(2,1)}, u32[]{:S(2)}) copy-start(bf16[8,2,64,1024]{3,2,1,0:T(8,128)(2,1)} %param.21) | copy-start | bytes 6291460
  265.9 9.1 %collective-permute-start.9 = (bf16[96,1536]{1,0:T(8,128)(2,1)S(1)}, bf16[96,1536]{1,0:T(8,128)(2,1)S(1)}, u32[]{:S(2)}, u32[]{:S(2)}) collective-permute-start(bf16[96,1536]{1,0:T(8,128)(2,1)S(1)} %fusion.42), channel_id=1, source_target_pairs={{0,8},{8,0},{1,9},{9,1},{2,10},{10,2},{3,11},{11,3},{4,12},{12,4},... | collective-permute-start | bytes 884744 | tf_op jit(solution)/shard_map/ppermute | solution.py:152
Sparse Core Ops, SparseCore 0:
  26.3 51.9 all-gather.4
  124.3 62.0 all-gather.8
  187.9 62.1 all-gather.6

commit v15 on v13

--- a/solution.py
+++ b/solution.py
@@ -133,9 +133,35 @@
             weight[:, expert_number, None] * jax.nn.silu(gate_pre) * up_value
         ).astype(jnp.bfloat16)
         gathered = lax.all_gather(hidden, "expert", axis=1, tiled=True)
+        if expert_number == window - 1 and lax.axis_size("wy") == 2 and cores == 2:
+            return split_last(gathered, down_weight[expert_number], running, core)
         part = jnp.dot(gathered, down_weight[expert_number], preferred_element_type=jnp.float32)
         running = part if running is None else running + part
     return reduce_rows(running, core, cores).astype(jnp.bfloat16)
+
+
+def split_last(gathered, down, running, core):
+    chip = lax.axis_index("wy")
+    span_rows = gathered.shape[0] // 2
+    block = span_rows // 2
+    pair = [(0, 1), (1, 0)]
+
+    def chip_rows(which, source=gathered):
+        part = jnp.dot(
+            lax.dynamic_slice_in_dim(source, which * span_rows, span_rows, 0),
+            down,
+            preferred_element_type=jnp.float32,
+        )
+        if running is not None:
+            part = lax.dynamic_slice_in_dim(running, which * span_rows, span_rows, 0) + part
+        keep = lax.dynamic_slice_in_dim(part, core * block, block, 0)
+        send = lax.dynamic_slice_in_dim(part, (1 - core) * block, block, 0)
+        return keep + lax.ppermute(send, "wc", pair)
+
+    away_sum = chip_rows(1 - chip)
+    away = lax.ppermute(away_sum, "wy", pair)
+    gathered, _ = lax.optimization_barrier((gathered, away_sum))
+    return (chip_rows(chip, gathered) + away).astype(jnp.bfloat16)
 
 
 def reduce_rows(running, core, cores):

time: 289 us -> 283 us (0.979)
  waiting for transfers between devices: 167 us -> 158 us
  matrix products: 59.1 us -> 66 us
    dot_general x0 -> x2, matrix products: none -> 15.9 us  [chip_rows(): jnp.dot(lax.dynamic_slice_in_dim(source, which * span_rows, span_rows, 0)...]
    dot_general x2 -> x1, matrix products: 19.3 us -> 10 us  [per_device(): jnp.dot(gathered, down_weight[expert_number], preferred_element_type=jnp....]
    ppermute x2 -> x3, waiting for transfers between devices: 16.7 us -> 7.7 us  [the longest x1 5.7 us: split_last(): away = lax.ppermute(away_sum, 'wy', pair)]
  transfers between devices with their start and end apart: 13 -> 14, of which waited for: 10 -> 10; matrix products, arithmetic and copies ran while one was open for 14% -> 17% of each run, Pallas kernels for 0% -> 0%
where the time goes in v15:
time: 283 us
  waiting for transfers between devices  158 us (56%)
  matrix products  66 us (23%)
  blocking collectives  15.9 us (6%)
  between operations  13.5 us (5%)
  other arithmetic  13.1 us (5%)
  local copies, waits for them, and re-layouts  10.1 us (4%)
  starting transfers between devices  6.81 us (2%)
    all_gather x2, waiting for transfers between devices, per_device(): gathered = lax.all_gather(hidden, 'expert', axis=1, tiled=True)  95.3 us
    all_gather x1, waiting for transfers between devices, per_device(): mine = lax.all_gather(mine_q, 'expert', axis=1, tiled=True)  23.7 us
    dot_general x2, matrix products, per_device(): jnp.dot(input_rows, gate_weight[expert_number], preferred_element_type=jn...  19.4 us
    ppermute x1, waiting for transfers between devices, per_device(): from_chip = lax.ppermute(adapter_down_weight, 'wy', swap)  18.2 us
    dot_general x2, matrix products, per_device(): jnp.dot(input_rows, up_weight[expert_number], preferred_element_type=jnp....  18.1 us
    dot_general x2, matrix products, chip_rows(): jnp.dot(lax.dynamic_slice_in_dim(source, which * span_rows, span_rows, 0)...  15.9 us
    all_gather x1, blocking collectives, per_device(): lax.all_gather(rank_q, 'expert', axis=1, tiled=False).astype(jnp.float32)  15.9 us
    dot_general x1, matrix products, per_device(): jnp.dot(gathered, down_weight[expert_number], preferred_element_type=jnp....  10 us
  transfers between devices with their start and end apart: 14, of which 10 were waited for; matrix products, arithmetic and copies ran while one was open for 17% of the time, Pallas kernels for 0%

profile of v15, /device:TPU:0, one launch (start us, length us, event | category | flops | bytes accessed | tf_op | source)
XLA Modules:
  0.0 283.0 jit_solution(9302136341838518646)
XLA Ops:
  6.5 3.0 %collective-permute-start.1 = (bf16[1,128,1536]{2,1,0:T(8,128)(2,1)}, bf16[1,128,1536]{2,1,0:T(8,128)(2,1)S(1)}, u32[]{:S(2)}, u32[]{:S(2)}) collective-permute-start(bf16[1,128,1536]{2,1,0:T(8,128)(2,1)} %param.11), channel_id=1, source_target_pairs={{0,8},{8,0},{1,9},{9,1},{2,10},{10,2},{3,11},{11,3},{4,12},{12,4},... | collective-permute-start | bytes 1179656 | tf_op jit(solution)/shard_map/ppermute | solution.py:44
  9.5 9.3 %collective-permute-done.1 = bf16[1,128,1536]{2,1,0:T(8,128)(2,1)S(1)} collective-permute-done((bf16[1,128,1536]{2,1,0:T(8,128)(2,1)}, bf16[1,128,1536]{2,1,0:T(8,128)(2,1)S(1)}, u32[]{:S(2)}, u32[]{:S(2)}) %collective-permute-start.1) | collective-permute-done | bytes 393248 | tf_op jit(solution)/shard_map/ppermute | solution.py:44
  18.8 0.7 compare_and_fusion.2
  19.7 0.9 collective-permute-done.2
  20.6 2.4 pad_maximum_fusion.1
  22.9 2.1 gather_fusion
  25.0 1.2 dynamic-slice_select_fusion
  26.3 1.8 collective-permute-start.5
  28.1 18.2 %collective-permute-done.5 = bf16[2,2,1536,64]{2,3,1,0:T(8,128)(2,1)} collective-permute-done((bf16[2,2,1536,64]{2,3,1,0:T(8,128)(2,1)}, bf16[2,2,1536,64]{2,3,1,0:T(8,128)(2,1)}, u32[]{:S(2)}, u32[]{:S(2)}) %collective-permute-start.5) | collective-permute-done | bytes 786464 | tf_op jit(solution)/shard_map/ppermute | solution.py:63
  46.3 0.6 gather_fusion.2
  47.0 1.9 collective-permute-done.6
  48.9 3.2 %pad_maximum_fusion = bf16[4,2,2,1536,64]{3,4,2,1,0:T(8,128)(2,1)} fusion(bf16[1,2,2,1536,64]{3,4,2,1,0:T(8,128)(2,1)} %bitcast.9, bf16[1,2,2,1536,64]{3,4,2,1,0:T(8,128)(2,1)} %bitcast.8, bf16[1,2,2,1536,64]{3,4,2,1,0:T(8,128)(2,1)} %bitcast.7, bf16[1,2,2,1536,64]{3,4,2,1,0:T(8,128)(2,1)} %bitcast.97), kind=kLoop, calls=%fused_computation.26 | loop fusion | flops 4718592 | bytes 6291456 | tf_op jit(solution)/shard_map/stack | solution.py:66
  52.1 2.5 gather_fusion.3
  54.6 23.7 %all-gather.5.cloned.1.call-done = bf16[192,6144]{1,0:T(8,128)(2,1)} async-done(((bf16[192,1536]{1,0:T(8,128)(2,1)}), bf16[192,6144]{1,0:T(8,128)(2,1)}) %all-gather.5.cloned.1.call-update) | async-done | bytes 2359312 | tf_op jit(solution)/shard_map/all_gather | solution.py:88
  78.5 1.1 copy-done.8
  80.5 15.9 %all-gather = bf16[192,1024]{0,1:T(8,128)(2,1)S(1)} all-gather(bf16[192,256]{0,1:T(8,128)(2,1)S(1)} %fusion.50), channel_id=2, replica_groups=mesh['groups'=2,'wy'=2,'wc'=2,'expert'=4] {'expert'}, dimensions={1}, use_global_device_ids=true | all-gather | bytes 491520 | tf_op jit(solution)/shard_map/all_gather | solution.py:93
  99.0 2.5 copy-done.9
  101.5 4.0 %maximum_select_fusion = bf16[384,6144]{1,0:T(8,128)(2,1)S(1)} fusion(bf16[192,6144]{1,0:T(8,128)(2,1)} %collective-permute-done.3, bf16[192,6144]{1,0:T(8,128)(2,1)S(1)} %copy-done.9, pred[]{:T(512)S(6)} %eq.23), kind=kLoop, calls=%fused_computation.25 | loop fusion | flops 21233664 | bytes 9437185 | tf_op jit(solution)/shard_map/jit(_where)/select_n | solution.py:98
  105.5 1.3 fusion.61
  107.0 8.1 %fusion.12 = f32[384,1024]{1,0:T(8,128)S(1)} fusion(bf16[384,6144]{1,0:T(8,128)(2,1)S(1)} %maximum_select_fusion, bf16[2,6144,1024]{2,1,0:T(8,128)(2,1)} %param.17), kind=kOutput, calls=%fused_computation.16 | convolution fusion | flops 4831838208 | bytes 18874368 | tf_op jit(solution)/shard_map/dot_general | solution.py:125
  115.1 9.1 %fusion.34 = bf16[384,1024]{1,0:T(8,128)(2,1)} fusion(f32[384,2,1024]{2,0,1:T(8,128)S(1)} %bitcast.92, f32[384,1024]{1,0:T(8,128)S(1)} %fusion.12, bf16[384,6144]{1,0:T(8,128)(2,1)S(1)} %maximum_select_fusion, bf16[2,6144,1024]{2,1,0:T(8,128)(2,1)} %param.18, f32[384]{0:T(512)S(1)} %get-tuple-element.9), kind=kOutput, calls=%fused_computation.39 | convolution fusion | flops 4835377152 | bytes 21235200 | tf_op jit(solution)/shard_map/dot_general | solution.py:129
  124.5 11.3 %fusion.6 = f32[384,1024]{1,0:T(8,128)S(1)} fusion(bf16[384,6144]{1,0:T(8,128)(2,1)} %copy-done.3, bf16[2,6144,1024]{2,1,0:T(8,128)(2,1)} %param.17), kind=kOutput, calls=%fused_computation.10 | convolution fusion | flops 4831838208 | bytes 18874368 | tf_op jit(solution)/shard_map/dot_general | solution.py:125
  135.8 9.0 %fusion.30 = bf16[384,1024]{1,0:T(8,128)(2,1)} fusion(f32[384,2,1024]{2,0,1:T(8,128)S(1)} %bitcast.93, f32[384,1024]{1,0:T(8,128)S(1)} %fusion.6, bf16[384,6144]{1,0:T(8,128)(2,1)S(1)} %copy-done.4, bf16[2,6144,1024]{2,1,0:T(8,128)(2,1)} %param.18, f32[384]{0:T(512)S(1)} %get-tuple-element.10), kind=kOutput, calls=%fused_computation.34 | convolution fusion | flops 4835377152 | bytes 21235200 | tf_op jit(solution)/shard_map/dot_general | solution.py:129
  144.8 41.6 %all-gather.7.cloned.1.call-done = bf16[384,4096]{1,0:T(8,128)(2,1)} async-done(((bf16[384,1024]{1,0:T(8,128)(2,1)}), bf16[384,4096]{1,0:T(8,128)(2,1)}) %all-gather.7.cloned.1.call-update) | async-done | bytes 3145744 | tf_op jit(solution)/shard_map/all_gather | solution.py:135
  186.4 10.0 %fusion.8 = f32[384,1536]{1,0:T(8,128)} fusion(bf16[384,4096]{1,0:T(8,128)(2,1)} %all-gather.7.cloned.1.call-done, bf16[2,4096,1536]{2,1,0:T(8,128)(2,1)} %param.19), kind=kOutput, calls=%fused_computation.12 | convolution fusion | flops 4831838208 | bytes 18087936 | tf_op jit(solution)/shard_map/dot_general | solution.py:138
  196.4 53.7 %all-gather.9.cloned.1.call-done = bf16[384,4096]{1,0:T(8,128)(2,1)} async-done(((bf16[384,1024]{1,0:T(8,128)(2,1)}), bf16[384,4096]{1,0:T(8,128)(2,1)}) %all-gather.9.cloned.1.call-update) | async-done | bytes 3145744 | tf_op jit(solution)/shard_map/all_gather | solution.py:135
  250.2 7.9 %fusion.21 = f32[192,1536]{1,0:T(8,128)S(1)} fusion(bf16[2,4096,1536]{2,1,0:T(8,128)(2,1)} %param.19, bf16[384,4096]{1,0:T(8,128)(2,1)} %all-gather.9.cloned.1.call-done, s32[]{:T(128)S(6)} %select_n.125, f32[384,1536]{1,0:T(8,128)} %fusion.8), kind=kOutput, calls=%fused_computation.27 | convolution fusion | flops 2416214016 | bytes 16516096 | tf_op jit(solution)/shard_map/dot_general | solution.py:150
  258.2 2.0 collective-permute-done.8
  260.3 1.5 collective-permute-start.10
  261.8 8.0 %fusion.24 = f32[192,1536]{1,0:T(8,128)S(1)} fusion(bf16[2,4096,1536]{2,1,0:T(8,128)(2,1)} %param.19, bf16[384,4096]{1,0:T(8,128)(2,1)} %all-gather.9.cloned.1.call-done, s32[]{:T(128)S(6)} %select_n.124, f32[384,1536]{1,0:T(8,128)} %fusion.8), kind=kOutput, calls=%fused_computation.28 | convolution fusion | flops 2416214016 | bytes 16516096 | tf_op jit(solution)/shard_map/dot_general | solution.py:150
  270.0 5.7 %collective-permute-done.10 = f32[96,1536]{1,0:T(8,128)S(1)} collective-permute-done((f32[96,1536]{1,0:T(8,128)S(1)}, f32[96,1536]{1,0:T(8,128)S(1)}, u32[]{:S(2)}, u32[]{:S(2)}) %collective-permute-start.10) | collective-permute-done | bytes 589856 | tf_op jit(solution)/shard_map/ppermute | solution.py:162
  275.7 0.8 add_convert_fusion
  (70 shorter events, 4.5 us)
Async XLA Ops:
  6.5 90.2 %copy-start = (bf16[8,2,64,1024]{3,2,1,0:T(8,128)(2,1)S(1)}, bf16[8,2,64,1024]{3,2,1,0:T(8,128)(2,1)}, u32[]{:S(2)}) copy-start(bf16[8,2,64,1024]{3,2,1,0:T(8,128)(2,1)} %param.21) | copy-start | bytes 6291460
  6.5 71.8 %all-gather.5.cloned.1.call-start = ((), (), s32[]{:S(2)}) async-start(), calls=%async_computation | async-start | bytes 2949120 | tf_op jit(solution)/shard_map/all_gather | solution.py:88
  6.5 12.3 %collective-permute-start.1 = (bf16[1,128,1536]{2,1,0:T(8,128)(2,1)}, bf16[1,128,1536]{2,1,0:T(8,128)(2,1)S(1)}, u32[]{:S(2)}, u32[]{:S(2)}) collective-permute-start(bf16[1,128,1536]{2,1,0:T(8,128)(2,1)} %param.11), channel_id=1, source_target_pairs={{0,8},{8,0},{1,9},{9,1},{2,10},{10,2},{3,11},{11,3},{4,12},{12,4},... | collective-permute-start | bytes 1179656 | tf_op jit(solution)/shard_map/ppermute | solution.py:44
  9.5 10.2 %collective-permute-start = (bf16[1,128,1536]{2,1,0:T(8,128)(2,1)}, bf16[1,128,1536]{2,1,0:T(8,128)(2,1)S(1)}, u32[]{:S(2)}, u32[]{:S(2)}) collective-permute-start(bf16[1,128,1536]{2,1,0:T(8,128)(2,1)} %param.11), channel_id=1, source_target_pairs={{0,4},{4,0},{1,5},{5,1},{2,6},{6,2},{3,7},{7,3},{8,12},{12,8},{9,1... | collective-permute-start | bytes 1179656 | tf_op jit(solution)/shard_map/ppermute | solution.py:45
  18.8 1.7 collective-permute-start.2
  22.9 23.3 %copy-start.12 = (s32[3]{0:T(128)S(1)}, s32[3]{0:T(128)}, u32[]{:S(2)}) copy-start(s32[3]{0:T(128)} %param.14) | copy-start | bytes 40
  22.9 23.3 %copy-start.2 = (s32[8]{0:T(128)S(1)}, s32[8]{0:T(128)}, u32[]{:S(2)}) copy-start(s32[8]{0:T(128)} %param.15) | copy-start | bytes 100
  25.0 27.1 %copy-start.7 = (bf16[3,128,1536]{2,1,0:T(8,128)(2,1)}, bf16[3,128,1536]{2,1,0:T(8,128)(2,1)S(1)}, u32[]{:S(2)}) copy-start(bf16[3,128,1536]{2,1,0:T(8,128)(2,1)S(1)} %gather_fusion) | copy-start | bytes 3538948
  26.2 160.2 %all-gather.7.cloned.1.call-start = ((), (), s32[]{:S(2)}) async-start(), calls=%async_computation.1 | async-start | bytes 3932160 | tf_op jit(solution)/shard_map/all_gather | solution.py:135
  26.3 20.0 %collective-permute-start.5 = (bf16[2,2,1536,64]{2,3,1,0:T(8,128)(2,1)}, bf16[2,2,1536,64]{2,3,1,0:T(8,128)(2,1)}, u32[]{:S(2)}, u32[]{:S(2)}) collective-permute-start(bf16[2,2,1536,64]{2,3,1,0:T(8,128)(2,1)} %param.20), channel_id=1, source_target_pairs={{0,8},{8,0},{1,9},{9,1},{2,10},{10,2},{3,11},{11,3},{4,12},{12,4},... | collective-permute-start | bytes 2359304 | tf_op jit(solution)/shard_map/ppermute | solution.py:63
  28.1 18.9 %collective-permute-start.4 = (bf16[2,2,1536,64]{2,3,1,0:T(8,128)(2,1)}, bf16[2,2,1536,64]{2,3,1,0:T(8,128)(2,1)}, u32[]{:S(2)}, u32[]{:S(2)}) collective-permute-start(bf16[2,2,1536,64]{2,3,1,0:T(8,128)(2,1)} %param.20), channel_id=1, source_target_pairs={{0,4},{4,0},{1,5},{5,1},{2,6},{6,2},{3,7},{7,3},{8,12},{12,8},{9,1... | collective-permute-start | bytes 2359304 | tf_op jit(solution)/shard_map/ppermute | solution.py:64
  46.2 2.6 collective-permute-start.6
  78.3 1.3 copy-start.8
  78.3 20.7 %collective-permute-start.3 = (bf16[192,6144]{1,0:T(8,128)(2,1)}, bf16[192,6144]{1,0:T(8,128)(2,1)}, u32[]{:S(2)}, u32[]{:S(2)}) collective-permute-start(bf16[192,6144]{1,0:T(8,128)(2,1)} %all-gather.5.cloned.1.call-done), channel_id=1, source_target_pairs={{0,4},{4,0},{1,5},{5,1},{2,6},{6,2},{3,7},{7,3},{8,12},{12,8},{9,1... | collective-permute-start | bytes 7077896 | tf_op jit(solution)/shard_map/ppermute | solution.py:96
  80.1 16.6 %copy-start.11 = (s32[384,2]{0,1:T(2,128)S(1)}, s32[384,2]{0,1:T(2,128)}, u32[]{:S(2)}) copy-start(s32[384,2]{0,1:T(2,128)} %param.13) | copy-start | bytes 9220
  96.6 1.3 collective-permute-start.7
  98.7 2.8 copy-start.9
  98.9 16.2 %copy-start.5 = (f32[3,128,2,1024]{3,1,0,2:T(8,128)}, f32[3,128,2,1024]{3,1,0,2:T(8,128)S(1)}, u32[]{:S(2)}) copy-start(f32[3,128,2,1024]{3,1,0,2:T(8,128)S(1)} %copy.18) | copy-start | bytes 9437188
  98.9 6.6 %copy-start.10 = (bf16[6144,8]{0,1:T(8,128)(2,1)S(1)}, bf16[6144,8]{0,1:T(8,128)(2,1)}, u32[]{:S(2)}) copy-start(bf16[6144,8]{0,1:T(8,128)(2,1)} %param.16) | copy-start | bytes 294916
  105.5 9.6 %copy-start.3 = (bf16[384,6144]{1,0:T(8,128)(2,1)}, bf16[384,6144]{1,0:T(8,128)(2,1)S(1)}, u32[]{:S(2)}) copy-start(bf16[384,6144]{1,0:T(8,128)(2,1)S(1)} %maximum_select_fusion) | copy-start | bytes 14155780
  124.2 125.9 %all-gather.9.cloned.1.call-start = ((), (), s32[]{:S(2)}) async-start(), calls=%async_computation.2 | async-start | bytes 3932160 | tf_op jit(solution)/shard_map/all_gather | solution.py:135
  124.5 11.3 %copy-start.4 = (bf16[384,6144]{1,0:T(8,128)(2,1)S(1)}, bf16[384,6144]{1,0:T(8,128)(2,1)}, u32[]{:S(2)}) copy-start(bf16[384,6144]{1,0:T(8,128)(2,1)} %copy-done.3) | copy-start | bytes 14155780
  124.5 11.3 %copy-start.6 = (f32[3,128,2,1024]{3,1,0,2:T(8,128)S(1)}, f32[3,128,2,1024]{3,1,0,2:T(8,128)}, u32[]{:S(2)}) copy-start(f32[3,128,2,1024]{3,1,0,2:T(8,128)} %copy-done.5) | copy-start | bytes 9437188
  258.1 2.1 collective-permute-start.8
  260.3 15.4 %collective-permute-start.10 = (f32[96,1536]{1,0:T(8,128)S(1)}, f32[96,1536]{1,0:T(8,128)S(1)}, u32[]{:S(2)}, u32[]{:S(2)}) collective-permute-start(f32[96,1536]{1,0:T(8,128)S(1)} %dynamic-slice_add_fusion), channel_id=1, source_target_pairs={{0,8},{8,0},{1,9},{9,1},{2,10},{10,2},{3,11},{11,3},{4,12},{12,4},... | collective-permute-start | bytes 1769480 | tf_op jit(solution)/shard_map/ppermute | solution.py:162
  261.8 14.7 %copy-start.1 = (bf16[8,2,64,1024]{3,2,1,0:T(8,128)(2,1)S(1)}, bf16[8,2,64,1024]{3,2,1,0:T(8,128)(2,1)}, u32[]{:S(2)}) copy-start(bf16[8,2,64,1024]{3,2,1,0:T(8,128)(2,1)} %param.21) | copy-start | bytes 6291460
  269.9 5.8 %collective-permute-start.9 = (f32[96,1536]{1,0:T(8,128)S(1)}, f32[96,1536]{1,0:T(8,128)S(1)}, u32[]{:S(2)}, u32[]{:S(2)}) collective-permute-start(f32[96,1536]{1,0:T(8,128)S(1)} %constant_dynamic-slice_fusion.1), channel_id=1, source_target_pairs={{0,4},{4,0},{1,5},{5,1},{2,6},{6,2},{3,7},{7,3},{8,12},{12,8},{9,1... | collective-permute-start | bytes 1769480 | tf_op jit(solution)/shard_map/ppermute | solution.py:159
Sparse Core Ops, SparseCore 0:
  26.3 51.9 all-gather.4
  124.4 62.0 all-gather.6
  188.0 62.1 all-gather.8

commit v16 on v15

--- a/solution.py
+++ b/solution.py
@@ -89,16 +89,24 @@
     rank_q = lax.dynamic_slice_in_dim(
         jnp.concatenate([rank_hi, rank_lo], axis=1), core * half, half, 0
     )
-    rank_q, _ = lax.optimization_barrier((rank_q, mine))
-    pieces = lax.all_gather(rank_q, "expert", axis=1, tiled=False).astype(jnp.float32)
-    mine_rank = jnp.sum(pieces[:, :, : window * rank] + pieces[:, :, window * rank :], axis=1)
-    mine_rank = mine_rank.astype(jnp.bfloat16)
+    arrivals = [rank_q] + [
+        lax.ppermute(rank_q, "expert", [(i, (i + shift) % expert_size) for i in range(expert_size)])
+        for shift in range(1, expert_size)
+    ]
     other = lax.ppermute(mine, "wc", swap)
-    other_rank = lax.ppermute(mine_rank, "wc", swap)
     input_rows = jnp.where(
         core == 0, jnp.concatenate([mine, other], axis=0), jnp.concatenate([other, mine], axis=0)
     )
     input_rows = lax.optimization_barrier(input_rows)
+    gate_first = jnp.dot(input_rows, gate_weight[0], preferred_element_type=jnp.float32)
+    arrivals, gate_first = lax.optimization_barrier((arrivals, gate_first))
+    mine_rank = None
+    for piece in arrivals:
+        piece = piece.astype(jnp.float32)
+        piece = piece[:, : window * rank] + piece[:, window * rank :]
+        mine_rank = piece if mine_rank is None else mine_rank + piece
+    mine_rank = mine_rank.astype(jnp.bfloat16)
+    other_rank = lax.ppermute(mine_rank, "wc", swap)
     lowrank = jnp.where(
         core == 0,
         jnp.concatenate([mine_rank, other_rank], axis=0),
@@ -122,7 +130,7 @@
 
     running = None
     for expert_number in range(window):
-        gate_pre = jnp.dot(
+        gate_pre = gate_first if expert_number == 0 else jnp.dot(
             input_rows, gate_weight[expert_number], preferred_element_type=jnp.float32
         )
         up_value = (

time: 283 us -> 290 us (1.025)
  waiting for transfers between devices: 158 us -> 174 us
  blocking collectives: 15.9 us -> 0 us
  starting transfers between devices: 6.81 us -> 11.1 us
    all_gather x1 -> x0, blocking collectives: 15.9 us -> none  [per_device(): lax.all_gather(rank_q, 'expert', axis=1, tiled=False).astype(jnp.float32)]
    dot_general x2 -> x1, matrix products: 19.4 us -> 9.53 us  [per_device(): jnp.dot(input_rows, gate_weight[expert_number], preferred_element_type=jn...]
    dot_general x0 -> x1, matrix products: none -> 9.2 us  [per_device(): jnp.dot(input_rows, gate_weight[0], preferred_element_type=jnp.float32)]
    all_gather x1, waiting for transfers between devices: 23.7 us -> 32.1 us  [per_device(): mine = lax.all_gather(mine_q, 'expert', axis=1, tiled=True)]
    ppermute x1, waiting for transfers between devices: 5.7 us -> 13.7 us  [split_last(): away = lax.ppermute(away_sum, 'wy', pair)]
    ppermute x0 -> x3, starting transfers between devices: none -> 4.23 us  [per_device(): lax.ppermute(rank_q, 'expert', [(i, (i + shift) % expert_size) for i in r...]
  transfers between devices with their start and end apart: 14 -> 17, of which waited for: 10 -> 10; matrix products, arithmetic and copies ran while one was open for 17% -> 18% of each run, Pallas kernels for 0% -> 0%
where the time goes in v16:
time: 290 us
  waiting for transfers between devices  174 us (60%)
  matrix products  66.5 us (23%)
  between operations  13.5 us (5%)
  other arithmetic  13.2 us (5%)
  local copies, waits for them, and re-layouts  11.5 us (4%)
  starting transfers between devices  11.1 us (4%)
    all_gather x2, waiting for transfers between devices, per_device(): gathered = lax.all_gather(hidden, 'expert', axis=1, tiled=True)  96.6 us
    all_gather x1, waiting for transfers between devices, per_device(): mine = lax.all_gather(mine_q, 'expert', axis=1, tiled=True)  32.1 us
    dot_general x2, matrix products, per_device(): jnp.dot(input_rows, up_weight[expert_number], preferred_element_type=jnp....  19.4 us
    ppermute x1, waiting for transfers between devices, per_device(): from_chip = lax.ppermute(adapter_down_weight, 'wy', swap)  18.2 us
    dot_general x2, matrix products, chip_rows(): jnp.dot(lax.dynamic_slice_in_dim(source, which * span_rows, span_rows, 0)...  16 us
    ppermute x1, waiting for transfers between devices, split_last(): away = lax.ppermute(away_sum, 'wy', pair)  13.7 us
    dot_general x1, matrix products, per_device(): jnp.dot(gathered, down_weight[expert_number], preferred_element_type=jnp....  9.95 us
    dot_general x1, matrix products, per_device(): jnp.dot(input_rows, gate_weight[expert_number], preferred_element_type=jn...  9.53 us
  transfers between devices with their start and end apart: 17, of which 10 were waited for; matrix products, arithmetic and copies ran while one was open for 18% of the time, Pallas kernels for 0%

profile of v16, /device:TPU:0, one launch (start us, length us, event | category | flops | bytes accessed | tf_op | source)
XLA Modules:
  0.0 290.1 jit_solution(2674760241630729523)
XLA Ops:
  6.5 3.0 %collective-permute-start.1 = (bf16[1,128,1536]{2,1,0:T(8,128)(2,1)}, bf16[1,128,1536]{2,1,0:T(8,128)(2,1)S(1)}, u32[]{:S(2)}, u32[]{:S(2)}) collective-permute-start(bf16[1,128,1536]{2,1,0:T(8,128)(2,1)} %param.11), channel_id=1, source_target_pairs={{0,8},{8,0},{1,9},{9,1},{2,10},{10,2},{3,11},{11,3},{4,12},{12,4},... | collective-permute-start | bytes 1179656 | tf_op jit(solution)/shard_map/ppermute | solution.py:44
  9.5 9.3 %collective-permute-done.1 = bf16[1,128,1536]{2,1,0:T(8,128)(2,1)S(1)} collective-permute-done((bf16[1,128,1536]{2,1,0:T(8,128)(2,1)}, bf16[1,128,1536]{2,1,0:T(8,128)(2,1)S(1)}, u32[]{:S(2)}, u32[]{:S(2)}) %collective-permute-start.1) | collective-permute-done | bytes 393248 | tf_op jit(solution)/shard_map/ppermute | solution.py:44
  19.7 0.9 collective-permute-done.2
  20.6 2.4 pad_maximum_fusion.1
  22.9 2.1 gather_fusion
  25.0 1.2 dynamic-slice_select_fusion
  26.3 1.8 collective-permute-start.5
  28.2 18.2 %collective-permute-done.5 = bf16[2,2,1536,64]{2,3,1,0:T(8,128)(2,1)} collective-permute-done((bf16[2,2,1536,64]{2,3,1,0:T(8,128)(2,1)}, bf16[2,2,1536,64]{2,3,1,0:T(8,128)(2,1)}, u32[]{:S(2)}, u32[]{:S(2)}) %collective-permute-start.5) | collective-permute-done | bytes 786464 | tf_op jit(solution)/shard_map/ppermute | solution.py:63
  46.3 32.1 %all-gather.4.cloned.1.call-done = bf16[192,6144]{1,0:T(8,128)(2,1)} async-done(((bf16[192,1536]{1,0:T(8,128)(2,1)}), bf16[192,6144]{1,0:T(8,128)(2,1)}) %all-gather.4.cloned.1.call-update) | async-done | bytes 2359312 | tf_op jit(solution)/shard_map/all_gather | solution.py:88
  79.7 3.2 %pad_maximum_fusion = bf16[4,2,2,1536,64]{3,4,2,1,0:T(8,128)(2,1)} fusion(bf16[1,2,2,1536,64]{3,4,2,1,0:T(8,128)(2,1)} %bitcast.7, bf16[1,2,2,1536,64]{3,4,2,1,0:T(8,128)(2,1)} %bitcast.6, bf16[1,2,2,1536,64]{3,4,2,1,0:T(8,128)(2,1)} %bitcast.5, bf16[1,2,2,1536,64]{3,4,2,1,0:T(8,128)(2,1)} %bitcast.96), kind=kLoop, calls=%fused_computation.26 | loop fusion | flops 4718592 | bytes 6291456 | tf_op jit(solution)/shard_map/stack | solution.py:66
  82.9 2.5 gather_fusion.2
  85.7 1.1 copy-done.7
  87.7 1.5 collective-permute-start.8
  89.2 2.7 collective-permute-start.9
  91.9 4.0 %maximum_select_fusion = bf16[384,6144]{1,0:T(8,128)(2,1)S(1)} fusion(bf16[192,6144]{1,0:T(8,128)(2,1)} %collective-permute-done.3, bf16[192,6144]{1,0:T(8,128)(2,1)S(1)} %copy-done.8, pred[]{:T(512)S(6)} %eq.23), kind=kLoop, calls=%fused_computation.25 | loop fusion | flops 21233664 | bytes 9437185 | tf_op jit(solution)/shard_map/jit(_where)/select_n | solution.py:97
  96.0 1.3 fusion.64
  98.1 9.2 %fusion.12 = f32[384,1024]{1,0:T(8,128)} fusion(bf16[384,6144]{1,0:T(8,128)(2,1)S(1)} %maximum_select_fusion, bf16[2,6144,1024]{2,1,0:T(8,128)(2,1)} %param.17), kind=kOutput, calls=%fused_computation.16 | convolution fusion | flops 4831838208 | bytes 18874368 | tf_op jit(solution)/shard_map/dot_general | solution.py:101
  107.7 1.2 collective-permute-done.10
  110.0 1.8 copy-done.4
  112.1 0.9 copy-done.12
  113.0 9.0 %fusion.34 = bf16[384,1024]{1,0:T(8,128)(2,1)} fusion(f32[384,2,1024]{2,0,1:T(8,128)S(1)} %bitcast.91, f32[384,1024]{1,0:T(8,128)S(1)} %copy-done.12, bf16[384,6144]{1,0:T(8,128)(2,1)S(1)} %bitcast.89, bf16[2,6144,1024]{2,1,0:T(8,128)(2,1)} %param.18, f32[384]{0:T(512)S(1)} %get-tuple-element.17), kind=kOutput, calls=%fused_computation.39 | convolution fusion | flops 4835377152 | bytes 21235200 | tf_op jit(solution)/shard_map/dot_general | solution.py:137
  122.3 9.5 %fusion.6 = f32[384,1024]{1,0:T(8,128)S(1)} fusion(bf16[384,6144]{1,0:T(8,128)(2,1)} %copy-done.3, bf16[2,6144,1024]{2,1,0:T(8,128)(2,1)} %param.17), kind=kOutput, calls=%fused_computation.10 | convolution fusion | flops 4831838208 | bytes 18874368 | tf_op jit(solution)/shard_map/dot_general | solution.py:133
  131.9 10.3 %fusion.30 = bf16[384,1024]{1,0:T(8,128)(2,1)} fusion(f32[384,2,1024]{2,0,1:T(8,128)S(1)} %bitcast.92, f32[384,1024]{1,0:T(8,128)S(1)} %fusion.6, bf16[384,6144]{1,0:T(8,128)(2,1)} %copy-done.3, bf16[2,6144,1024]{2,1,0:T(8,128)(2,1)} %param.18, f32[384]{0:T(512)S(1)} %get-tuple-element.18), kind=kOutput, calls=%fused_computation.34 | convolution fusion | flops 4835377152 | bytes 21235200 | tf_op jit(solution)/shard_map/dot_general | solution.py:137
  142.3 42.7 %all-gather.6.cloned.1.call-done = bf16[384,4096]{1,0:T(8,128)(2,1)} async-done(((bf16[384,1024]{1,0:T(8,128)(2,1)}), bf16[384,4096]{1,0:T(8,128)(2,1)}) %all-gather.6.cloned.1.call-update) | async-done | bytes 3145744 | tf_op jit(solution)/shard_map/all_gather | solution.py:143
  185.0 9.9 %fusion.8 = f32[384,1536]{1,0:T(8,128)} fusion(bf16[384,4096]{1,0:T(8,128)(2,1)} %all-gather.6.cloned.1.call-done, bf16[2,4096,1536]{2,1,0:T(8,128)(2,1)} %param.19), kind=kOutput, calls=%fused_computation.12 | convolution fusion | flops 4831838208 | bytes 18087936 | tf_op jit(solution)/shard_map/dot_general | solution.py:146
  195.0 53.8 %all-gather.8.cloned.1.call-done = bf16[384,4096]{1,0:T(8,128)(2,1)} async-done(((bf16[384,1024]{1,0:T(8,128)(2,1)}), bf16[384,4096]{1,0:T(8,128)(2,1)}) %all-gather.8.cloned.1.call-update) | async-done | bytes 3145744 | tf_op jit(solution)/shard_map/all_gather | solution.py:143
  248.8 7.9 %fusion.21 = f32[192,1536]{1,0:T(8,128)S(1)} fusion(bf16[2,4096,1536]{2,1,0:T(8,128)(2,1)} %param.19, bf16[384,4096]{1,0:T(8,128)(2,1)} %all-gather.8.cloned.1.call-done, s32[]{:T(128)S(6)} %select_n.125, f32[384,1536]{1,0:T(8,128)} %fusion.8), kind=kOutput, calls=%fused_computation.27 | convolution fusion | flops 2416214016 | bytes 16516096 | tf_op jit(solution)/shard_map/dot_general | solution.py:158
  256.8 2.0 collective-permute-done.11
  258.9 8.1 %fusion.24 = f32[192,1536]{1,0:T(8,128)S(1)} fusion(bf16[2,4096,1536]{2,1,0:T(8,128)(2,1)} %param.19, bf16[384,4096]{1,0:T(8,128)(2,1)} %all-gather.8.cloned.1.call-done, s32[]{:T(128)S(6)} %select_n.124, f32[384,1536]{1,0:T(8,128)} %fusion.8), kind=kOutput, calls=%fused_computation.28 | convolution fusion | flops 2416214016 | bytes 16516096 | tf_op jit(solution)/shard_map/dot_general | solution.py:158
  267.2 1.5 collective-permute-start.13
  269.1 13.7 %collective-permute-done.13 = f32[96,1536]{1,0:T(8,128)S(1)} collective-permute-done((f32[96,1536]{1,0:T(8,128)S(1)}, f32[96,1536]{1,0:T(8,128)S(1)}, u32[]{:S(2)}, u32[]{:S(2)}) %collective-permute-start.13) | collective-permute-done | bytes 589856 | tf_op jit(solution)/shard_map/ppermute | solution.py:170
  282.8 0.8 add_convert_fusion
  (83 shorter events, 7.0 us)
Async XLA Ops:
  6.5 72.5 %copy-start = (bf16[8,2,64,1024]{3,2,1,0:T(8,128)(2,1)S(1)}, bf16[8,2,64,1024]{3,2,1,0:T(8,128)(2,1)}, u32[]{:S(2)}) copy-start(bf16[8,2,64,1024]{3,2,1,0:T(8,128)(2,1)} %param.21) | copy-start | bytes 6291460
  6.5 71.8 %all-gather.4.cloned.1.call-start = ((), (), s32[]{:S(2)}) async-start(), calls=%async_computation | async-start | bytes 2949120 | tf_op jit(solution)/shard_map/all_gather | solution.py:88
  6.5 12.3 %collective-permute-start.1 = (bf16[1,128,1536]{2,1,0:T(8,128)(2,1)}, bf16[1,128,1536]{2,1,0:T(8,128)(2,1)S(1)}, u32[]{:S(2)}, u32[]{:S(2)}) collective-permute-start(bf16[1,128,1536]{2,1,0:T(8,128)(2,1)} %param.11), channel_id=1, source_target_pairs={{0,8},{8,0},{1,9},{9,1},{2,10},{10,2},{3,11},{11,3},{4,12},{12,4},... | collective-permute-start | bytes 1179656 | tf_op jit(solution)/shard_map/ppermute | solution.py:44
  9.5 10.2 %collective-permute-start = (bf16[1,128,1536]{2,1,0:T(8,128)(2,1)}, bf16[1,128,1536]{2,1,0:T(8,128)(2,1)S(1)}, u32[]{:S(2)}, u32[]{:S(2)}) collective-permute-start(bf16[1,128,1536]{2,1,0:T(8,128)(2,1)} %param.11), channel_id=1, source_target_pairs={{0,4},{4,0},{1,5},{5,1},{2,6},{6,2},{3,7},{7,3},{8,12},{12,8},{9,1... | collective-permute-start | bytes 1179656 | tf_op jit(solution)/shard_map/ppermute | solution.py:45
  18.8 1.7 collective-permute-start.2
  22.9 55.4 %copy-start.11 = (s32[3]{0:T(128)S(1)}, s32[3]{0:T(128)}, u32[]{:S(2)}) copy-start(s32[3]{0:T(128)} %param.14) | copy-start | bytes 40
  22.9 55.5 %copy-start.2 = (s32[8]{0:T(128)S(1)}, s32[8]{0:T(128)}, u32[]{:S(2)}) copy-start(s32[8]{0:T(128)} %param.15) | copy-start | bytes 100
  25.0 53.4 %copy-start.6 = (bf16[3,128,1536]{2,1,0:T(8,128)(2,1)}, bf16[3,128,1536]{2,1,0:T(8,128)(2,1)S(1)}, u32[]{:S(2)}) copy-start(bf16[3,128,1536]{2,1,0:T(8,128)(2,1)S(1)} %gather_fusion) | copy-start | bytes 3538948
  25.0 54.7 %copy-start.10 = (s32[384,2]{0,1:T(2,128)S(1)}, s32[384,2]{0,1:T(2,128)}, u32[]{:S(2)}) copy-start(s32[384,2]{0,1:T(2,128)} %param.13) | copy-start | bytes 9220
  26.3 158.7 %all-gather.6.cloned.1.call-start = ((), (), s32[]{:S(2)}) async-start(), calls=%async_computation.1 | async-start | bytes 3932160 | tf_op jit(solution)/shard_map/all_gather | solution.py:143
  26.3 20.0 %collective-permute-start.5 = (bf16[2,2,1536,64]{2,3,1,0:T(8,128)(2,1)}, bf16[2,2,1536,64]{2,3,1,0:T(8,128)(2,1)}, u32[]{:S(2)}, u32[]{:S(2)}) collective-permute-start(bf16[2,2,1536,64]{2,3,1,0:T(8,128)(2,1)} %param.20), channel_id=1, source_target_pairs={{0,8},{8,0},{1,9},{9,1},{2,10},{10,2},{3,11},{11,3},{4,12},{12,4},... | collective-permute-start | bytes 2359304 | tf_op jit(solution)/shard_map/ppermute | solution.py:63
  28.2 51.6 %collective-permute-start.4 = (bf16[2,2,1536,64]{2,3,1,0:T(8,128)(2,1)}, bf16[2,2,1536,64]{2,3,1,0:T(8,128)(2,1)}, u32[]{:S(2)}, u32[]{:S(2)}) collective-permute-start(bf16[2,2,1536,64]{2,3,1,0:T(8,128)(2,1)} %param.20), channel_id=1, source_target_pairs={{0,4},{4,0},{1,5},{5,1},{2,6},{6,2},{3,7},{7,3},{8,12},{12,8},{9,1... | collective-permute-start | bytes 2359304 | tf_op jit(solution)/shard_map/ppermute | solution.py:64
  46.3 33.4 %collective-permute-start.6 = (bf16[2,2,1536,64]{2,3,1,0:T(8,128)(2,1)}, bf16[2,2,1536,64]{2,3,1,0:T(8,128)(2,1)}, u32[]{:S(2)}, u32[]{:S(2)}) collective-permute-start(bf16[2,2,1536,64]{2,3,1,0:T(8,128)(2,1)} %collective-permute-done.5), channel_id=1, source_target_pairs={{0,4},{4,0},{1,5},{5,1},{2,6},{6,2},{3,7},{7,3},{8,12},{12,8},{9,1... | collective-permute-start | bytes 2359304 | tf_op jit(solution)/shard_map/ppermute | solution.py:65
  78.4 13.5 %collective-permute-start.3 = (bf16[192,6144]{1,0:T(8,128)(2,1)}, bf16[192,6144]{1,0:T(8,128)(2,1)}, u32[]{:S(2)}, u32[]{:S(2)}) collective-permute-start(bf16[192,6144]{1,0:T(8,128)(2,1)} %all-gather.4.cloned.1.call-done), channel_id=1, source_target_pairs={{0,4},{4,0},{1,5},{5,1},{2,6},{6,2},{3,7},{7,3},{8,12},{12,8},{9,1... | collective-permute-start | bytes 7077896 | tf_op jit(solution)/shard_map/ppermute | solution.py:96
  85.5 1.3 copy-start.7
  85.7 6.3 %copy-start.8 = (bf16[192,6144]{1,0:T(8,128)(2,1)S(1)}, bf16[192,6144]{1,0:T(8,128)(2,1)}, u32[]{:S(2)}) copy-start(bf16[192,6144]{1,0:T(8,128)(2,1)} %all-gather.4.cloned.1.call-done) | copy-start | bytes 7077892
  87.7 8.3 %copy-start.9 = (bf16[6144,8]{0,1:T(8,128)(2,1)S(1)}, bf16[6144,8]{0,1:T(8,128)(2,1)}, u32[]{:S(2)}) copy-start(bf16[6144,8]{0,1:T(8,128)(2,1)} %param.16) | copy-start | bytes 294916
  87.7 19.7 %collective-permute-start.7 = (bf16[192,256]{0,1:T(8,128)(2,1)S(1)}, bf16[192,256]{0,1:T(8,128)(2,1)S(1)}, u32[]{:S(2)}, u32[]{:S(2)}) collective-permute-start(bf16[192,256]{0,1:T(8,128)(2,1)S(1)} %fusion.49), channel_id=1, source_target_pairs={{0,1},{1,2},{2,3},{3,0},{4,5},{5,6},{6,7},{7,4},{8,9},{9,10},{10,1... | collective-permute-start | bytes 294920 | tf_op jit(solution)/shard_map/ppermute | solution.py:93
  87.7 19.6 %collective-permute-start.8 = (bf16[192,256]{0,1:T(8,128)(2,1)S(1)}, bf16[192,256]{0,1:T(8,128)(2,1)S(1)}, u32[]{:S(2)}, u32[]{:S(2)}) collective-permute-start(bf16[192,256]{0,1:T(8,128)(2,1)S(1)} %fusion.49), channel_id=1, source_target_pairs={{0,2},{1,3},{2,0},{3,1},{4,6},{5,7},{6,4},{7,5},{8,10},{9,11},{10,... | collective-permute-start | bytes 294920 | tf_op jit(solution)/shard_map/ppermute | solution.py:93
  89.2 18.1 %collective-permute-start.9 = (bf16[192,256]{0,1:T(8,128)(2,1)S(1)}, bf16[192,256]{0,1:T(8,128)(2,1)S(1)}, u32[]{:S(2)}, u32[]{:S(2)}) collective-permute-start(bf16[192,256]{0,1:T(8,128)(2,1)S(1)} %fusion.49), channel_id=1, source_target_pairs={{0,3},{1,0},{2,1},{3,2},{4,7},{5,4},{6,5},{7,6},{8,11},{9,8},{10,9... | collective-permute-start | bytes 294920 | tf_op jit(solution)/shard_map/ppermute | solution.py:93
  96.0 2.2 copy-start.3
  107.4 4.3 %slice-start = ((s8[4718592]{0:T(1024)(128)(4,1)}), s8[524288]{0:T(1024)(128)(4,1)S(1)}, s32[]{:S(2)}) async-start(s8[4718592]{0:T(1024)(128)(4,1)} %bitcast.88), calls=%async_computation.3 | async-start | bytes 1048576
  107.6 1.3 collective-permute-start.10
  109.1 3.1 %slice-start.1 = ((s8[4718592]{0:T(1024)(128)(4,1)}), s8[4194304]{0:T(1024)(128)(4,1)S(1)}, s32[]{:S(2)}) async-start(s8[4718592]{0:T(1024)(128)(4,1)} %bitcast.88), calls=%async_computation.4 | async-start | bytes 8388608
  109.7 3.3 %copy-start.12 = (f32[384,1024]{1,0:T(8,128)S(1)}, f32[384,1024]{1,0:T(8,128)}, u32[]{:S(2)}) copy-start(f32[384,1024]{1,0:T(8,128)} %fusion.12) | copy-start | bytes 4718596
  110.0 1.8 copy-start.4
  122.1 126.7 %all-gather.8.cloned.1.call-start = ((), (), s32[]{:S(2)}) async-start(), calls=%async_computation.2 | async-start | bytes 3932160 | tf_op jit(solution)/shard_map/all_gather | solution.py:143
  122.3 9.5 %copy-start.5 = (f32[3,128,2,1024]{3,1,0,2:T(8,128)S(1)}, f32[3,128,2,1024]{3,1,0,2:T(8,128)}, u32[]{:S(2)}) copy-start(f32[3,128,2,1024]{3,1,0,2:T(8,128)} %copy-done.4) | copy-start | bytes 9437188
  256.7 2.1 collective-permute-start.11
  258.9 24.7 %copy-start.1 = (bf16[8,2,64,1024]{3,2,1,0:T(8,128)(2,1)S(1)}, bf16[8,2,64,1024]{3,2,1,0:T(8,128)(2,1)}, u32[]{:S(2)}) copy-start(bf16[8,2,64,1024]{3,2,1,0:T(8,128)(2,1)} %param.21) | copy-start | bytes 6291460
  267.0 2.1 collective-permute-start.12
  267.2 15.6 %collective-permute-start.13 = (f32[96,1536]{1,0:T(8,128)S(1)}, f32[96,1536]{1,0:T(8,128)S(1)}, u32[]{:S(2)}, u32[]{:S(2)}) collective-permute-start(f32[96,1536]{1,0:T(8,128)S(1)} %dynamic-slice_add_fusion), channel_id=1, source_target_pairs={{0,8},{8,0},{1,9},{9,1},{2,10},{10,2},{3,11},{11,3},{4,12},{12,4},... | collective-permute-start | bytes 1769480 | tf_op jit(solution)/shard_map/ppermute | solution.py:170
Sparse Core Ops, SparseCore 0:
  26.4 51.9 all-gather.3
  122.2 62.7 all-gather.5
  186.6 62.1 all-gather.7

commit v17 on v15

--- a/solution.py
+++ b/solution.py
@@ -95,8 +95,8 @@
     mine_rank = mine_rank.astype(jnp.bfloat16)
     other = lax.ppermute(mine, "wc", swap)
     other_rank = lax.ppermute(mine_rank, "wc", swap)
-    input_rows = jnp.where(
-        core == 0, jnp.concatenate([mine, other], axis=0), jnp.concatenate([other, mine], axis=0)
+    input_rows = lax.dynamic_slice_in_dim(
+        jnp.concatenate([mine, other, mine], axis=0), core * half, tokens, 0
     )
     input_rows = lax.optimization_barrier(input_rows)
     lowrank = jnp.where(

time: 283 us -> 285 us (level)
    concatenate x0 -> x1, other arithmetic: none -> 5.99 us  [per_device(): jnp.concatenate([mine, other, mine], axis=0)]
    select_n x1 -> x0, other arithmetic: 4 us -> none  [per_device(): jnp.where(core == 0, jnp.concatenate([mine, other], axis=0), jnp.concaten...]
where the time goes in v17:
time: 285 us
  waiting for transfers between devices  158 us (55%)
  matrix products  66 us (23%)
  blocking collectives  15.9 us (6%)
  other arithmetic  15.1 us (5%)
  between operations  13.5 us (5%)
  local copies, waits for them, and re-layouts  10.1 us (4%)
  starting transfers between devices  6.81 us (2%)
    all_gather x2, waiting for transfers between devices, per_device(): gathered = lax.all_gather(hidden, 'expert', axis=1, tiled=True)  95.3 us
    all_gather x1, waiting for transfers between devices, per_device(): mine = lax.all_gather(mine_q, 'expert', axis=1, tiled=True)  23.7 us
    dot_general x2, matrix products, per_device(): jnp.dot(input_rows, gate_weight[expert_number], preferred_element_type=jn...  19.4 us
    ppermute x1, waiting for transfers between devices, per_device(): from_chip = lax.ppermute(adapter_down_weight, 'wy', swap)  18.2 us
    dot_general x2, matrix products, per_device(): jnp.dot(input_rows, up_weight[expert_number], preferred_element_type=jnp....  18.1 us
    dot_general x2, matrix products, chip_rows(): jnp.dot(lax.dynamic_slice_in_dim(source, which * span_rows, span_rows, 0)...  15.9 us
    all_gather x1, blocking collectives, per_device(): lax.all_gather(rank_q, 'expert', axis=1, tiled=False).astype(jnp.float32)  15.9 us
    dot_general x1, matrix products, per_device(): jnp.dot(gathered, down_weight[expert_number], preferred_element_type=jnp....  10 us
  transfers between devices with their start and end apart: 14, of which 10 were waited for; matrix products, arithmetic and copies ran while one was open for 17% of the time, Pallas kernels for 0%

profile of v17, /device:TPU:0, one launch (start us, length us, event | category | flops | bytes accessed | tf_op | source)
XLA Modules:
  0.0 285.0 jit_solution(10244655498078403797)
XLA Ops:
  6.5 3.0 %collective-permute-start.1 = (bf16[1,128,1536]{2,1,0:T(8,128)(2,1)}, bf16[1,128,1536]{2,1,0:T(8,128)(2,1)S(1)}, u32[]{:S(2)}, u32[]{:S(2)}) collective-permute-start(bf16[1,128,1536]{2,1,0:T(8,128)(2,1)} %param.11), channel_id=1, source_target_pairs={{0,8},{8,0},{1,9},{9,1},{2,10},{10,2},{3,11},{11,3},{4,12},{12,4},... | collective-permute-start | bytes 1179656 | tf_op jit(solution)/shard_map/ppermute | solution.py:44
  9.5 9.3 %collective-permute-done.1 = bf16[1,128,1536]{2,1,0:T(8,128)(2,1)S(1)} collective-permute-done((bf16[1,128,1536]{2,1,0:T(8,128)(2,1)}, bf16[1,128,1536]{2,1,0:T(8,128)(2,1)S(1)}, u32[]{:S(2)}, u32[]{:S(2)}) %collective-permute-start.1) | collective-permute-done | bytes 393248 | tf_op jit(solution)/shard_map/ppermute | solution.py:44
  18.8 0.7 compare_and_fusion.2
  19.7 0.9 collective-permute-done.2
  20.6 2.4 pad_maximum_fusion.1
  22.9 2.1 gather_fusion
  25.0 1.2 dynamic-slice_select_fusion
  26.3 1.8 collective-permute-start.5
  28.1 18.2 %collective-permute-done.5 = bf16[2,2,1536,64]{2,3,1,0:T(8,128)(2,1)} collective-permute-done((bf16[2,2,1536,64]{2,3,1,0:T(8,128)(2,1)}, bf16[2,2,1536,64]{2,3,1,0:T(8,128)(2,1)}, u32[]{:S(2)}, u32[]{:S(2)}) %collective-permute-start.5) | collective-permute-done | bytes 786464 | tf_op jit(solution)/shard_map/ppermute | solution.py:63
  46.3 0.6 gather_fusion.2
  47.0 1.9 collective-permute-done.6
  48.9 3.2 %pad_maximum_fusion = bf16[4,2,2,1536,64]{3,4,2,1,0:T(8,128)(2,1)} fusion(bf16[1,2,2,1536,64]{3,4,2,1,0:T(8,128)(2,1)} %bitcast.9, bf16[1,2,2,1536,64]{3,4,2,1,0:T(8,128)(2,1)} %bitcast.8, bf16[1,2,2,1536,64]{3,4,2,1,0:T(8,128)(2,1)} %bitcast.7, bf16[1,2,2,1536,64]{3,4,2,1,0:T(8,128)(2,1)} %bitcast.97), kind=kLoop, calls=%fused_computation.30 | loop fusion | flops 4718592 | bytes 6291456 | tf_op jit(solution)/shard_map/stack | solution.py:66
  52.1 2.5 gather_fusion.3
  54.6 23.7 %all-gather.5.cloned.1.call-done = bf16[192,6144]{1,0:T(8,128)(2,1)} async-done(((bf16[192,1536]{1,0:T(8,128)(2,1)}), bf16[192,6144]{1,0:T(8,128)(2,1)}) %all-gather.5.cloned.1.call-update) | async-done | bytes 2359312 | tf_op jit(solution)/shard_map/all_gather | solution.py:88
  78.5 1.1 copy-done.8
  80.5 15.9 %all-gather = bf16[192,1024]{0,1:T(8,128)(2,1)S(1)} all-gather(bf16[192,256]{0,1:T(8,128)(2,1)S(1)} %fusion.52), channel_id=2, replica_groups=mesh['groups'=2,'wy'=2,'wc'=2,'expert'=4] {'expert'}, dimensions={1}, use_global_device_ids=true | all-gather | bytes 491520 | tf_op jit(solution)/shard_map/all_gather | solution.py:93
  99.0 2.5 copy-done.9
  101.5 6.0 %fusion.22 = bf16[384,6144]{1,0:T(8,128)(2,1)S(1)} fusion(s32[]{:T(128)S(6)} %select_n.105, bf16[192,6144]{1,0:T(8,128)(2,1)S(1)} %copy-done.9, bf16[192,6144]{1,0:T(8,128)(2,1)} %collective-permute-done.3), kind=kLoop, calls=%fused_computation.29 | loop fusion | flops 14155776 | bytes 9437188 | tf_op jit(solution)/shard_map/concatenate | solution.py:99
  107.5 1.3 fusion.63
  108.9 8.1 %fusion.12 = f32[384,1024]{1,0:T(8,128)S(1)} fusion(bf16[384,6144]{1,0:T(8,128)(2,1)S(1)} %fusion.22, bf16[2,6144,1024]{2,1,0:T(8,128)(2,1)} %param.17), kind=kOutput, calls=%fused_computation.16 | convolution fusion | flops 4831838208 | bytes 18874368 | tf_op jit(solution)/shard_map/dot_general | solution.py:125
  117.1 9.1 %fusion.36 = bf16[384,1024]{1,0:T(8,128)(2,1)} fusion(f32[384,2,1024]{2,0,1:T(8,128)S(1)} %bitcast.92, f32[384,1024]{1,0:T(8,128)S(1)} %fusion.12, bf16[384,6144]{1,0:T(8,128)(2,1)S(1)} %fusion.22, bf16[2,6144,1024]{2,1,0:T(8,128)(2,1)} %param.18, f32[384]{0:T(512)S(1)} %get-tuple-element.9), kind=kOutput, calls=%fused_computation.43 | convolution fusion | flops 4835377152 | bytes 21235200 | tf_op jit(solution)/shard_map/dot_general | solution.py:129
  126.5 11.3 %fusion.6 = f32[384,1024]{1,0:T(8,128)S(1)} fusion(bf16[384,6144]{1,0:T(8,128)(2,1)} %copy-done.3, bf16[2,6144,1024]{2,1,0:T(8,128)(2,1)} %param.17), kind=kOutput, calls=%fused_computation.10 | convolution fusion | flops 4831838208 | bytes 18874368 | tf_op jit(solution)/shard_map/dot_general | solution.py:125
  137.8 9.0 %fusion.32 = bf16[384,1024]{1,0:T(8,128)(2,1)} fusion(f32[384,2,1024]{2,0,1:T(8,128)S(1)} %bitcast.93, f32[384,1024]{1,0:T(8,128)S(1)} %fusion.6, bf16[384,6144]{1,0:T(8,128)(2,1)S(1)} %copy-done.4, bf16[2,6144,1024]{2,1,0:T(8,128)(2,1)} %param.18, f32[384]{0:T(512)S(1)} %get-tuple-element.10), kind=kOutput, calls=%fused_computation.38 | convolution fusion | flops 4835377152 | bytes 21235200 | tf_op jit(solution)/shard_map/dot_general | solution.py:129
  146.8 41.6 %all-gather.7.cloned.1.call-done = bf16[384,4096]{1,0:T(8,128)(2,1)} async-done(((bf16[384,1024]{1,0:T(8,128)(2,1)}), bf16[384,4096]{1,0:T(8,128)(2,1)}) %all-gather.7.cloned.1.call-update) | async-done | bytes 3145744 | tf_op jit(solution)/shard_map/all_gather | solution.py:135
  188.4 10.0 %fusion.8 = f32[384,1536]{1,0:T(8,128)} fusion(bf16[384,4096]{1,0:T(8,128)(2,1)} %all-gather.7.cloned.1.call-done, bf16[2,4096,1536]{2,1,0:T(8,128)(2,1)} %param.19), kind=kOutput, calls=%fused_computation.12 | convolution fusion | flops 4831838208 | bytes 18087936 | tf_op jit(solution)/shard_map/dot_general | solution.py:138
  198.4 53.7 %all-gather.9.cloned.1.call-done = bf16[384,4096]{1,0:T(8,128)(2,1)} async-done(((bf16[384,1024]{1,0:T(8,128)(2,1)}), bf16[384,4096]{1,0:T(8,128)(2,1)}) %all-gather.9.cloned.1.call-update) | async-done | bytes 3145744 | tf_op jit(solution)/shard_map/all_gather | solution.py:135
  252.2 7.9 %fusion.23 = f32[192,1536]{1,0:T(8,128)S(1)} fusion(bf16[2,4096,1536]{2,1,0:T(8,128)(2,1)} %param.19, bf16[384,4096]{1,0:T(8,128)(2,1)} %all-gather.9.cloned.1.call-done, s32[]{:T(128)S(6)} %select_n.119, f32[384,1536]{1,0:T(8,128)} %fusion.8), kind=kOutput, calls=%fused_computation.31 | convolution fusion | flops 2416214016 | bytes 16516096 | tf_op jit(solution)/shard_map/dot_general | solution.py:150
  260.2 2.0 collective-permute-done.8
  262.3 1.5 collective-permute-start.10
  263.8 8.0 %fusion.26 = f32[192,1536]{1,0:T(8,128)S(1)} fusion(bf16[2,4096,1536]{2,1,0:T(8,128)(2,1)} %param.19, bf16[384,4096]{1,0:T(8,128)(2,1)} %all-gather.9.cloned.1.call-done, s32[]{:T(128)S(6)} %select_n.118, f32[384,1536]{1,0:T(8,128)} %fusion.8), kind=kOutput, calls=%fused_computation.32 | convolution fusion | flops 2416214016 | bytes 16516096 | tf_op jit(solution)/shard_map/dot_general | solution.py:150
  272.0 5.7 %collective-permute-done.10 = f32[96,1536]{1,0:T(8,128)S(1)} collective-permute-done((f32[96,1536]{1,0:T(8,128)S(1)}, f32[96,1536]{1,0:T(8,128)S(1)}, u32[]{:S(2)}, u32[]{:S(2)}) %collective-permute-start.10) | collective-permute-done | bytes 589856 | tf_op jit(solution)/shard_map/ppermute | solution.py:162
  277.7 0.8 add_convert_fusion
  (70 shorter events, 4.5 us)
Async XLA Ops:
  6.5 90.2 %copy-start = (bf16[8,2,64,1024]{3,2,1,0:T(8,128)(2,1)S(1)}, bf16[8,2,64,1024]{3,2,1,0:T(8,128)(2,1)}, u32[]{:S(2)}) copy-start(bf16[8,2,64,1024]{3,2,1,0:T(8,128)(2,1)} %param.21) | copy-start | bytes 6291460
  6.5 71.8 %all-gather.5.cloned.1.call-start = ((), (), s32[]{:S(2)}) async-start(), calls=%async_computation | async-start | bytes 2949120 | tf_op jit(solution)/shard_map/all_gather | solution.py:88
  6.5 12.3 %collective-permute-start.1 = (bf16[1,128,1536]{2,1,0:T(8,128)(2,1)}, bf16[1,128,1536]{2,1,0:T(8,128)(2,1)S(1)}, u32[]{:S(2)}, u32[]{:S(2)}) collective-permute-start(bf16[1,128,1536]{2,1,0:T(8,128)(2,1)} %param.11), channel_id=1, source_target_pairs={{0,8},{8,0},{1,9},{9,1},{2,10},{10,2},{3,11},{11,3},{4,12},{12,4},... | collective-permute-start | bytes 1179656 | tf_op jit(solution)/shard_map/ppermute | solution.py:44
  9.5 10.2 %collective-permute-start = (bf16[1,128,1536]{2,1,0:T(8,128)(2,1)}, bf16[1,128,1536]{2,1,0:T(8,128)(2,1)S(1)}, u32[]{:S(2)}, u32[]{:S(2)}) collective-permute-start(bf16[1,128,1536]{2,1,0:T(8,128)(2,1)} %param.11), channel_id=1, source_target_pairs={{0,4},{4,0},{1,5},{5,1},{2,6},{6,2},{3,7},{7,3},{8,12},{12,8},{9,1... | collective-permute-start | bytes 1179656 | tf_op jit(solution)/shard_map/ppermute | solution.py:45
  18.8 1.7 collective-permute-start.2
  22.9 23.3 %copy-start.12 = (s32[3]{0:T(128)S(1)}, s32[3]{0:T(128)}, u32[]{:S(2)}) copy-start(s32[3]{0:T(128)} %param.14) | copy-start | bytes 40
  22.9 23.3 %copy-start.2 = (s32[8]{0:T(128)S(1)}, s32[8]{0:T(128)}, u32[]{:S(2)}) copy-start(s32[8]{0:T(128)} %param.15) | copy-start | bytes 100
  25.0 27.1 %copy-start.7 = (bf16[3,128,1536]{2,1,0:T(8,128)(2,1)}, bf16[3,128,1536]{2,1,0:T(8,128)(2,1)S(1)}, u32[]{:S(2)}) copy-start(bf16[3,128,1536]{2,1,0:T(8,128)(2,1)S(1)} %gather_fusion) | copy-start | bytes 3538948
  26.2 162.2 %all-gather.7.cloned.1.call-start = ((), (), s32[]{:S(2)}) async-start(), calls=%async_computation.1 | async-start | bytes 3932160 | tf_op jit(solution)/shard_map/all_gather | solution.py:135
  26.3 20.0 %collective-permute-start.5 = (bf16[2,2,1536,64]{2,3,1,0:T(8,128)(2,1)}, bf16[2,2,1536,64]{2,3,1,0:T(8,128)(2,1)}, u32[]{:S(2)}, u32[]{:S(2)}) collective-permute-start(bf16[2,2,1536,64]{2,3,1,0:T(8,128)(2,1)} %param.20), channel_id=1, source_target_pairs={{0,8},{8,0},{1,9},{9,1},{2,10},{10,2},{3,11},{11,3},{4,12},{12,4},... | collective-permute-start | bytes 2359304 | tf_op jit(solution)/shard_map/ppermute | solution.py:63
  28.1 18.9 %collective-permute-start.4 = (bf16[2,2,1536,64]{2,3,1,0:T(8,128)(2,1)}, bf16[2,2,1536,64]{2,3,1,0:T(8,128)(2,1)}, u32[]{:S(2)}, u32[]{:S(2)}) collective-permute-start(bf16[2,2,1536,64]{2,3,1,0:T(8,128)(2,1)} %param.20), channel_id=1, source_target_pairs={{0,4},{4,0},{1,5},{5,1},{2,6},{6,2},{3,7},{7,3},{8,12},{12,8},{9,1... | collective-permute-start | bytes 2359304 | tf_op jit(solution)/shard_map/ppermute | solution.py:64
  46.2 2.6 collective-permute-start.6
  78.3 1.3 copy-start.8
  78.3 20.7 %collective-permute-start.3 = (bf16[192,6144]{1,0:T(8,128)(2,1)}, bf16[192,6144]{1,0:T(8,128)(2,1)}, u32[]{:S(2)}, u32[]{:S(2)}) collective-permute-start(bf16[192,6144]{1,0:T(8,128)(2,1)} %all-gather.5.cloned.1.call-done), channel_id=1, source_target_pairs={{0,4},{4,0},{1,5},{5,1},{2,6},{6,2},{3,7},{7,3},{8,12},{12,8},{9,1... | collective-permute-start | bytes 7077896 | tf_op jit(solution)/shard_map/ppermute | solution.py:96
  80.1 16.6 %copy-start.11 = (s32[384,2]{0,1:T(2,128)S(1)}, s32[384,2]{0,1:T(2,128)}, u32[]{:S(2)}) copy-start(s32[384,2]{0,1:T(2,128)} %param.13) | copy-start | bytes 9220
  96.6 1.3 collective-permute-start.7
  98.7 2.8 copy-start.9
  98.9 18.2 %copy-start.5 = (f32[3,128,2,1024]{3,1,0,2:T(8,128)}, f32[3,128,2,1024]{3,1,0,2:T(8,128)S(1)}, u32[]{:S(2)}) copy-start(f32[3,128,2,1024]{3,1,0,2:T(8,128)S(1)} %copy.18) | copy-start | bytes 9437188
  98.9 8.6 %copy-start.10 = (bf16[6144,8]{0,1:T(8,128)(2,1)S(1)}, bf16[6144,8]{0,1:T(8,128)(2,1)}, u32[]{:S(2)}) copy-start(bf16[6144,8]{0,1:T(8,128)(2,1)} %param.16) | copy-start | bytes 294916
  107.5 9.6 %copy-start.3 = (bf16[384,6144]{1,0:T(8,128)(2,1)}, bf16[384,6144]{1,0:T(8,128)(2,1)S(1)}, u32[]{:S(2)}) copy-start(bf16[384,6144]{1,0:T(8,128)(2,1)S(1)} %fusion.22) | copy-start | bytes 14155780
  126.2 125.9 %all-gather.9.cloned.1.call-start = ((), (), s32[]{:S(2)}) async-start(), calls=%async_computation.2 | async-start | bytes 3932160 | tf_op jit(solution)/shard_map/all_gather | solution.py:135
  126.5 11.3 %copy-start.4 = (bf16[384,6144]{1,0:T(8,128)(2,1)S(1)}, bf16[384,6144]{1,0:T(8,128)(2,1)}, u32[]{:S(2)}) copy-start(bf16[384,6144]{1,0:T(8,128)(2,1)} %copy-done.3) | copy-start | bytes 14155780
  126.5 11.3 %copy-start.6 = (f32[3,128,2,1024]{3,1,0,2:T(8,128)S(1)}, f32[3,128,2,1024]{3,1,0,2:T(8,128)}, u32[]{:S(2)}) copy-start(f32[3,128,2,1024]{3,1,0,2:T(8,128)} %copy-done.5) | copy-start | bytes 9437188
  260.1 2.1 collective-permute-start.8
  262.3 15.4 %collective-permute-start.10 = (f32[96,1536]{1,0:T(8,128)S(1)}, f32[96,1536]{1,0:T(8,128)S(1)}, u32[]{:S(2)}, u32[]{:S(2)}) collective-permute-start(f32[96,1536]{1,0:T(8,128)S(1)} %dynamic-slice_add_fusion), channel_id=1, source_target_pairs={{0,8},{8,0},{1,9},{9,1},{2,10},{10,2},{3,11},{11,3},{4,12},{12,4},... | collective-permute-start | bytes 1769480 | tf_op jit(solution)/shard_map/ppermute | solution.py:162
  263.8 14.7 %copy-start.1 = (bf16[8,2,64,1024]{3,2,1,0:T(8,128)(2,1)S(1)}, bf16[8,2,64,1024]{3,2,1,0:T(8,128)(2,1)}, u32[]{:S(2)}) copy-start(bf16[8,2,64,1024]{3,2,1,0:T(8,128)(2,1)} %param.21) | copy-start | bytes 6291460
  271.9 5.8 %collective-permute-start.9 = (f32[96,1536]{1,0:T(8,128)S(1)}, f32[96,1536]{1,0:T(8,128)S(1)}, u32[]{:S(2)}, u32[]{:S(2)}) collective-permute-start(f32[96,1536]{1,0:T(8,128)S(1)} %constant_dynamic-slice_fusion.1), channel_id=1, source_target_pairs={{0,4},{4,0},{1,5},{5,1},{2,6},{6,2},{3,7},{7,3},{8,12},{12,8},{9,1... | collective-permute-start | bytes 1769480 | tf_op jit(solution)/shard_map/ppermute | solution.py:159
Sparse Core Ops, SparseCore 0:
  26.3 51.9 all-gather.4
  126.3 62.0 all-gather.6
  190.0 62.1 all-gather.8
